TPU v7x, 128 devices: a whole 4x4x4 slice. The times are simulated.
128 devices in a mesh: owner: 32 (over z, x, core), tensor: 4 (over y).
Axes of the slice: x: 4, y: 4, z: 4, core: 2. Of those that a mesh axis runs over, the one named last changes fastest.
Arguments:
- gradients: bfloat16 [160, 1536, 512], P(None, 'owner', 'tensor'), may hold values from -12 to 12
- moments: bfloat16 [160, 1536, 512], P(None, 'owner', 'tensor'), may hold values from -12 to 12
- stats: float32 [256, 512, 512], P(('owner', 'tensor')), may hold values from -1 to 11, as said below
- bases: float32 [256, 512, 512], P(('owner', 'tensor')), may hold values from -1 to 2
- second: bfloat16 [256, 1536, 512], P(('owner', 'tensor')), may hold values from 0.19921875 to 8
- owner_list: int32 [160], replicated, may hold values from 0 to 127, as said below
Outputs:
- new_moments: bfloat16 [160, 1536, 512], P(None, 'owner', 'tensor')
- update: bfloat16 [160, 1536, 512], P(None, 'owner', 'tensor')
- new_stats: float32 [256, 512, 512], P(('owner', 'tensor'))
- new_bases: float32 [256, 512, 512], P(('owner', 'tensor'))
- new_second: bfloat16 [256, 1536, 512], P(('owner', 'tensor'))
Inputs may be any that keep to these rules, and one draw needn't show every extreme that they name: `owner_list`: no device owns more than 2 matrices, and at least one owns 2. `stats`: Symmetric.
All inputs are finite; a program needn't handle non-finite values.
Results may differ from a plain program's by a relative error of at most 0.0077.
Values may be sent and summed in bfloat16 or wider, within the bound.
No kernel may reach another device: no remote copies, remote signals or barrier semaphores. Data moves between devices by JAX's collectives and lax.ppermute only.
A program may use at most 128 MiB of HBM per device.

v0:
```python
import jax
import jax.numpy as jnp
from jax import lax
from jax.sharding import PartitionSpec as P


def refine(iterate):
    for sweep in range(2):
        iter_b = iterate.astype(jnp.bfloat16)
        square = jnp.einsum(
            "cki,ckj->cij", iter_b, iter_b, preferred_element_type=jnp.float32
        ).astype(jnp.bfloat16)
        iterate = 1.5 * iterate - 0.5 * jnp.einsum(
            "cik,ckj->cij", iter_b, square, preferred_element_type=jnp.float32
        )
    return iterate


def local(gradients, moments, stats, bases, second, owner_list):
    matrices, piece_rows, piece_cols = gradients.shape
    capacity = stats.shape[0]
    owners = lax.axis_size("owner")
    tensors = lax.axis_size("tensor")
    devices = owners * tensors
    myself = lax.axis_index(("owner", "tensor"))
    matrix_ids = jnp.arange(matrices, dtype=jnp.int32)
    shared = owner_list[:, None] == owner_list[None, :]
    earlier = matrix_ids[:, None] < matrix_ids[None, :]
    position = jnp.sum((shared & earlier).astype(jnp.int32), axis=0)
    slot_id = owner_list * capacity + position
    targets = (
        jnp.arange(devices, dtype=jnp.int32)[None, :] * capacity
        + jnp.arange(capacity, dtype=jnp.int32)[:, None]
    )
    selector = (targets[:, :, None] == slot_id[None, None, :]).astype(jnp.bfloat16)
    new_moments = (0.9 * moments.astype(jnp.float32) + 0.1 * gradients.astype(jnp.float32)).astype(
        jnp.bfloat16
    )
    flat_grads = gradients.reshape(matrices, piece_rows * piece_cols)
    flat_moms = new_moments.reshape(matrices, piece_rows * piece_cols)
    send_grads = jnp.einsum(
        "cdn,nk->cdk", selector, flat_grads, preferred_element_type=jnp.float32
    ).astype(jnp.bfloat16)
    send_moms = jnp.einsum(
        "cdn,nk->cdk", selector, flat_moms, preferred_element_type=jnp.float32
    ).astype(jnp.bfloat16)
    got_grads, got_moms = (
        lax.all_to_all(
            send_grads.reshape(capacity, devices, piece_rows, piece_cols),
            ("owner", "tensor"),
            split_axis=1,
            concat_axis=1,
            tiled=True,
        ),
        lax.all_to_all(
            send_moms.reshape(capacity, devices, piece_rows, piece_cols),
            ("owner", "tensor"),
            split_axis=1,
            concat_axis=1,
            tiled=True,
        ),
    )

    def assemble(pieces):
        blocks = pieces.reshape(capacity, owners, tensors, piece_rows, piece_cols)
        return blocks.transpose(0, 1, 3, 2, 4).reshape(
            capacity, owners * piece_rows, tensors * piece_cols
        )

    grad_mats = assemble(got_grads)
    moment_mats = assemble(got_moms)
    full_rows = grad_mats.shape[1]
    full_cols = grad_mats.shape[2]
    gram = jnp.einsum("cri,crj->cij", grad_mats, grad_mats, preferred_element_type=jnp.float32)
    stat_next = 0.95 * stats + 0.05 / full_rows * gram
    basis_b = bases.astype(jnp.bfloat16)
    rotated = jnp.einsum("crk,ckj->crj", grad_mats, basis_b, preferred_element_type=jnp.float32)
    second_next = 0.95 * second.astype(jnp.float32) + 0.05 * rotated * rotated
    moment_rot = jnp.einsum(
        "crk,ckj->crj", moment_mats, basis_b, preferred_element_type=jnp.float32
    )
    scaled = (moment_rot / (jnp.sqrt(second_next) + 1e-06)).astype(jnp.bfloat16)
    step_mats = jnp.einsum(
        "crj,ckj->crk", scaled, basis_b, preferred_element_type=jnp.float32
    ).astype(jnp.bfloat16)
    step_pieces = step_mats.reshape(capacity, owners, piece_rows, tensors, piece_cols).transpose(
        0, 1, 3, 2, 4
    )
    returned = lax.all_to_all(
        step_pieces.reshape(capacity, devices, piece_rows, piece_cols),
        ("owner", "tensor"),
        split_axis=1,
        concat_axis=1,
        tiled=True,
    )
    returned = returned.reshape(capacity, devices, piece_rows * piece_cols)
    update = jnp.einsum(
        "cdn,cdk->nk", selector, returned, preferred_element_type=jnp.float32
    ).astype(jnp.bfloat16)
    update = update.reshape(matrices, piece_rows, piece_cols)
    power = jnp.einsum(
        "cij,cjk->cik",
        stat_next,
        bases,
        precision=lax.Precision.HIGHEST,
        preferred_element_type=jnp.float32,
    )
    iterate = power / (
        2.0 * jnp.sqrt(full_cols * jnp.mean(power * power, axis=(1, 2), keepdims=True) + 1e-06)
    )
    iterate = refine(iterate)
    my_slots = myself * capacity + jnp.arange(capacity, dtype=jnp.int32)
    filled = jnp.any(my_slots[:, None] == slot_id[None, :], axis=1).astype(jnp.float32)[
        :, None, None
    ]
    new_stats = stat_next * filled
    new_bases = iterate * filled
    new_second = (second_next * filled).astype(jnp.bfloat16)
    return (new_moments, update, new_stats, new_bases, new_second)


def solution(mesh):
    placed = (
        P(None, "owner", "tensor"),
        P(None, "owner", "tensor"),
        P(("owner", "tensor"), None, None),
        P(("owner", "tensor"), None, None),
        P(("owner", "tensor"), None, None),
        P(),
    )
    return jax.shard_map(
        local,
        mesh=mesh,
        in_specs=placed,
        out_specs=(
            P(None, "owner", "tensor"),
            P(None, "owner", "tensor"),
            P(("owner", "tensor"), None, None),
            P(("owner", "tensor"), None, None),
            P(("owner", "tensor"), None, None),
        ),
        check_vma=False,
    )
```

profile of v0, /device:TPU:1, one launch (start us, length us, event | category | flops | bytes accessed | tf_op | source)
XLA Modules:
  0.0 206.2 jit_solution(12441411162503713069)
XLA Ops:
  0.6 2.9 %add_convert_fusion = bf16[160,48,128]{2,1,0:T(8,128)(2,1)S(1)} fusion(bf16[160,48,128]{2,1,0:T(8,128)(2,1)} %param.6, bf16[160,48,128]{2,1,0:T(8,128)(2,1)} %param.7), kind=kLoop, calls=%fused_computation.8 | loop fusion | flops 5898240 | bytes 5898240 | tf_op jit(solution)/shard_map/convert_element_type | solution.py:36
  3.5 0.0 copy-start.1
  3.6 0.0 copy-start.2
  3.6 1.9 reshape.103
  5.5 0.0 copy-done.2
  5.5 0.1 convert_reduce_fusion
  5.6 2.6 %convolution_convert_fusion.1 = bf16[2,128,6144]{2,1,0:T(8,128)(2,1)S(1)} fusion(bf16[160,6144,1]{1,0,2:T(8,128)(2,1)} %reshape.103, s32[2,128]{1,0:T(2,128)S(1)} %iota_add_fusion, s32[160]{0:T(256)S(1)} %multiply_add_fusion.1), kind=kOutput, calls=%fused_computation.2 | convolution fusion | flops 504930304 | bytes 5113472 | tf_op jit(solution)/shard_map/cdn,nk->cdk/dot_general | solution.py:44
  8.2 0.0 copy-done.1
  8.2 0.7 copy.50
  9.0 2.2 %copy.33 = bf16[2,128,48,128]{3,2,0,1:T(8,128)(2,1)} copy(bf16[2,128,48,128]{3,2,1,0:T(8,128)(2,1)S(1)} %bitcast.42) | data formatting | bytes 6291456 | tf_op jit(solution)/shard_map/reshape | solution.py:56
  11.2 11.5 %all-to-all-start = ((bf16[2,128,48,128]{3,2,0,1:T(8,128)(2,1)}), bf16[2,128,48,128]{3,2,0,1:T(8,128)(2,1)S(1)}, u32[]{:S(2)}, u32[]{:S(2)}) async-start(bf16[2,128,48,128]{3,2,0,1:T(8,128)(2,1)} %copy.33), calls=%async_computation | async-start | bytes 6291456 | tf_op jit(solution)/shard_map/all_to_all | solution.py:55
  22.7 4.0 %reshape.104 = bf16[160,6144,1]{1,0,2:T(8,128)(2,1)} reshape(bf16[160,48,128]{2,1,0:T(8,128)(2,1)} %param.6) | data formatting | bytes 3932160 | tf_op jit(solution)/shard_map/reshape | solution.py:39
  26.6 2.6 %convolution_convert_fusion = bf16[2,128,6144]{2,1,0:T(8,128)(2,1)S(1)} fusion(bf16[160,6144,1]{1,0,2:T(8,128)(2,1)} %reshape.104, s32[2,128]{1,0:T(2,128)S(1)} %iota_add_fusion, s32[160]{0:T(256)S(1)} %multiply_add_fusion.1), kind=kOutput, calls=%fused_computation.1 | convolution fusion | flops 504930304 | bytes 5113472 | tf_op jit(solution)/shard_map/cdn,nk->cdk/dot_general | solution.py:41
  29.3 0.7 copy.51
  30.0 2.2 %copy.36 = bf16[2,128,48,128]{3,2,0,1:T(8,128)(2,1)} copy(bf16[2,128,48,128]{3,2,1,0:T(8,128)(2,1)S(1)} %bitcast.44) | data formatting | bytes 6291456 | tf_op jit(solution)/shard_map/reshape | solution.py:49
  32.2 32.1 %all-to-all-done = bf16[2,128,48,128]{3,2,0,1:T(8,128)(2,1)S(1)} async-done(((bf16[2,128,48,128]{3,2,0,1:T(8,128)(2,1)}), bf16[2,128,48,128]{3,2,0,1:T(8,128)(2,1)S(1)}, u32[]{:S(2)}, u32[]{:S(2)}) %all-to-all-start) | async-done | bytes 3145760 | tf_op jit(solution)/shard_map/all_to_all | solution.py:55
  64.4 4.8 %all-to-all-start.1 = ((bf16[2,128,48,128]{3,2,0,1:T(8,128)(2,1)}), bf16[2,128,48,128]{3,2,0,1:T(8,128)(2,1)}, u32[]{:S(2)}, u32[]{:S(2)}) async-start(bf16[2,128,48,128]{3,2,0,1:T(8,128)(2,1)} %copy.36), calls=%async_computation.1 | async-start | bytes 6291456 | tf_op jit(solution)/shard_map/all_to_all | solution.py:48
  69.2 0.2 compare_reduce_fusion
  69.4 3.3 %copy.35 = bf16[2,32,48,4,128]{4,3,2,1,0:T(4,128)(2,1)} copy(bf16[2,32,48,4,128]{4,2,0,3,1:T(8,128)(2,1)S(1)} %bitcast.39) | data formatting | bytes 6291456 | tf_op jit(solution)/shard_map/transpose | solution.py:66
  72.7 5.7 %reshape.94 = bf16[2,1536,512]{2,1,0:T(8,128)(2,1)} reshape(bf16[2,32,48,4,128]{4,3,2,1,0:T(4,128)(2,1)} %copy.35) | data formatting | bytes 6291456 | tf_op jit(solution)/shard_map/reshape | solution.py:66
  78.4 32.1 %all-to-all-done.1 = bf16[2,128,48,128]{3,2,0,1:T(8,128)(2,1)} async-done(((bf16[2,128,48,128]{3,2,0,1:T(8,128)(2,1)}), bf16[2,128,48,128]{3,2,0,1:T(8,128)(2,1)}, u32[]{:S(2)}, u32[]{:S(2)}) %all-to-all-start.1) | async-done | bytes 3145760 | tf_op jit(solution)/shard_map/all_to_all | solution.py:48
  110.5 5.2 %copy.58 = bf16[2,32,4,48,128]{4,2,3,1,0:T(4,128)(2,1)} copy(bf16[2,32,4,48,128]{4,3,0,2,1:T(8,128)(2,1)} %bitcast.3) | data formatting | bytes 6291456 | tf_op jit(solution)/shard_map/reshape | solution.py:65
  115.7 4.0 %reshape.98 = bf16[2,1536,512]{2,1,0:T(8,128)(2,1)S(1)} reshape(bf16[2,32,48,4,128]{4,3,2,1,0:T(4,128)(2,1)} %bitcast.45) | data formatting | bytes 6291456 | tf_op jit(solution)/shard_map/reshape | solution.py:66
  119.7 8.5 %multiply_convert_fusion = (bf16[2,1536,512]{2,1,0:T(8,128)(2,1)}, f32[2,1536,512]{2,1,0:T(8,128)}) fusion(bf16[2,1536,512]{2,1,0:T(8,128)(2,1)} %param.10, f32[2]{0:T(128)S(1)} %convert_element_type.67, bf16[2,1536,512]{2,1,0:T(8,128)(2,1)S(1)} %reshape.98, f32[2,512,512]{2,1,0:T(8,128)} %param.9), kind=kOutput, calls=%fused_computation.6 | convolution fusion | flops 1622147072 | bytes 17825800 | tf_op jit(solution)/shard_map/crk,ckj->crj/dot_general | solution.py:77
  128.2 12.4 %convolution_convert_fusion.2 = bf16[2,1536,512]{2,1,0:T(8,128)(2,1)} fusion(bf16[2,1536,512]{2,1,0:T(8,128)(2,1)} %reshape.94, f32[2,1536,512]{2,1,0:T(8,128)} %get-tuple-element.10, bf16[2,1536,512]{2,1,0:T(8,128)(2,1)} %param.10, f32[2,512,512]{2,1,0:T(8,128)} %param.9), kind=kOutput, calls=%fused_computation.9 | convolution fusion | flops 3236429824 | bytes 17825792 | tf_op jit(solution)/shard_map/crj,ckj->crk/dot_general | solution.py:83
  140.6 5.5 %reshape.99 = bf16[2,32,48,4,128]{4,3,2,1,0:T(4,128)(2,1)} reshape(bf16[2,1536,512]{2,1,0:T(8,128)(2,1)} %convolution_convert_fusion.2) | data formatting | bytes 6291456 | tf_op jit(solution)/shard_map/reshape | solution.py:86
  146.1 4.2 %copy.48 = bf16[2,32,48,4,128]{4,2,0,3,1:T(8,128)(2,1)} copy(bf16[2,32,48,4,128]{4,3,2,1,0:T(4,128)(2,1)} %reshape.99) | data formatting | bytes 6291456 | tf_op jit(solution)/shard_map/reshape | solution.py:90
  150.3 4.9 %all-to-all-start.2 = ((bf16[2,128,48,128]{3,2,0,1:T(8,128)(2,1)}), bf16[2,128,48,128]{3,2,0,1:T(8,128)(2,1)}, u32[]{:S(2)}, u32[]{:S(2)}) async-start(bf16[2,128,48,128]{3,2,0,1:T(8,128)(2,1)} %bitcast.40), calls=%async_computation.2 | async-start | bytes 6291456 | tf_op jit(solution)/shard_map/all_to_all | solution.py:89
  155.2 0.0 copy-start
  155.2 5.0 %broadcast_multiply_fusion = (f32[2,512,512]{2,1,0:T(8,128)}, f32[2,512,512]{2,1,0:T(8,128)S(1)}) fusion(f32[2]{0:T(128)S(1)} %convert_element_type.67, bf16[2,1536,512]{2,1,0:T(8,128)(2,1)S(1)} %reshape.98, f32[2,512,512]{2,1,0:T(8,128)} %param.8), kind=kOutput, calls=%fused_computation.23 | convolution fusion | flops 1612709888 | bytes 9437192 | tf_op jit(solution)/shard_map/cri,crj->cij/dot_general | solution.py:74
  160.2 0.0 copy-done
  160.2 3.7 %multiply_reduce_fusion = (f32[2]{0:T(128)S(1)}, f32[2,512,512]{2,1,0:T(8,128)S(1)}) fusion(f32[2,512,512]{2,1,0:T(8,128)S(1)} %get-tuple-element.6, f32[2,512,512]{2,1,0:T(8,128)S(1)} %copy-done), kind=kOutput, calls=%fused_computation.14 | convolution fusion | flops 3222274048 | bytes 6291464 | tf_op jit(solution)/shard_map/cij,cjk->cik/dot_general | solution.py:101
  163.9 2.8 %multiply_subtract_fusion = f32[2,512,512]{2,1,0:T(8,128)} fusion(f32[2,512,512]{2,1,0:T(8,128)S(1)} %get-tuple-element.8, f32[2]{0:T(128)S(1)} %sqrt_multiply_fusion), kind=kOutput, calls=%fused_computation.13 | convolution fusion | flops 1078460416 | bytes 4194312 | tf_op jit(solution)/shard_map/cik,ckj->cij/dot_general | solution.py:13
  166.7 6.3 %subtract_multiply_fusion = f32[2,512,512]{2,1,0:T(8,128)} fusion(f32[2,512,512]{2,1,0:T(8,128)} %multiply_subtract_fusion, f32[2]{0:T(128)S(1)} %convert_element_type.67), kind=kOutput, calls=%fused_computation.12 | convolution fusion | flops 1077411840 | bytes 4194312 | tf_op jit(solution)/shard_map/cik,ckj->cij/dot_general | solution.py:13
  173.1 23.4 %all-to-all-done.2 = bf16[2,128,48,128]{3,2,0,1:T(8,128)(2,1)} async-done(((bf16[2,128,48,128]{3,2,0,1:T(8,128)(2,1)}), bf16[2,128,48,128]{3,2,0,1:T(8,128)(2,1)}, u32[]{:S(2)}, u32[]{:S(2)}) %all-to-all-start.2) | async-done | bytes 3145760 | tf_op jit(solution)/shard_map/all_to_all | solution.py:89
  196.4 6.0 %reshape.108 = bf16[2,128,6144]{2,0,1:T(2,128)(2,1)S(1)} reshape(bf16[2,128,48,128]{3,2,0,1:T(8,128)(2,1)} %all-to-all-done.2) | data formatting | bytes 6291456 | tf_op jit(solution)/shard_map/reshape | solution.py:96
  202.4 2.1 %fusion.3 = bf16[20,8,48,128]{3,1,2,0:T(8,128)(2,1)S(1)} fusion(bf16[2,128,6144]{2,0,1:T(2,128)(2,1)S(1)} %reshape.108, s32[2,128]{1,0:T(2,128)S(1)} %iota_add_fusion, s32[160]{0:T(256)S(1)} %multiply_add_fusion.1), kind=kOutput, calls=%fused_computation.16 | convolution fusion | flops 504340480 | bytes 5113472 | tf_op jit(solution)/shard_map/cdn,cdk->nk/dot_general | solution.py:97
  204.5 1.7 copy.52
  (6 shorter events, 0.0 us)
Async XLA Ops:
  3.5 4.7 %copy-start.1 = (bf16[160,48,128]{2,1,0:T(8,128)(2,1)}, bf16[160,48,128]{2,1,0:T(8,128)(2,1)S(1)}, u32[]{:S(2)}) copy-start(bf16[160,48,128]{2,1,0:T(8,128)(2,1)S(1)} %add_convert_fusion) | copy-start | bytes 5898244
  3.6 1.9 copy-start.2
  11.2 53.2 %all-to-all-start = ((bf16[2,128,48,128]{3,2,0,1:T(8,128)(2,1)}), bf16[2,128,48,128]{3,2,0,1:T(8,128)(2,1)S(1)}, u32[]{:S(2)}, u32[]{:S(2)}) async-start(bf16[2,128,48,128]{3,2,0,1:T(8,128)(2,1)} %copy.33), calls=%async_computation | async-start | bytes 6291456 | tf_op jit(solution)/shard_map/all_to_all | solution.py:55
  64.4 46.2 %all-to-all-start.1 = ((bf16[2,128,48,128]{3,2,0,1:T(8,128)(2,1)}), bf16[2,128,48,128]{3,2,0,1:T(8,128)(2,1)}, u32[]{:S(2)}, u32[]{:S(2)}) async-start(bf16[2,128,48,128]{3,2,0,1:T(8,128)(2,1)} %copy.36), calls=%async_computation.1 | async-start | bytes 6291456 | tf_op jit(solution)/shard_map/all_to_all | solution.py:48
  150.3 46.1 %all-to-all-start.2 = ((bf16[2,128,48,128]{3,2,0,1:T(8,128)(2,1)}), bf16[2,128,48,128]{3,2,0,1:T(8,128)(2,1)}, u32[]{:S(2)}, u32[]{:S(2)}) async-start(bf16[2,128,48,128]{3,2,0,1:T(8,128)(2,1)} %bitcast.40), calls=%async_computation.2 | async-start | bytes 6291456 | tf_op jit(solution)/shard_map/all_to_all | solution.py:89
  155.2 5.0 %copy-start = (f32[2,512,512]{2,1,0:T(8,128)S(1)}, f32[2,512,512]{2,1,0:T(8,128)}, u32[]{:S(2)}) copy-start(f32[2,512,512]{2,1,0:T(8,128)} %param.9) | copy-start | bytes 6291460
where the time goes:
time: 207 us; the launch traced here: 206 us
  waiting for transfers between devices  87.6 us (42%)
  local copies, waits for them, and re-layouts  47.3 us (23%)
  matrix products  46.2 us (22%)
  starting transfers between devices  21.2 us (10%)
  other arithmetic  3.23 us (2%)
    all_to_all x1, waiting for transfers between devices, local(): lax.all_to_all(send_moms.reshape(capacity, devices, piece_rows, piece_col...  32.1 us
    all_to_all x1, waiting for transfers between devices, local(): lax.all_to_all(send_grads.reshape(capacity, devices, piece_rows, piece_co...  32.1 us
    all_to_all x1, waiting for transfers between devices, local(): lax.all_to_all(step_pieces.reshape(capacity, devices, piece_rows, piece_c...  23.4 us
    dot_general x1, matrix products, local(): jnp.einsum('crj,ckj->crk', scaled, basis_b, preferred_element_type=jnp.fl...  12.4 us
    all_to_all x1, starting transfers between devices, local(): lax.all_to_all(send_moms.reshape(capacity, devices, piece_rows, piece_col...  11.5 us
    reshape x2, local copies, waits for them, and re-layouts, assemble(): blocks.transpose(0, 1, 3, 2, 4)  9.76 us
    dot_general x2, matrix products, refine(): jnp.einsum('cik,ckj->cij', iter_b, square, preferred_element_type=jnp.flo...  9.13 us
    dot_general x1, matrix products, local(): jnp.einsum('crk,ckj->crj', grad_mats, basis_b, preferred_element_type=jnp...  8.48 us
  transfers between devices with their start and end apart: 3, of which 3 were waited for; matrix products, arithmetic and copies ran while one was open for 18% of the time, Pallas kernels for 0%

commit v1 on v0

v1 whole, which is shorter than its diff:
```python
import jax
import jax.numpy as jnp
from jax import lax
from jax.sharding import PartitionSpec as P


def refine(iterate):
    for sweep in range(2):
        iter_b = iterate.astype(jnp.bfloat16)
        square = jnp.einsum(
            "cki,ckj->cij", iter_b, iter_b, preferred_element_type=jnp.float32
        ).astype(jnp.bfloat16)
        iterate = 1.5 * iterate - 0.5 * jnp.einsum(
            "cik,ckj->cij", iter_b, square, preferred_element_type=jnp.float32
        )
    return iterate


def exchange(pieces):
    return lax.all_to_all(
        pieces, ("owner", "tensor"), split_axis=1, concat_axis=1, tiled=True
    )


def local(gradients, moments, stats, bases, second, owner_list):
    matrices, piece_rows, piece_cols = gradients.shape
    capacity = stats.shape[0]
    owners = lax.axis_size("owner")
    tensors = lax.axis_size("tensor")
    devices = owners * tensors
    myself = lax.axis_index(("owner", "tensor"))
    matrix_ids = jnp.arange(matrices, dtype=jnp.int32)
    shared = owner_list[:, None] == owner_list[None, :]
    earlier = matrix_ids[:, None] < matrix_ids[None, :]
    position = jnp.sum((shared & earlier).astype(jnp.int32), axis=0)
    slot_id = owner_list * capacity + position
    targets = (
        jnp.arange(devices, dtype=jnp.int32)[None, :] * capacity
        + jnp.arange(capacity, dtype=jnp.int32)[:, None]
    )
    hit = targets[:, :, None] == slot_id[None, None, :]
    which = jnp.sum(jnp.where(hit, matrix_ids[None, None, :], 0), axis=2)

    send_grads = jnp.take(gradients, which, axis=0, mode="clip")
    got_grads = exchange(send_grads)

    new_moments = (0.9 * moments.astype(jnp.float32) + 0.1 * gradients.astype(jnp.float32)).astype(
        jnp.bfloat16
    )
    send_moms = jnp.take(new_moments, which, axis=0, mode="clip")
    got_moms = exchange(send_moms)

    def assemble(pieces):
        blocks = pieces.reshape(capacity, owners, tensors, piece_rows, piece_cols)
        return blocks.transpose(0, 1, 3, 2, 4).reshape(
            capacity, owners * piece_rows, tensors * piece_cols
        )

    grad_mats = assemble(got_grads)
    full_rows = grad_mats.shape[1]
    full_cols = grad_mats.shape[2]
    gram = jnp.einsum("cri,crj->cij", grad_mats, grad_mats, preferred_element_type=jnp.float32)
    stat_next = 0.95 * stats + 0.05 / full_rows * gram
    basis_b = bases.astype(jnp.bfloat16)
    rotated = jnp.einsum("crk,ckj->crj", grad_mats, basis_b, preferred_element_type=jnp.float32)
    second_next = 0.95 * second.astype(jnp.float32) + 0.05 * rotated * rotated
    power = jnp.einsum(
        "cij,cjk->cik",
        stat_next,
        bases,
        precision=lax.Precision.HIGHEST,
        preferred_element_type=jnp.float32,
    )
    iterate = power / (
        2.0 * jnp.sqrt(full_cols * jnp.mean(power * power, axis=(1, 2), keepdims=True) + 1e-06)
    )
    iterate = refine(iterate)

    moment_mats = assemble(got_moms)
    moment_rot = jnp.einsum(
        "crk,ckj->crj", moment_mats, basis_b, preferred_element_type=jnp.float32
    )
    scaled = (moment_rot / (jnp.sqrt(second_next) + 1e-06)).astype(jnp.bfloat16)
    step_mats = jnp.einsum(
        "crj,ckj->crk", scaled, basis_b, preferred_element_type=jnp.float32
    ).astype(jnp.bfloat16)
    step_pieces = step_mats.reshape(capacity, owners, piece_rows, tensors, piece_cols).transpose(
        0, 1, 3, 2, 4
    )
    returned = exchange(step_pieces.reshape(capacity, devices, piece_rows, piece_cols))
    back_index = position * devices + owner_list
    update = jnp.take(
        returned.reshape(capacity * devices, piece_rows, piece_cols), back_index, axis=0,
        mode="clip",
    )

    my_slots = myself * capacity + jnp.arange(capacity, dtype=jnp.int32)
    filled = jnp.any(my_slots[:, None] == slot_id[None, :], axis=1)[:, None, None]
    new_stats = jnp.where(filled, stat_next, 0.0)
    new_bases = jnp.where(filled, iterate, 0.0)
    new_second = jnp.where(filled, second_next, 0.0).astype(jnp.bfloat16)
    return (new_moments, update, new_stats, new_bases, new_second)


def solution(mesh):
    placed = (
        P(None, "owner", "tensor"),
        P(None, "owner", "tensor"),
        P(("owner", "tensor"), None, None),
        P(("owner", "tensor"), None, None),
        P(("owner", "tensor"), None, None),
        P(),
    )
    return jax.shard_map(
        local,
        mesh=mesh,
        in_specs=placed,
        out_specs=(
            P(None, "owner", "tensor"),
            P(None, "owner", "tensor"),
            P(("owner", "tensor"), None, None),
            P(("owner", "tensor"), None, None),
            P(("owner", "tensor"), None, None),
        ),
        check_vma=False,
    )
```

time: 207 us -> 200 us (0.966)
  matrix products: 46.2 us -> 38.8 us
    reshape x6 -> x0, local copies, waits for them, and re-layouts: 21.4 us -> none  [the longest x1 6 us: local(): returned = returned.reshape(capacity, devices, piece_rows * piece_cols)]
    gather x0 -> x5, local copies, waits for them, and re-layouts: none -> 15.7 us  [the longest x2 6.75 us: local(): send_moms = jnp.take(new_moments, which, axis=0, mode='clip')]
    dot_general x3 -> x0, matrix products: 7.42 us -> none  [the longest x1 2.64 us: local(): jnp.einsum('cdn,nk->cdk', selector, flat_moms, preferred_element_type=jnp...]
    transpose x1 -> x2, local copies, waits for them, and re-layouts: 3.28 us -> 8.45 us  [assemble(): blocks.transpose(0, 1, 3, 2, 4)]
    unnamed x9 -> x6, local copies, waits for them, and re-layouts: 3.15 us -> 0.02 us
    all_to_all x0 -> x1, local copies, waits for them, and re-layouts: none -> 2.43 us  [exchange(): lax.all_to_all(pieces, ('owner', 'tensor'), split_axis=1, concat_axis=1,...]
where the time goes in v1:
time: 200 us
  waiting for transfers between devices  88.5 us (44%)
  local copies, waits for them, and re-layouts  46 us (23%)
  matrix products  38.8 us (19%)
  starting transfers between devices  20.7 us (10%)
  other arithmetic  4.77 us (2%)
    all_to_all x3, waiting for transfers between devices, exchange(): lax.all_to_all(pieces, ('owner', 'tensor'), split_axis=1, concat_axis=1,...  88.5 us
    all_to_all x3, starting transfers between devices, exchange(): lax.all_to_all(pieces, ('owner', 'tensor'), split_axis=1, concat_axis=1,...  20.7 us
    dot_general x1, matrix products, local(): jnp.einsum('crj,ckj->crk', scaled, basis_b, preferred_element_type=jnp.fl...  12.4 us
    reshape x2, local copies, waits for them, and re-layouts, assemble(): blocks.transpose(0, 1, 3, 2, 4)  9.76 us
    dot_general x2, matrix products, refine(): jnp.einsum('cik,ckj->cij', iter_b, square, preferred_element_type=jnp.flo...  9.14 us
    dot_general x1, matrix products, local(): jnp.einsum('crk,ckj->crj', grad_mats, basis_b, preferred_element_type=jnp...  8.48 us
    transpose x2, local copies, waits for them, and re-layouts, assemble(): blocks.transpose(0, 1, 3, 2, 4)  8.45 us
    gather x2, local copies, waits for them, and re-layouts, local(): send_moms = jnp.take(new_moments, which, axis=0, mode='clip')  6.75 us
  transfers between devices with their start and end apart: 3, of which 3 were waited for; matrix products, arithmetic and copies ran while one was open for 18% of the time, Pallas kernels for 0%

profile of v1, /device:TPU:1, one launch (start us, length us, event | category | flops | bytes accessed | tf_op | source)
XLA Modules:
  0.0 199.5 jit_solution(13515185469149297261)
XLA Ops:
  0.7 0.9 convert_reduce_fusion
  1.5 0.7 multiply_add_fusion.1
  2.2 0.1 select_reduce_fusion
  2.3 2.9 %add_convert_fusion = bf16[160,48,128]{2,1,0:T(8,128)(2,1)S(1)} fusion(bf16[160,48,128]{2,1,0:T(8,128)(2,1)} %param.6, bf16[160,48,128]{2,1,0:T(8,128)(2,1)} %param.7), kind=kLoop, calls=%fused_computation.7 | loop fusion | flops 5898240 | bytes 5898240 | tf_op jit(solution)/shard_map/convert_element_type | solution.py:47
  5.2 0.0 copy-start.1
  5.2 2.6 %gather_fusion = bf16[256,48,128]{2,1,0:T(8,128)(2,1)} fusion(bf16[160,48,128]{2,1,0:T(8,128)(2,1)S(1)} %add_convert_fusion, s32[1024]{0:T(1024)S(1)} %pad_clamp_fusion.1), kind=kCustom, calls=%fused_computation | custom fusion | bytes 6292480 | tf_op jit(solution)/shard_map/jit(_take)/gather | solution.py:50
  7.9 0.0 copy-done.1
  7.9 4.1 %copy.43 = bf16[2,128,48,128]{3,2,0,1:T(8,128)(2,1)} copy(bf16[2,128,48,128]{3,2,1,0:T(8,128)(2,1)} %bitcast.22) | data formatting | bytes 6291456 | tf_op jit(solution)/shard_map/jit(_take)/gather | solution.py:50
  12.0 0.0 copy-start
  12.0 11.9 %all-to-all-start = ((bf16[2,128,48,128]{3,2,0,1:T(8,128)(2,1)}), bf16[2,128,48,128]{3,2,0,1:T(8,128)(2,1)}, u32[]{:S(2)}, u32[]{:S(2)}) async-start(bf16[2,128,48,128]{3,2,0,1:T(8,128)(2,1)} %copy.43), calls=%async_computation | async-start | bytes 6291456 | tf_op jit(solution)/shard_map/all_to_all | solution.py:20
  23.9 0.0 copy-done
  23.9 2.6 %gather_fusion.1 = bf16[256,48,128]{2,1,0:T(8,128)(2,1)} fusion(bf16[160,48,128]{2,1,0:T(8,128)(2,1)S(1)} %copy-done, s32[1024]{0:T(1024)S(1)} %pad_clamp_fusion.1), kind=kCustom, calls=%fused_computation.1 | custom fusion | bytes 6292480 | tf_op jit(solution)/shard_map/jit(_take)/gather | solution.py:44
  26.5 4.1 %copy.46 = bf16[2,128,48,128]{3,2,0,1:T(8,128)(2,1)} copy(bf16[2,128,48,128]{3,2,1,0:T(8,128)(2,1)} %bitcast.21) | data formatting | bytes 6291456 | tf_op jit(solution)/shard_map/jit(_take)/gather | solution.py:44
  30.6 34.7 %all-to-all-done = bf16[2,128,48,128]{3,2,0,1:T(8,128)(2,1)} async-done(((bf16[2,128,48,128]{3,2,0,1:T(8,128)(2,1)}), bf16[2,128,48,128]{3,2,0,1:T(8,128)(2,1)}, u32[]{:S(2)}, u32[]{:S(2)}) %all-to-all-start) | async-done | bytes 3145760 | tf_op jit(solution)/shard_map/all_to_all | solution.py:20
  65.3 3.9 %all-to-all-start.1 = ((bf16[2,128,48,128]{3,2,0,1:T(8,128)(2,1)}), bf16[2,128,48,128]{3,2,0,1:T(8,128)(2,1)S(1)}, u32[]{:S(2)}, u32[]{:S(2)}) async-start(bf16[2,128,48,128]{3,2,0,1:T(8,128)(2,1)} %copy.46), calls=%async_computation.1 | async-start | bytes 6291456 | tf_op jit(solution)/shard_map/all_to_all | solution.py:20
  69.2 0.2 compare_reduce_fusion
  69.4 5.2 %copy.45 = bf16[2,32,48,4,128]{4,3,2,1,0:T(4,128)(2,1)} copy(bf16[2,32,48,4,128]{4,2,0,3,1:T(8,128)(2,1)} %bitcast.4) | data formatting | bytes 6291456 | tf_op jit(solution)/shard_map/transpose | solution.py:55
  74.6 5.7 %reshape.75 = bf16[2,1536,512]{2,1,0:T(8,128)(2,1)} reshape(bf16[2,32,48,4,128]{4,3,2,1,0:T(4,128)(2,1)} %copy.45) | data formatting | bytes 6291456 | tf_op jit(solution)/shard_map/reshape | solution.py:55
  80.3 30.6 %all-to-all-done.1 = bf16[2,128,48,128]{3,2,0,1:T(8,128)(2,1)S(1)} async-done(((bf16[2,128,48,128]{3,2,0,1:T(8,128)(2,1)}), bf16[2,128,48,128]{3,2,0,1:T(8,128)(2,1)S(1)}, u32[]{:S(2)}, u32[]{:S(2)}) %all-to-all-start.1) | async-done | bytes 3145760 | tf_op jit(solution)/shard_map/all_to_all | solution.py:20
  110.9 3.3 %copy.48 = bf16[2,32,48,4,128]{4,3,2,1,0:T(4,128)(2,1)} copy(bf16[2,32,48,4,128]{4,2,0,3,1:T(8,128)(2,1)S(1)} %bitcast.19) | data formatting | bytes 6291456 | tf_op jit(solution)/shard_map/transpose | solution.py:55
  114.2 4.0 %reshape.77 = bf16[2,1536,512]{2,1,0:T(8,128)(2,1)S(1)} reshape(bf16[2,32,48,4,128]{4,3,2,1,0:T(4,128)(2,1)} %copy.48) | data formatting | bytes 6291456 | tf_op jit(solution)/shard_map/reshape | solution.py:55
  118.2 8.5 %select_convert_fusion = (bf16[2,1536,512]{2,1,0:T(8,128)(2,1)}, f32[2,1536,512]{2,1,0:T(8,128)}) fusion(bf16[2,1536,512]{2,1,0:T(8,128)(2,1)} %param.10, pred[2]{0:T(512)(128)(4,1)S(1)} %compare_reduce_fusion, bf16[2,1536,512]{2,1,0:T(8,128)(2,1)S(1)} %reshape.77, f32[2,512,512]{2,1,0:T(8,128)} %param.9), kind=kOutput, calls=%fused_computation.5 | convolution fusion | flops 1622147072 | bytes 17825794 | tf_op jit(solution)/shard_map/crk,ckj->crj/dot_general | solution.py:65
  126.7 12.4 %convolution_convert_fusion = bf16[2,1536,512]{2,1,0:T(8,128)(2,1)} fusion(bf16[2,1536,512]{2,1,0:T(8,128)(2,1)} %reshape.75, f32[2,1536,512]{2,1,0:T(8,128)} %get-tuple-element.12, bf16[2,1536,512]{2,1,0:T(8,128)(2,1)} %param.10, f32[2,512,512]{2,1,0:T(8,128)} %param.9), kind=kOutput, calls=%fused_computation.8 | convolution fusion | flops 3236429824 | bytes 17825792 | tf_op jit(solution)/shard_map/crj,ckj->crk/dot_general | solution.py:84
  139.1 5.5 %reshape.78 = bf16[2,32,48,4,128]{4,3,2,1,0:T(4,128)(2,1)} reshape(bf16[2,1536,512]{2,1,0:T(8,128)(2,1)} %convolution_convert_fusion) | data formatting | bytes 6291456 | tf_op jit(solution)/shard_map/reshape | solution.py:87
  144.6 4.2 %copy.60 = bf16[2,32,48,4,128]{4,2,0,3,1:T(8,128)(2,1)} copy(bf16[2,32,48,4,128]{4,3,2,1,0:T(4,128)(2,1)} %reshape.78) | data formatting | bytes 6291456 | tf_op jit(solution)/shard_map/reshape | solution.py:90
  148.7 4.9 %all-to-all-start.2 = ((bf16[2,128,48,128]{3,2,0,1:T(8,128)(2,1)}), bf16[2,128,48,128]{3,2,0,1:T(8,128)(2,1)}, u32[]{:S(2)}, u32[]{:S(2)}) async-start(bf16[2,128,48,128]{3,2,0,1:T(8,128)(2,1)} %bitcast.20), calls=%async_computation.2 | async-start | bytes 6291456 | tf_op jit(solution)/shard_map/all_to_all | solution.py:20
  153.6 0.0 copy-start.2
  153.7 5.0 %broadcast_select_fusion = (f32[2,512,512]{2,1,0:T(8,128)}, f32[2,512,512]{2,1,0:T(8,128)S(1)}) fusion(pred[2]{0:T(512)(128)(4,1)S(1)} %compare_reduce_fusion, bf16[2,1536,512]{2,1,0:T(8,128)(2,1)S(1)} %reshape.77, f32[2,512,512]{2,1,0:T(8,128)} %param.8), kind=kOutput, calls=%fused_computation.19 | convolution fusion | flops 1612709888 | bytes 9437186 | tf_op jit(solution)/shard_map/cri,crj->cij/dot_general | solution.py:62
  158.7 0.0 copy-done.2
  158.7 3.7 %multiply_reduce_fusion = (f32[2]{0:T(128)S(1)}, f32[2,512,512]{2,1,0:T(8,128)S(1)}) fusion(f32[2,512,512]{2,1,0:T(8,128)S(1)} %get-tuple-element.8, f32[2,512,512]{2,1,0:T(8,128)S(1)} %copy-done.2), kind=kOutput, calls=%fused_computation.11 | convolution fusion | flops 3222274048 | bytes 6291464 | tf_op jit(solution)/shard_map/cij,cjk->cik/dot_general | solution.py:67
  162.5 2.8 %multiply_subtract_fusion = f32[2,512,512]{2,1,0:T(8,128)} fusion(f32[2,512,512]{2,1,0:T(8,128)S(1)} %get-tuple-element.10, f32[2]{0:T(128)S(1)} %sqrt_multiply_fusion), kind=kOutput, calls=%fused_computation.10 | convolution fusion | flops 1078460416 | bytes 4194312 | tf_op jit(solution)/shard_map/cik,ckj->cij/dot_general | solution.py:13
  165.2 6.4 %subtract_select_fusion = f32[2,512,512]{2,1,0:T(8,128)} fusion(f32[2,512,512]{2,1,0:T(8,128)} %multiply_subtract_fusion, pred[2]{0:T(512)(128)(4,1)S(1)} %compare_reduce_fusion), kind=kOutput, calls=%fused_computation.9 | convolution fusion | flops 1077411840 | bytes 4194306 | tf_op jit(solution)/shard_map/cik,ckj->cij/dot_general | solution.py:13
  171.6 23.3 %all-to-all-done.2 = bf16[2,128,48,128]{3,2,0,1:T(8,128)(2,1)} async-done(((bf16[2,128,48,128]{3,2,0,1:T(8,128)(2,1)}), bf16[2,128,48,128]{3,2,0,1:T(8,128)(2,1)}, u32[]{:S(2)}, u32[]{:S(2)}) %all-to-all-start.2) | async-done | bytes 3145760 | tf_op jit(solution)/shard_map/all_to_all | solution.py:20
  194.9 2.4 %copy.51 = bf16[2,128,48,128]{3,2,1,0:T(8,128)(2,1)S(1)} copy(bf16[2,128,48,128]{3,2,0,1:T(8,128)(2,1)} %all-to-all-done.2) | data formatting | bytes 6291456 | tf_op jit(solution)/shard_map/all_to_all | solution.py:20
  197.3 2.2 %gather_fusion.2 = bf16[160,48,128]{2,1,0:T(8,128)(2,1)} fusion(bf16[256,48,128]{2,1,0:T(8,128)(2,1)S(1)} %bitcast.23, s32[1024]{0:T(1024)S(1)} %pad_clamp_fusion), kind=kCustom, calls=%fused_computation.2 | custom fusion | bytes 3932800 | tf_op jit(solution)/shard_map/jit(_take)/gather | solution.py:92
  (6 shorter events, 0.0 us)
Async XLA Ops:
  5.2 2.7 %copy-start.1 = (bf16[160,48,128]{2,1,0:T(8,128)(2,1)}, bf16[160,48,128]{2,1,0:T(8,128)(2,1)S(1)}, u32[]{:S(2)}) copy-start(bf16[160,48,128]{2,1,0:T(8,128)(2,1)S(1)} %add_convert_fusion) | copy-start | bytes 5898244
  12.0 11.9 %copy-start = (bf16[160,48,128]{2,1,0:T(8,128)(2,1)S(1)}, bf16[160,48,128]{2,1,0:T(8,128)(2,1)}, u32[]{:S(2)}) copy-start(bf16[160,48,128]{2,1,0:T(8,128)(2,1)} %param.6) | copy-start | bytes 5898244
  12.0 53.3 %all-to-all-start = ((bf16[2,128,48,128]{3,2,0,1:T(8,128)(2,1)}), bf16[2,128,48,128]{3,2,0,1:T(8,128)(2,1)}, u32[]{:S(2)}, u32[]{:S(2)}) async-start(bf16[2,128,48,128]{3,2,0,1:T(8,128)(2,1)} %copy.43), calls=%async_computation | async-start | bytes 6291456 | tf_op jit(solution)/shard_map/all_to_all | solution.py:20
  65.3 45.6 %all-to-all-start.1 = ((bf16[2,128,48,128]{3,2,0,1:T(8,128)(2,1)}), bf16[2,128,48,128]{3,2,0,1:T(8,128)(2,1)S(1)}, u32[]{:S(2)}, u32[]{:S(2)}) async-start(bf16[2,128,48,128]{3,2,0,1:T(8,128)(2,1)} %copy.46), calls=%async_computation.1 | async-start | bytes 6291456 | tf_op jit(solution)/shard_map/all_to_all | solution.py:20
  148.7 46.2 %all-to-all-start.2 = ((bf16[2,128,48,128]{3,2,0,1:T(8,128)(2,1)}), bf16[2,128,48,128]{3,2,0,1:T(8,128)(2,1)}, u32[]{:S(2)}, u32[]{:S(2)}) async-start(bf16[2,128,48,128]{3,2,0,1:T(8,128)(2,1)} %bitcast.20), calls=%async_computation.2 | async-start | bytes 6291456 | tf_op jit(solution)/shard_map/all_to_all | solution.py:20
  153.6 5.1 %copy-start.2 = (f32[2,512,512]{2,1,0:T(8,128)S(1)}, f32[2,512,512]{2,1,0:T(8,128)}, u32[]{:S(2)}) copy-start(f32[2,512,512]{2,1,0:T(8,128)} %param.9) | copy-start | bytes 6291460

commit v2 on v1

v2 whole, which is shorter than its diff:
```python
import jax
import jax.numpy as jnp
from jax import lax
from jax.sharding import PartitionSpec as P


def refine(iterate):
    for sweep in range(2):
        iter_b = iterate.astype(jnp.bfloat16)
        square = jnp.einsum(
            "cki,ckj->cij", iter_b, iter_b, preferred_element_type=jnp.float32
        ).astype(jnp.bfloat16)
        iterate = 1.5 * iterate - 0.5 * jnp.einsum(
            "cik,ckj->cij", iter_b, square, preferred_element_type=jnp.float32
        )
    return iterate


def exchange(pieces):
    return lax.all_to_all(
        pieces, ("tensor", "owner"), split_axis=0, concat_axis=0, tiled=True
    )


def local(gradients, moments, stats, bases, second, owner_list):
    matrices, piece_rows, piece_cols = gradients.shape
    capacity = stats.shape[0]
    owners = lax.axis_size("owner")
    tensors = lax.axis_size("tensor")
    devices = owners * tensors
    myself = lax.axis_index(("owner", "tensor"))
    matrix_ids = jnp.arange(matrices, dtype=jnp.int32)
    shared = owner_list[:, None] == owner_list[None, :]
    earlier = matrix_ids[:, None] < matrix_ids[None, :]
    position = jnp.sum((shared & earlier).astype(jnp.int32), axis=0)
    slot_id = owner_list * capacity + position
    place = jnp.arange(devices, dtype=jnp.int32)
    device_at = (place % owners) * tensors + place // owners
    targets = device_at[:, None] * capacity + jnp.arange(capacity, dtype=jnp.int32)[None, :]
    hit = targets[:, :, None] == slot_id[None, None, :]
    which = jnp.sum(jnp.where(hit, matrix_ids[None, None, :], 0), axis=2)

    got_grads = [exchange(jnp.take(gradients, which[:, c], axis=0, mode="clip")) for c in range(capacity)]
    new_moments = (0.9 * moments.astype(jnp.float32) + 0.1 * gradients.astype(jnp.float32)).astype(
        jnp.bfloat16
    )
    got_moms = [exchange(jnp.take(new_moments, which[:, c], axis=0, mode="clip")) for c in range(capacity)]

    def column_blocks(pieces):
        return pieces.reshape(tensors, owners * piece_rows, piece_cols)

    full_rows = owners * piece_rows
    full_cols = tensors * piece_cols
    basis_b = bases.astype(jnp.bfloat16)
    returned, stat_list, second_list = [], [], []
    for c in range(capacity):
        grad_b = column_blocks(got_grads[c])
        basis_rows = basis_b[c].reshape(tensors, piece_cols, full_cols)
        gram = jnp.einsum(
            "tik,sil->tksl", grad_b, grad_b, preferred_element_type=jnp.float32
        ).reshape(full_cols, full_cols)
        stat_list.append(0.95 * stats[c] + 0.05 / full_rows * gram)
        rotated = jnp.einsum(
            "tik,tkj->ij", grad_b, basis_rows, preferred_element_type=jnp.float32
        )
        second_next = 0.95 * second[c].astype(jnp.float32) + 0.05 * rotated * rotated
        second_list.append(second_next)
        moment_rot = jnp.einsum(
            "tik,tkj->ij", column_blocks(got_moms[c]), basis_rows,
            preferred_element_type=jnp.float32,
        )
        scaled = (moment_rot / (jnp.sqrt(second_next) + 1e-06)).astype(jnp.bfloat16)
        step_b = jnp.einsum(
            "ij,tkj->tik", scaled, basis_rows, preferred_element_type=jnp.float32
        ).astype(jnp.bfloat16)
        returned.append(exchange(step_b.reshape(devices, piece_rows, piece_cols)))
    owner_place = (owner_list % tensors) * owners + owner_list // tensors
    update = jnp.take(
        jnp.concatenate(returned, axis=0), position * devices + owner_place, axis=0, mode="clip"
    )

    stat_next = jnp.stack(stat_list)
    second_next = jnp.stack(second_list)
    power = jnp.einsum(
        "cij,cjk->cik",
        stat_next,
        bases,
        precision=lax.Precision.HIGHEST,
        preferred_element_type=jnp.float32,
    )
    iterate = power / (
        2.0 * jnp.sqrt(full_cols * jnp.mean(power * power, axis=(1, 2), keepdims=True) + 1e-06)
    )
    iterate = refine(iterate)

    my_slots = myself * capacity + jnp.arange(capacity, dtype=jnp.int32)
    filled = jnp.any(my_slots[:, None] == slot_id[None, :], axis=1)[:, None, None]
    new_stats = jnp.where(filled, stat_next, 0.0)
    new_bases = jnp.where(filled, iterate, 0.0)
    new_second = jnp.where(filled, second_next, 0.0).astype(jnp.bfloat16)
    return (new_moments, update, new_stats, new_bases, new_second)


def solution(mesh):
    placed = (
        P(None, "owner", "tensor"),
        P(None, "owner", "tensor"),
        P(("owner", "tensor"), None, None),
        P(("owner", "tensor"), None, None),
        P(("owner", "tensor"), None, None),
        P(),
    )
    return jax.shard_map(
        local,
        mesh=mesh,
        in_specs=placed,
        out_specs=(
            P(None, "owner", "tensor"),
            P(None, "owner", "tensor"),
            P(("owner", "tensor"), None, None),
            P(("owner", "tensor"), None, None),
            P(("owner", "tensor"), None, None),
        ),
        check_vma=False,
    )
```

time: 200 us -> 198 us (0.990)
  local copies, waits for them, and re-layouts: 46 us -> 20 us
  starting transfers between devices: 20.7 us -> 36.5 us
  other arithmetic: 4.77 us -> 19.9 us
  waiting for transfers between devices: 88.5 us -> 77.2 us
  matrix products: 38.8 us -> 42.7 us
    reshape x4 -> x0, local copies, waits for them, and re-layouts: 19.4 us -> none  [the longest x2 9.76 us: assemble(): blocks.transpose(0, 1, 3, 2, 4)]
    all_to_all x3 -> x6, starting transfers between devices: 20.7 us -> 36.5 us  [exchange(): lax.all_to_all(pieces, ('tensor', 'owner'), split_axis=0, concat_axis=0,...]
    all_to_all x3 -> x6, waiting for transfers between devices: 88.5 us -> 77.2 us  [exchange(): lax.all_to_all(pieces, ('tensor', 'owner'), split_axis=0, concat_axis=0,...]
    transpose x2 -> x0, local copies, waits for them, and re-layouts: 8.45 us -> none  [assemble(): blocks.transpose(0, 1, 3, 2, 4)]
    convert_element_type x0 -> x2, other arithmetic: none -> 8.24 us  [the longest x1 5.43 us: local(): new_second = jnp.where(filled, second_next, 0.0).astype(jnp.bfloat16)]
    dot_general x2, matrix products: 9.14 us -> 12.8 us  [refine(): jnp.einsum('cik,ckj->cij', iter_b, square, preferred_element_type=jnp.flo...]
    select_n x0 -> x1, other arithmetic: none -> 3.38 us  [local(): new_stats = jnp.where(filled, stat_next, 0.0)]
    dot_general x0 -> x2, local copies, waits for them, and re-layouts: none -> 3.12 us  [local(): jnp.einsum('tik,sil->tksl', grad_b, grad_b, preferred_element_type=jnp.fl...]
  transfers between devices with their start and end apart: 3 -> 6, of which waited for: 3 -> 6; matrix products, arithmetic and copies ran while one was open for 18% -> 36% of each run, Pallas kernels for 0% -> 0%
where the time goes in v2:
time: 198 us; the launch traced here: 197 us
  waiting for transfers between devices  77.2 us (39%)
  matrix products  42.7 us (22%)
  starting transfers between devices  36.5 us (18%)
  local copies, waits for them, and re-layouts  20 us (10%)
  other arithmetic  19.9 us (10%)
    all_to_all x6, waiting for transfers between devices, exchange(): lax.all_to_all(pieces, ('tensor', 'owner'), split_axis=0, concat_axis=0,...  77.2 us
    all_to_all x6, starting transfers between devices, exchange(): lax.all_to_all(pieces, ('tensor', 'owner'), split_axis=0, concat_axis=0,...  36.5 us
    dot_general x2, matrix products, refine(): jnp.einsum('cik,ckj->cij', iter_b, square, preferred_element_type=jnp.flo...  12.8 us
    dot_general x2, matrix products, local(): jnp.einsum('ij,tkj->tik', scaled, basis_rows, preferred_element_type=jnp....  12 us
    dot_general x2, matrix products, local(): jnp.einsum('tik,sil->tksl', grad_b, grad_b, preferred_element_type=jnp.fl...  7.56 us
    dot_general x2, matrix products, local(): jnp.einsum('tik,tkj->ij', grad_b, basis_rows, preferred_element_type=jnp....  5.61 us
    convert_element_type x1, other arithmetic, local(): new_second = jnp.where(filled, second_next, 0.0).astype(jnp.bfloat16)  5.43 us
    gather x2, local copies, waits for them, and re-layouts, local(): jnp.take(new_moments, which[:, c], axis=0, mode='clip')  5.34 us
  transfers between devices with their start and end apart: 6, of which 6 were waited for; matrix products, arithmetic and copies ran while one was open for 36% of the time, Pallas kernels for 0%

profile of v2, /device:TPU:1, one launch (start us, length us, event | category | flops | bytes accessed | tf_op | source)
XLA Modules:
  0.0 197.2 jit_solution(11827694421602638952)
XLA Ops:
  0.6 0.9 convert_reduce_fusion
  1.5 0.7 fusion.22
  2.2 0.1 select_reduce_fusion
  2.3 0.5 slice_bitcast_fusion.1
  2.8 3.4 %gather_fusion.1 = bf16[128,48,128]{2,1,0:T(8,128)(2,1)} fusion(bf16[160,48,128]{2,1,0:T(8,128)(2,1)} %param.6, s32[1024]{0:T(1024)S(1)} %pad_clamp_fusion.2), kind=kCustom, calls=%fused_computation.1 | custom fusion | bytes 3146240 | tf_op jit(solution)/shard_map/jit(_take)/gather | solution.py:43
  6.3 11.5 %all-to-all-start.1 = ((bf16[128,48,128]{2,1,0:T(8,128)(2,1)}), bf16[128,48,128]{2,1,0:T(8,128)(2,1)S(1)}, u32[]{:S(2)}, u32[]{:S(2)}) async-start(bf16[128,48,128]{2,1,0:T(8,128)(2,1)} %gather_fusion.1), calls=%async_computation.1 | async-start | bytes 3145728 | tf_op jit(solution)/shard_map/all_to_all | solution.py:20
  17.8 0.7 pad_clamp_fusion.1
  18.4 0.0 copy-done
  18.4 1.9 gather_fusion.3
  20.3 22.3 %all-to-all-done.1 = bf16[128,48,128]{2,1,0:T(8,128)(2,1)S(1)} async-done(((bf16[128,48,128]{2,1,0:T(8,128)(2,1)}), bf16[128,48,128]{2,1,0:T(8,128)(2,1)S(1)}, u32[]{:S(2)}, u32[]{:S(2)}) %all-to-all-start.1) | async-done | bytes 1572896 | tf_op jit(solution)/shard_map/all_to_all | solution.py:20
  42.6 1.1 copy-done.3
  43.8 4.4 %all-to-all-start.4 = ((bf16[128,48,128]{2,1,0:T(8,128)(2,1)}), bf16[128,48,128]{2,1,0:T(8,128)(2,1)S(1)}, u32[]{:S(2)}, u32[]{:S(2)}) async-start(bf16[128,48,128]{2,1,0:T(8,128)(2,1)} %gather_fusion.3), calls=%async_computation.4 | async-start | bytes 3145728 | tf_op jit(solution)/shard_map/all_to_all | solution.py:20
  48.2 3.6 %add_convert_fusion = bf16[160,48,128]{2,1,0:T(8,128)(2,1)} fusion(bf16[160,48,128]{2,1,0:T(8,128)(2,1)S(1)} %copy-done, bf16[160,48,128]{2,1,0:T(8,128)(2,1)} %param.7), kind=kLoop, calls=%fused_computation.9 | loop fusion | flops 5898240 | bytes 5898240 | tf_op jit(solution)/shard_map/convert_element_type | solution.py:44
  51.7 3.4 %gather_fusion = bf16[128,48,128]{2,1,0:T(8,128)(2,1)} fusion(bf16[160,48,128]{2,1,0:T(8,128)(2,1)} %add_convert_fusion, s32[1024]{0:T(1024)S(1)} %pad_clamp_fusion.2), kind=kCustom, calls=%fused_computation | custom fusion | bytes 3146240 | tf_op jit(solution)/shard_map/jit(_take)/gather | solution.py:47
  55.2 18.0 %all-to-all-done.4 = bf16[128,48,128]{2,1,0:T(8,128)(2,1)S(1)} async-done(((bf16[128,48,128]{2,1,0:T(8,128)(2,1)}), bf16[128,48,128]{2,1,0:T(8,128)(2,1)S(1)}, u32[]{:S(2)}, u32[]{:S(2)}) %all-to-all-start.4) | async-done | bytes 1572896 | tf_op jit(solution)/shard_map/all_to_all | solution.py:20
  73.2 5.4 %all-to-all-start = ((bf16[128,48,128]{2,1,0:T(8,128)(2,1)}), bf16[128,48,128]{2,1,0:T(8,128)(2,1)}, u32[]{:S(2)}, u32[]{:S(2)}) async-start(bf16[128,48,128]{2,1,0:T(8,128)(2,1)} %gather_fusion), calls=%async_computation | async-start | bytes 3145728 | tf_op jit(solution)/shard_map/all_to_all | solution.py:20
  78.6 1.9 gather_fusion.2
  80.5 2.8 %convert_element_type.60 = bf16[2,512,512]{2,1,0:T(8,128)(2,1)} convert(f32[2,512,512]{2,1,0:T(8,128)} %param.9) | non-fusion elementwise | flops 524288 | bytes 3145728 | tf_op jit(solution)/shard_map/convert_element_type | solution.py:54
  83.3 0.2 compare_reduce_fusion
  83.5 2.3 %fusion.29 = (bf16[1,512,512]{2,1,0:T(8,128)(2,1)}, bf16[1,512,512]{2,1,0:T(8,128)(2,1)}) fusion(bf16[2,512,512]{2,1,0:T(8,128)(2,1)} %convert_element_type.60), kind=kLoop, calls=%fused_computation.74 | loop fusion | bytes 2097152 | tf_op jit(solution)/shard_map/slice | solution.py:58
  85.8 0.0 copy-done.4
  85.8 1.6 copy.13
  87.3 1.6 copy.14
  88.9 4.2 %fusion.12 = f32[1,512,512]{2,1,0:T(8,128)} fusion(bf16[512,1536]{1,0:T(8,128)(2,1)} %bitcast.95, f32[2,512,512]{2,1,0:T(8,128)} %param.8), kind=kOutput, calls=%fused_computation.36 | convolution fusion | flops 806092800 | bytes 5242880 | tf_op jit(solution)/shard_map/tik,sil->tksl/dot_general | solution.py:59
  93.1 10.1 %all-to-all-done = bf16[128,48,128]{2,1,0:T(8,128)(2,1)} async-done(((bf16[128,48,128]{2,1,0:T(8,128)(2,1)}), bf16[128,48,128]{2,1,0:T(8,128)(2,1)}, u32[]{:S(2)}, u32[]{:S(2)}) %all-to-all-start) | async-done | bytes 1572896 | tf_op jit(solution)/shard_map/all_to_all | solution.py:20
  103.2 5.4 %all-to-all-start.3 = ((bf16[128,48,128]{2,1,0:T(8,128)(2,1)}), bf16[128,48,128]{2,1,0:T(8,128)(2,1)}, u32[]{:S(2)}, u32[]{:S(2)}) async-start(bf16[128,48,128]{2,1,0:T(8,128)(2,1)} %gather_fusion.2), calls=%async_computation.3 | async-start | bytes 3145728 | tf_op jit(solution)/shard_map/all_to_all | solution.py:20
  108.7 0.0 copy-start.2
  108.7 3.3 %fusion.14 = f32[1,512,512]{2,1,0:T(8,128)S(1)} fusion(bf16[512,1536]{1,0:T(8,128)(2,1)} %bitcast.94, f32[2,512,512]{2,1,0:T(8,128)} %param.8), kind=kOutput, calls=%fused_computation.38 | convolution fusion | flops 806092800 | bytes 5242880 | tf_op jit(solution)/shard_map/tik,sil->tksl/dot_general | solution.py:59
  112.1 0.0 copy-start.10
  112.1 4.8 %multiply_reduce_fusion = (f32[2]{0:T(128)S(1)}, f32[2,512,512]{2,1,0:T(8,128)}) fusion(f32[2,512,512]{2,1,0:T(8,128)S(1)} %copy-done.2, f32[1,512,512]{2,1,0:T(8,128)S(1)} %fusion.14, f32[1,512,512]{2,1,0:T(8,128)S(1)} %copy-done.6), kind=kOutput, calls=%fused_computation.26 | convolution fusion | flops 3222798336 | bytes 6291464 | tf_op jit(solution)/shard_map/cij,cjk->cik/dot_general | solution.py:84
  116.9 2.8 %fusion.2 = f32[1536,512]{1,0:T(8,128)} fusion(bf16[4,1536,128]{2,1,0:T(8,128)(2,1)S(1)} %bitcast.90, bf16[4,128,512]{2,1,0:T(8,128)(2,1)S(1)} %bitcast.99, bf16[2,1536,512]{2,1,0:T(8,128)(2,1)S(1)} %copy-done.10), kind=kOutput, calls=%fused_computation.14 | convolution fusion | flops 809238528 | bytes 6815744 | tf_op jit(solution)/shard_map/tik,tkj->ij/dot_general | solution.py:63
  119.7 6.0 %convolution_convert_fusion.1 = bf16[1536,4,128]{2,0,1:T(8,128)(2,1)} fusion(bf16[4,128,512]{2,1,0:T(8,128)(2,1)} %bitcast.98, f32[1536,512]{1,0:T(8,128)} %fusion.2, bf16[4,1536,128]{2,1,0:T(8,128)(2,1)} %bitcast.1), kind=kOutput, calls=%fused_computation.20 | convolution fusion | flops 1613758464 | bytes 6815744 | tf_op jit(solution)/shard_map/ij,tkj->tik/dot_general | solution.py:73
  125.7 7.6 %all-to-all-done.3 = bf16[128,48,128]{2,1,0:T(8,128)(2,1)} async-done(((bf16[128,48,128]{2,1,0:T(8,128)(2,1)}), bf16[128,48,128]{2,1,0:T(8,128)(2,1)}, u32[]{:S(2)}, u32[]{:S(2)}) %all-to-all-start.3) | async-done | bytes 1572896 | tf_op jit(solution)/shard_map/all_to_all | solution.py:20
  133.3 4.4 %all-to-all-start.2 = ((bf16[128,48,128]{2,1,0:T(8,128)(2,1)}), bf16[128,48,128]{2,1,0:T(8,128)(2,1)S(1)}, u32[]{:S(2)}, u32[]{:S(2)}) async-start(bf16[128,48,128]{2,1,0:T(8,128)(2,1)} %bitcast.93), calls=%async_computation.2 | async-start | bytes 3145728 | tf_op jit(solution)/shard_map/all_to_all | solution.py:20
  137.8 0.0 copy-start.8
  137.8 0.0 copy-start.11
  137.8 3.4 %fusion.6 = f32[2,512,512]{2,1,0:T(8,128)} fusion(f32[1,512,512]{2,1,0:T(8,128)} %copy-done.7, f32[1,512,512]{2,1,0:T(8,128)} %fusion.12, pred[2]{0:T(512)(128)(4,1)S(1)} %compare_reduce_fusion), kind=kLoop, calls=%fused_computation.28 | loop fusion | flops 1048576 | bytes 4194306 | tf_op jit(solution)/shard_map/jit(_where)/select_n | solution.py:98
  141.2 0.0 copy-done.11
  141.2 2.8 %fusion.1 = f32[1536,512]{1,0:T(8,128)} fusion(bf16[4,1536,128]{2,1,0:T(8,128)(2,1)S(1)} %bitcast.88, bf16[4,128,512]{2,1,0:T(8,128)(2,1)S(1)} %bitcast.97, bf16[2,1536,512]{2,1,0:T(8,128)(2,1)S(1)} %copy-done.11), kind=kOutput, calls=%fused_computation.11 | convolution fusion | flops 809238528 | bytes 6815744 | tf_op jit(solution)/shard_map/tik,tkj->ij/dot_general | solution.py:63
  144.0 6.0 %convolution_convert_fusion = bf16[1536,4,128]{2,0,1:T(8,128)(2,1)} fusion(bf16[4,128,512]{2,1,0:T(8,128)(2,1)} %bitcast.96, f32[1536,512]{1,0:T(8,128)} %fusion.1, bf16[4,1536,128]{2,1,0:T(8,128)(2,1)} %bitcast.11), kind=kOutput, calls=%fused_computation.19 | convolution fusion | flops 1613758464 | bytes 6815744 | tf_op jit(solution)/shard_map/ij,tkj->tik/dot_general | solution.py:73
  150.0 12.8 %all-to-all-done.2 = bf16[128,48,128]{2,1,0:T(8,128)(2,1)S(1)} async-done(((bf16[128,48,128]{2,1,0:T(8,128)(2,1)}), bf16[128,48,128]{2,1,0:T(8,128)(2,1)S(1)}, u32[]{:S(2)}, u32[]{:S(2)}) %all-to-all-start.2) | async-done | bytes 1572896 | tf_op jit(solution)/shard_map/all_to_all | solution.py:20
  162.7 5.4 %all-to-all-start.5 = ((bf16[128,48,128]{2,1,0:T(8,128)(2,1)}), bf16[128,48,128]{2,1,0:T(8,128)(2,1)}, u32[]{:S(2)}, u32[]{:S(2)}) async-start(bf16[128,48,128]{2,1,0:T(8,128)(2,1)} %bitcast.19), calls=%async_computation.5 | async-start | bytes 3145728 | tf_op jit(solution)/shard_map/all_to_all | solution.py:20
  168.1 6.4 %multiply_subtract_fusion = f32[2,512,512]{2,1,0:T(8,128)} fusion(f32[2,512,512]{2,1,0:T(8,128)} %get-tuple-element.12, f32[2]{0:T(128)S(1)} %sqrt_multiply_fusion), kind=kOutput, calls=%fused_computation.25 | convolution fusion | flops 1078460416 | bytes 4194312 | tf_op jit(solution)/shard_map/cik,ckj->cij/dot_general | solution.py:13
  174.6 6.3 %subtract_select_fusion = f32[2,512,512]{2,1,0:T(8,128)} fusion(f32[2,512,512]{2,1,0:T(8,128)} %multiply_subtract_fusion, pred[2]{0:T(512)(128)(4,1)S(1)} %compare_reduce_fusion), kind=kOutput, calls=%fused_computation.24 | convolution fusion | flops 1077411840 | bytes 4194306 | tf_op jit(solution)/shard_map/cik,ckj->cij/dot_general | solution.py:13
  180.9 5.4 %fusion = bf16[2,1536,512]{2,1,0:T(8,128)(2,1)} fusion(f32[1,1536,512]{2,1,0:T(8,128)} %bitcast.92, f32[1,1536,512]{2,1,0:T(8,128)} %bitcast.91, pred[2]{0:T(512)(128)(4,1)S(1)} %compare_reduce_fusion), kind=kLoop, calls=%fused_computation.6 | loop fusion | flops 7864320 | bytes 9437186 | tf_op jit(solution)/shard_map/convert_element_type | solution.py:100
  186.4 6.5 %all-to-all-done.5 = bf16[128,48,128]{2,1,0:T(8,128)(2,1)} async-done(((bf16[128,48,128]{2,1,0:T(8,128)(2,1)}), bf16[128,48,128]{2,1,0:T(8,128)(2,1)}, u32[]{:S(2)}, u32[]{:S(2)}) %all-to-all-start.5) | async-done | bytes 1572896 | tf_op jit(solution)/shard_map/all_to_all | solution.py:20
  192.8 2.2 %pad_maximum_fusion = bf16[256,48,128]{2,1,0:T(8,128)(2,1)S(1)} fusion(bf16[128,48,128]{2,1,0:T(8,128)(2,1)} %all-to-all-done.5, bf16[128,48,128]{2,1,0:T(8,128)(2,1)} %copy-done.5), kind=kLoop, calls=%fused_computation.16 | loop fusion | flops 1572864 | bytes 6291456 | tf_op jit(solution)/shard_map/concatenate | solution.py:79
  195.0 2.2 %gather_fusion.4 = bf16[160,48,128]{2,1,0:T(8,128)(2,1)} fusion(bf16[256,48,128]{2,1,0:T(8,128)(2,1)S(1)} %pad_maximum_fusion, s32[1024]{0:T(1024)S(1)} %pad_clamp_fusion), kind=kCustom, calls=%fused_computation.4 | custom fusion | bytes 3932800 | tf_op jit(solution)/shard_map/jit(_take)/gather | solution.py:78
  (22 shorter events, 0.1 us)
Async XLA Ops:
  6.3 12.2 %copy-start = (bf16[160,48,128]{2,1,0:T(8,128)(2,1)S(1)}, bf16[160,48,128]{2,1,0:T(8,128)(2,1)}, u32[]{:S(2)}) copy-start(bf16[160,48,128]{2,1,0:T(8,128)(2,1)} %param.6) | copy-start | bytes 5898244
  6.3 36.3 %all-to-all-start.1 = ((bf16[128,48,128]{2,1,0:T(8,128)(2,1)}), bf16[128,48,128]{2,1,0:T(8,128)(2,1)S(1)}, u32[]{:S(2)}, u32[]{:S(2)}) async-start(bf16[128,48,128]{2,1,0:T(8,128)(2,1)} %gather_fusion.1), calls=%async_computation.1 | async-start | bytes 3145728 | tf_op jit(solution)/shard_map/all_to_all | solution.py:20
  42.6 1.1 copy-start.3
  43.8 29.4 %all-to-all-start.4 = ((bf16[128,48,128]{2,1,0:T(8,128)(2,1)}), bf16[128,48,128]{2,1,0:T(8,128)(2,1)S(1)}, u32[]{:S(2)}, u32[]{:S(2)}) async-start(bf16[128,48,128]{2,1,0:T(8,128)(2,1)} %gather_fusion.3), calls=%async_computation.4 | async-start | bytes 3145728 | tf_op jit(solution)/shard_map/all_to_all | solution.py:20
  55.2 23.4 %copy-start.1 = (bf16[160,48,128]{2,1,0:T(8,128)(2,1)S(1)}, bf16[160,48,128]{2,1,0:T(8,128)(2,1)}, u32[]{:S(2)}) copy-start(bf16[160,48,128]{2,1,0:T(8,128)(2,1)} %add_convert_fusion) | copy-start | bytes 5898244
  73.2 30.1 %all-to-all-start = ((bf16[128,48,128]{2,1,0:T(8,128)(2,1)}), bf16[128,48,128]{2,1,0:T(8,128)(2,1)}, u32[]{:S(2)}, u32[]{:S(2)}) async-start(bf16[128,48,128]{2,1,0:T(8,128)(2,1)} %gather_fusion), calls=%async_computation | async-start | bytes 3145728 | tf_op jit(solution)/shard_map/all_to_all | solution.py:20
  80.5 5.3 %copy-start.4 = (bf16[128,48,128]{2,1,0:T(8,128)(2,1)S(1)}, bf16[128,48,128]{2,1,0:T(8,128)(2,1)}, u32[]{:S(2)}) copy-start(bf16[128,48,128]{2,1,0:T(8,128)(2,1)} %copy-done.3) | copy-start | bytes 4718596
  103.2 30.1 %all-to-all-start.3 = ((bf16[128,48,128]{2,1,0:T(8,128)(2,1)}), bf16[128,48,128]{2,1,0:T(8,128)(2,1)}, u32[]{:S(2)}, u32[]{:S(2)}) async-start(bf16[128,48,128]{2,1,0:T(8,128)(2,1)} %gather_fusion.2), calls=%async_computation.3 | async-start | bytes 3145728 | tf_op jit(solution)/shard_map/all_to_all | solution.py:20
  108.7 3.4 %copy-start.2 = (f32[2,512,512]{2,1,0:T(8,128)S(1)}, f32[2,512,512]{2,1,0:T(8,128)}, u32[]{:S(2)}) copy-start(f32[2,512,512]{2,1,0:T(8,128)} %param.9) | copy-start | bytes 6291460
  108.7 3.4 %copy-start.6 = (f32[1,512,512]{2,1,0:T(8,128)S(1)}, f32[1,512,512]{2,1,0:T(8,128)}, u32[]{:S(2)}) copy-start(f32[1,512,512]{2,1,0:T(8,128)} %fusion.12) | copy-start | bytes 3145732
  112.1 4.9 %copy-start.7 = (f32[1,512,512]{2,1,0:T(8,128)}, f32[1,512,512]{2,1,0:T(8,128)S(1)}, u32[]{:S(2)}) copy-start(f32[1,512,512]{2,1,0:T(8,128)S(1)} %fusion.14) | copy-start | bytes 3145732
  112.1 4.9 %copy-start.9 = (bf16[1,512,512]{2,1,0:T(8,128)(2,1)S(1)}, bf16[1,512,512]{2,1,0:T(8,128)(2,1)}, u32[]{:S(2)}) copy-start(bf16[1,512,512]{2,1,0:T(8,128)(2,1)} %get-tuple-element.5) | copy-start | bytes 1572868
  112.1 4.8 %copy-start.10 = (bf16[2,1536,512]{2,1,0:T(8,128)(2,1)S(1)}, bf16[2,1536,512]{2,1,0:T(8,128)(2,1)}, u32[]{:S(2)}) copy-start(bf16[2,1536,512]{2,1,0:T(8,128)(2,1)} %param.10) | copy-start | bytes 9437188
  133.3 29.4 %all-to-all-start.2 = ((bf16[128,48,128]{2,1,0:T(8,128)(2,1)}), bf16[128,48,128]{2,1,0:T(8,128)(2,1)S(1)}, u32[]{:S(2)}, u32[]{:S(2)}) async-start(bf16[128,48,128]{2,1,0:T(8,128)(2,1)} %bitcast.93), calls=%async_computation.2 | async-start | bytes 3145728 | tf_op jit(solution)/shard_map/all_to_all | solution.py:20
  137.8 3.4 %copy-start.8 = (bf16[1,512,512]{2,1,0:T(8,128)(2,1)S(1)}, bf16[1,512,512]{2,1,0:T(8,128)(2,1)}, u32[]{:S(2)}) copy-start(bf16[1,512,512]{2,1,0:T(8,128)(2,1)} %get-tuple-element.6) | copy-start | bytes 1572868
  137.8 3.4 %copy-start.11 = (bf16[2,1536,512]{2,1,0:T(8,128)(2,1)S(1)}, bf16[2,1536,512]{2,1,0:T(8,128)(2,1)}, u32[]{:S(2)}) copy-start(bf16[2,1536,512]{2,1,0:T(8,128)(2,1)} %param.10) | copy-start | bytes 9437188
  162.7 11.8 %copy-start.5 = (bf16[128,48,128]{2,1,0:T(8,128)(2,1)}, bf16[128,48,128]{2,1,0:T(8,128)(2,1)S(1)}, u32[]{:S(2)}) copy-start(bf16[128,48,128]{2,1,0:T(8,128)(2,1)S(1)} %all-to-all-done.2) | copy-start | bytes 4718596
  162.7 30.1 %all-to-all-start.5 = ((bf16[128,48,128]{2,1,0:T(8,128)(2,1)}), bf16[128,48,128]{2,1,0:T(8,128)(2,1)}, u32[]{:S(2)}, u32[]{:S(2)}) async-start(bf16[128,48,128]{2,1,0:T(8,128)(2,1)} %bitcast.19), calls=%async_computation.5 | async-start | bytes 3145728 | tf_op jit(solution)/shard_map/all_to_all | solution.py:20

commit v3 on v2

--- a/solution.py
+++ b/solution.py
@@ -40,11 +40,14 @@
     hit = targets[:, :, None] == slot_id[None, None, :]
     which = jnp.sum(jnp.where(hit, matrix_ids[None, None, :], 0), axis=2)
 
-    got_grads = [exchange(jnp.take(gradients, which[:, c], axis=0, mode="clip")) for c in range(capacity)]
     new_moments = (0.9 * moments.astype(jnp.float32) + 0.1 * gradients.astype(jnp.float32)).astype(
         jnp.bfloat16
     )
-    got_moms = [exchange(jnp.take(new_moments, which[:, c], axis=0, mode="clip")) for c in range(capacity)]
+    outgoing = jnp.stack(
+        [jnp.take(gradients, which, axis=0, mode="clip"), jnp.take(new_moments, which, axis=0, mode="clip")],
+        axis=2,
+    )
+    incoming = exchange(outgoing)
 
     def column_blocks(pieces):
         return pieces.reshape(tensors, owners * piece_rows, piece_cols)
@@ -52,9 +55,9 @@
     full_rows = owners * piece_rows
     full_cols = tensors * piece_cols
     basis_b = bases.astype(jnp.bfloat16)
-    returned, stat_list, second_list = [], [], []
+    steps, stat_list, second_list = [], [], []
     for c in range(capacity):
-        grad_b = column_blocks(got_grads[c])
+        grad_b = column_blocks(incoming[:, c, 0])
         basis_rows = basis_b[c].reshape(tensors, piece_cols, full_cols)
         gram = jnp.einsum(
             "tik,sil->tksl", grad_b, grad_b, preferred_element_type=jnp.float32
@@ -66,17 +69,19 @@
         second_next = 0.95 * second[c].astype(jnp.float32) + 0.05 * rotated * rotated
         second_list.append(second_next)
         moment_rot = jnp.einsum(
-            "tik,tkj->ij", column_blocks(got_moms[c]), basis_rows,
+            "tik,tkj->ij", column_blocks(incoming[:, c, 1]), basis_rows,
             preferred_element_type=jnp.float32,
         )
         scaled = (moment_rot / (jnp.sqrt(second_next) + 1e-06)).astype(jnp.bfloat16)
         step_b = jnp.einsum(
             "ij,tkj->tik", scaled, basis_rows, preferred_element_type=jnp.float32
         ).astype(jnp.bfloat16)
-        returned.append(exchange(step_b.reshape(devices, piece_rows, piece_cols)))
+        steps.append(step_b.reshape(devices, piece_rows, piece_cols))
+    returned = exchange(jnp.stack(steps, axis=1))
     owner_place = (owner_list % tensors) * owners + owner_list // tensors
     update = jnp.take(
-        jnp.concatenate(returned, axis=0), position * devices + owner_place, axis=0, mode="clip"
+        returned.reshape(devices * capacity, piece_rows, piece_cols),
+        owner_place * capacity + position, axis=0, mode="clip",
     )
 
     stat_next = jnp.stack(stat_list)

time: 198 us -> 189 us (0.955)
  starting transfers between devices: 36.5 us -> 20.7 us
  waiting for transfers between devices: 77.2 us -> 82.8 us
  local copies, waits for them, and re-layouts: 20 us -> 23.9 us
  matrix products: 42.7 us -> 39.2 us
    all_to_all x6 -> x2, starting transfers between devices: 36.5 us -> 20.7 us  [exchange(): lax.all_to_all(pieces, ('tensor', 'owner'), split_axis=0, concat_axis=0,...]
    another operation x0 -> x2, other arithmetic: none -> 8.9 us  [the longest x1 5.07 us: local(): jnp.stack([jnp.take(gradients, which, axis=0, mode='clip'), jnp.take(new_...]
    all_to_all x6 -> x2, waiting for transfers between devices: 77.2 us -> 82.8 us  [exchange(): lax.all_to_all(pieces, ('tensor', 'owner'), split_axis=0, concat_axis=0,...]
    slice x1, local copies, waits for them, and re-layouts: 0.52 us -> 5.59 us  [local(): incoming[:, c, 1]]
    dot_general x2, matrix products: 12.8 us -> 9.01 us  [refine(): jnp.einsum('cik,ckj->cij', iter_b, square, preferred_element_type=jnp.flo...]
    convert_element_type x1, other arithmetic: 2.81 us -> 0.13 us  [local(): basis_b = bases.astype(jnp.bfloat16)]
    concatenate x1 -> x0, other arithmetic: 2.15 us -> none  [local(): jnp.concatenate(returned, axis=0)]
    dot_general x2, local copies, waits for them, and re-layouts: 3.12 us -> 5.16 us  [local(): jnp.einsum('tik,sil->tksl', grad_b, grad_b, preferred_element_type=jnp.fl...]
  transfers between devices with their start and end apart: 6 -> 2, of which waited for: 6 -> 2; matrix products, arithmetic and copies ran while one was open for 36% -> 17% of each run, Pallas kernels for 0% -> 0%
where the time goes in v3:
time: 189 us
  waiting for transfers between devices  82.8 us (44%)
  matrix products  39.2 us (21%)
  local copies, waits for them, and re-layouts  23.9 us (13%)
  other arithmetic  21.3 us (11%)
  starting transfers between devices  20.7 us (11%)
    all_to_all x2, waiting for transfers between devices, exchange(): lax.all_to_all(pieces, ('tensor', 'owner'), split_axis=0, concat_axis=0,...  82.8 us
    all_to_all x2, starting transfers between devices, exchange(): lax.all_to_all(pieces, ('tensor', 'owner'), split_axis=0, concat_axis=0,...  20.7 us
    dot_general x2, matrix products, local(): jnp.einsum('ij,tkj->tik', scaled, basis_rows, preferred_element_type=jnp....  11.5 us
    dot_general x2, matrix products, refine(): jnp.einsum('cik,ckj->cij', iter_b, square, preferred_element_type=jnp.flo...  9.01 us
    dot_general x2, matrix products, local(): jnp.einsum('tik,tkj->ij', grad_b, basis_rows, preferred_element_type=jnp....  7.42 us
    dot_general x2, matrix products, local(): jnp.einsum('tik,sil->tksl', grad_b, grad_b, preferred_element_type=jnp.fl...  6.41 us
    slice x1, local copies, waits for them, and re-layouts, local(): incoming[:, c, 1]  5.59 us
    dot_general x2, local copies, waits for them, and re-layouts, local(): jnp.einsum('tik,sil->tksl', grad_b, grad_b, preferred_element_type=jnp.fl...  5.16 us
  transfers between devices with their start and end apart: 2, of which 2 were waited for; matrix products, arithmetic and copies ran while one was open for 17% of the time, Pallas kernels for 0%

profile of v3, /device:TPU:1, one launch (start us, length us, event | category | flops | bytes accessed | tf_op | source)
XLA Modules:
  0.0 188.7 jit_solution(16817184324292864088)
XLA Ops:
  0.7 0.9 convert_reduce_fusion
  1.5 0.7 multiply_add_fusion
  2.2 0.1 select_reduce_fusion
  2.3 0.1 copy.25
  2.4 0.1 reshape.95
  2.6 0.0 copy-start
  2.6 4.3 %add_convert_fusion = bf16[160,48,128]{2,1,0:T(8,128)(2,1)} fusion(bf16[160,48,128]{2,1,0:T(8,128)(2,1)} %param.6, bf16[160,48,128]{2,1,0:T(8,128)(2,1)} %param.7), kind=kLoop, calls=%fused_computation.8 | loop fusion | flops 5898240 | bytes 5898240 | tf_op jit(solution)/shard_map/convert_element_type | solution.py:43
  6.9 0.0 copy-done
  6.9 2.6 %gather_fusion = bf16[256,48,128]{2,1,0:T(8,128)(2,1)} fusion(bf16[160,48,128]{2,1,0:T(8,128)(2,1)S(1)} %copy-done, s32[1024]{0:T(1024)S(1)} %pad_clamp_fusion.1), kind=kCustom, calls=%fused_computation | custom fusion | bytes 6292480 | tf_op jit(solution)/shard_map/jit(_take)/gather | solution.py:47
  9.5 0.0 copy-start.1
  9.5 4.3 %gather_fusion.1 = bf16[256,48,128]{2,1,0:T(8,128)(2,1)} fusion(bf16[160,48,128]{2,1,0:T(8,128)(2,1)} %add_convert_fusion, s32[1024]{0:T(1024)S(1)} %pad_clamp_fusion.1), kind=kCustom, calls=%fused_computation.1 | custom fusion | bytes 6292480 | tf_op jit(solution)/shard_map/jit(_take)/gather | solution.py:47
  13.9 0.0 copy-done.1
  13.9 5.1 %pad_maximum_fusion = bf16[128,2,2,48,128]{4,3,2,1,0:T(8,128)(2,1)} fusion(bf16[128,2,1,48,128]{4,3,2,1,0:T(8,128)(2,1)} %bitcast.91, bf16[128,2,1,48,128]{4,3,2,1,0:T(8,128)(2,1)S(1)} %bitcast.90), kind=kLoop, calls=%fused_computation.3 | loop fusion | flops 3145728 | bytes 12582912 | tf_op jit(solution)/shard_map/stack | solution.py:46
  19.0 0.0 copy-start.2
  19.0 11.9 %all-to-all-start = ((bf16[128,2,2,48,128]{4,3,2,1,0:T(8,128)(2,1)}), bf16[128,2,2,48,128]{4,3,2,1,0:T(8,128)(2,1)}, u32[]{:S(2)}, u32[]{:S(2)}) async-start(bf16[128,2,2,48,128]{4,3,2,1,0:T(8,128)(2,1)} %pad_maximum_fusion), calls=%async_computation | async-start | bytes 12582912 | tf_op jit(solution)/shard_map/all_to_all | solution.py:20
  30.9 0.0 copy-done.2
  30.9 0.1 convert_element_type.60
  31.0 0.2 compare_reduce_fusion
  31.2 1.0 fusion.29
  32.3 0.0 copy-start.7
  32.3 73.8 %all-to-all-done = bf16[128,2,2,48,128]{4,3,2,1,0:T(8,128)(2,1)} async-done(((bf16[128,2,2,48,128]{4,3,2,1,0:T(8,128)(2,1)}), bf16[128,2,2,48,128]{4,3,2,1,0:T(8,128)(2,1)}, u32[]{:S(2)}, u32[]{:S(2)}) %all-to-all-start) | async-done | bytes 6291488 | tf_op jit(solution)/shard_map/all_to_all | solution.py:20
  106.0 0.0 copy-start.8
  106.0 5.6 %fusion.28 = (bf16[128,1,1,48,128]{4,3,2,1,0:T(8,128)(2,1)}, bf16[128,1,1,48,128]{4,3,2,1,0:T(8,128)(2,1)S(1)}, bf16[128,1,1,48,128]{4,3,2,1,0:T(8,128)(2,1)}, bf16[128,1,1,48,128]{4,3,2,1,0:T(8,128)(2,1)}) fusion(bf16[128,2,2,48,128]{4,3,2,1,0:T(8,128)(2,1)} %all-to-all-done), kind=kLoop, calls=%fused_computation.70 | loop fusion | bytes 12582912 | tf_op jit(solution)/shard_map/slice | solution.py:72
  111.6 0.0 copy-start.3
  111.6 0.0 copy-done.7
  111.6 0.0 copy-done.8
  111.7 2.8 %fusion.1 = f32[1536,512]{1,0:T(8,128)} fusion(bf16[4,1536,128]{2,1,0:T(8,128)(2,1)S(1)} %bitcast.94, bf16[4,128,512]{2,1,0:T(8,128)(2,1)S(1)} %bitcast.106, bf16[2,1536,512]{2,1,0:T(8,128)(2,1)S(1)} %copy-done.8), kind=kOutput, calls=%fused_computation.10 | convolution fusion | flops 809238528 | bytes 6815744 | tf_op jit(solution)/shard_map/tik,tkj->ij/dot_general | solution.py:66
  114.4 0.0 copy-done.3
  114.4 0.0 copy-start.6
  114.5 5.8 %convolution_convert_fusion = bf16[1536,4,128]{2,0,1:T(8,128)(2,1)} fusion(bf16[4,128,512]{2,1,0:T(8,128)(2,1)S(1)} %bitcast.107, f32[1536,512]{1,0:T(8,128)} %fusion.1, bf16[4,1536,128]{2,1,0:T(8,128)(2,1)} %bitcast.99), kind=kOutput, calls=%fused_computation.18 | convolution fusion | flops 1613758464 | bytes 6815744 | tf_op jit(solution)/shard_map/ij,tkj->tik/dot_general | solution.py:76
  120.2 0.0 copy-done.6
  120.2 4.6 %fusion.2 = f32[1536,512]{1,0:T(8,128)} fusion(bf16[4,1536,128]{2,1,0:T(8,128)(2,1)} %bitcast.92, bf16[4,128,512]{2,1,0:T(8,128)(2,1)S(1)} %bitcast.104, bf16[2,1536,512]{2,1,0:T(8,128)(2,1)} %param.10), kind=kOutput, calls=%fused_computation.13 | convolution fusion | flops 809238528 | bytes 6815744 | tf_op jit(solution)/shard_map/tik,tkj->ij/dot_general | solution.py:66
  124.9 5.7 %convolution_convert_fusion.1 = bf16[1536,4,128]{2,0,1:T(8,128)(2,1)} fusion(bf16[4,128,512]{2,1,0:T(8,128)(2,1)S(1)} %bitcast.105, f32[1536,512]{1,0:T(8,128)} %fusion.2, bf16[4,1536,128]{2,1,0:T(8,128)(2,1)} %bitcast.98), kind=kOutput, calls=%fused_computation.19 | convolution fusion | flops 1613758464 | bytes 6815744 | tf_op jit(solution)/shard_map/ij,tkj->tik/dot_general | solution.py:76
  130.6 3.8 %pad_maximum_fusion.1 = bf16[128,2,48,128]{3,2,1,0:T(8,128)(2,1)} fusion(bf16[128,1,48,128]{3,2,1,0:T(8,128)(2,1)} %bitcast.102, bf16[128,1,48,128]{3,2,1,0:T(8,128)(2,1)} %bitcast.103), kind=kLoop, calls=%fused_computation.15 | loop fusion | flops 1572864 | bytes 6291456 | tf_op jit(solution)/shard_map/stack | solution.py:80
  134.4 8.8 %all-to-all-start.1 = ((bf16[128,2,48,128]{3,2,1,0:T(8,128)(2,1)}), bf16[128,2,48,128]{3,2,1,0:T(8,128)(2,1)}, u32[]{:S(2)}, u32[]{:S(2)}) async-start(bf16[128,2,48,128]{3,2,1,0:T(8,128)(2,1)} %pad_maximum_fusion.1), calls=%async_computation.1 | async-start | bytes 6291456 | tf_op jit(solution)/shard_map/all_to_all | solution.py:20
  143.2 2.6 %copy.29 = bf16[4,128,1536]{2,1,0:T(8,128)(2,1)} copy(bf16[4,128,1536]{1,2,0:T(8,128)(2,1)} %bitcast.95) | data formatting | bytes 3145728 | tf_op jit(solution)/shard_map/tik,sil->tksl/dot_general | solution.py:62
  145.8 3.2 %fusion.14 = f32[1,512,512]{2,1,0:T(8,128)S(1)} fusion(bf16[512,1536]{1,0:T(8,128)(2,1)} %bitcast.100, f32[2,512,512]{2,1,0:T(8,128)} %param.8), kind=kOutput, calls=%fused_computation.37 | convolution fusion | flops 806092800 | bytes 5242880 | tf_op jit(solution)/shard_map/tik,sil->tksl/dot_general | solution.py:62
  149.0 2.6 %copy.28 = bf16[4,128,1536]{2,1,0:T(8,128)(2,1)} copy(bf16[4,128,1536]{1,2,0:T(8,128)(2,1)} %bitcast.93) | data formatting | bytes 3145728 | tf_op jit(solution)/shard_map/tik,sil->tksl/dot_general | solution.py:62
  151.6 3.2 %fusion.12 = f32[1,512,512]{2,1,0:T(8,128)S(1)} fusion(bf16[512,1536]{1,0:T(8,128)(2,1)} %bitcast.101, f32[2,512,512]{2,1,0:T(8,128)} %param.8), kind=kOutput, calls=%fused_computation.35 | convolution fusion | flops 806092800 | bytes 5242880 | tf_op jit(solution)/shard_map/tik,sil->tksl/dot_general | solution.py:62
  154.8 4.8 %multiply_reduce_fusion = (f32[2]{0:T(128)S(1)}, f32[2,512,512]{2,1,0:T(8,128)}) fusion(f32[2,512,512]{2,1,0:T(8,128)S(1)} %copy-done.2, f32[1,512,512]{2,1,0:T(8,128)S(1)} %fusion.14, f32[1,512,512]{2,1,0:T(8,128)S(1)} %fusion.12), kind=kOutput, calls=%fused_computation.25 | convolution fusion | flops 3222798336 | bytes 6291464 | tf_op jit(solution)/shard_map/cij,cjk->cik/dot_general | solution.py:89
  159.7 1.6 fusion.6
  161.3 0.7 copy-done.5
  162.0 2.7 %multiply_subtract_fusion = f32[2,512,512]{2,1,0:T(8,128)} fusion(f32[2,512,512]{2,1,0:T(8,128)S(1)} %copy-done.5, f32[2]{0:T(128)S(1)} %sqrt_multiply_fusion), kind=kOutput, calls=%fused_computation.24 | convolution fusion | flops 1078460416 | bytes 4194312 | tf_op jit(solution)/shard_map/cik,ckj->cij/dot_general | solution.py:13
  164.8 6.3 %subtract_select_fusion = f32[2,512,512]{2,1,0:T(8,128)} fusion(f32[2,512,512]{2,1,0:T(8,128)} %multiply_subtract_fusion, pred[2]{0:T(512)(128)(4,1)S(1)} %compare_reduce_fusion), kind=kOutput, calls=%fused_computation.23 | convolution fusion | flops 1077411840 | bytes 4194306 | tf_op jit(solution)/shard_map/cik,ckj->cij/dot_general | solution.py:13
  171.1 0.0 copy-done.4
  171.1 4.5 %fusion = bf16[2,1536,512]{2,1,0:T(8,128)(2,1)} fusion(f32[1,1536,512]{2,1,0:T(8,128)S(1)} %bitcast.96, f32[1,1536,512]{2,1,0:T(8,128)} %bitcast.97, pred[2]{0:T(512)(128)(4,1)S(1)} %compare_reduce_fusion), kind=kLoop, calls=%fused_computation.5 | loop fusion | flops 7864320 | bytes 9437186 | tf_op jit(solution)/shard_map/convert_element_type | solution.py:105
  175.5 9.0 %all-to-all-done.1 = bf16[128,2,48,128]{3,2,1,0:T(8,128)(2,1)} async-done(((bf16[128,2,48,128]{3,2,1,0:T(8,128)(2,1)}), bf16[128,2,48,128]{3,2,1,0:T(8,128)(2,1)}, u32[]{:S(2)}, u32[]{:S(2)}) %all-to-all-start.1) | async-done | bytes 3145760 | tf_op jit(solution)/shard_map/all_to_all | solution.py:20
  184.6 4.1 %gather_fusion.2 = bf16[160,48,128]{2,1,0:T(8,128)(2,1)} fusion(bf16[256,48,128]{2,1,0:T(8,128)(2,1)} %bitcast.22, s32[1024]{0:T(1024)S(1)} %pad_clamp_fusion), kind=kCustom, calls=%fused_computation.2 | custom fusion | bytes 3932800 | tf_op jit(solution)/shard_map/jit(_take)/gather | solution.py:82
  (8 shorter events, 0.0 us)
Async XLA Ops:
  2.6 4.3 %copy-start = (bf16[160,48,128]{2,1,0:T(8,128)(2,1)S(1)}, bf16[160,48,128]{2,1,0:T(8,128)(2,1)}, u32[]{:S(2)}) copy-start(bf16[160,48,128]{2,1,0:T(8,128)(2,1)} %param.6) | copy-start | bytes 5898244
  9.5 4.3 %copy-start.1 = (bf16[256,48,128]{2,1,0:T(8,128)(2,1)S(1)}, bf16[256,48,128]{2,1,0:T(8,128)(2,1)}, u32[]{:S(2)}) copy-start(bf16[256,48,128]{2,1,0:T(8,128)(2,1)} %gather_fusion) | copy-start | bytes 9437188
  19.0 11.9 %copy-start.2 = (f32[2,512,512]{2,1,0:T(8,128)S(1)}, f32[2,512,512]{2,1,0:T(8,128)}, u32[]{:S(2)}) copy-start(f32[2,512,512]{2,1,0:T(8,128)} %param.9) | copy-start | bytes 6291460
  19.0 87.1 %all-to-all-start = ((bf16[128,2,2,48,128]{4,3,2,1,0:T(8,128)(2,1)}), bf16[128,2,2,48,128]{4,3,2,1,0:T(8,128)(2,1)}, u32[]{:S(2)}, u32[]{:S(2)}) async-start(bf16[128,2,2,48,128]{4,3,2,1,0:T(8,128)(2,1)} %pad_maximum_fusion), calls=%async_computation | async-start | bytes 12582912 | tf_op jit(solution)/shard_map/all_to_all | solution.py:20
  32.3 79.4 %copy-start.7 = (bf16[1,512,512]{2,1,0:T(8,128)(2,1)S(1)}, bf16[1,512,512]{2,1,0:T(8,128)(2,1)}, u32[]{:S(2)}) copy-start(bf16[1,512,512]{2,1,0:T(8,128)(2,1)} %get-tuple-element.10) | copy-start | bytes 1572868
  106.0 5.6 %copy-start.8 = (bf16[2,1536,512]{2,1,0:T(8,128)(2,1)S(1)}, bf16[2,1536,512]{2,1,0:T(8,128)(2,1)}, u32[]{:S(2)}) copy-start(bf16[2,1536,512]{2,1,0:T(8,128)(2,1)} %param.10) | copy-start | bytes 9437188
  111.6 2.8 %copy-start.3 = (bf16[128,1,1,48,128]{4,3,2,1,0:T(8,128)(2,1)}, bf16[128,1,1,48,128]{4,3,2,1,0:T(8,128)(2,1)S(1)}, u32[]{:S(2)}) copy-start(bf16[128,1,1,48,128]{4,3,2,1,0:T(8,128)(2,1)S(1)} %get-tuple-element.6) | copy-start | bytes 4718596
  114.4 5.8 %copy-start.6 = (bf16[1,512,512]{2,1,0:T(8,128)(2,1)S(1)}, bf16[1,512,512]{2,1,0:T(8,128)(2,1)}, u32[]{:S(2)}) copy-start(bf16[1,512,512]{2,1,0:T(8,128)(2,1)} %get-tuple-element.9) | copy-start | bytes 1572868
  134.4 50.1 %all-to-all-start.1 = ((bf16[128,2,48,128]{3,2,1,0:T(8,128)(2,1)}), bf16[128,2,48,128]{3,2,1,0:T(8,128)(2,1)}, u32[]{:S(2)}, u32[]{:S(2)}) async-start(bf16[128,2,48,128]{3,2,1,0:T(8,128)(2,1)} %pad_maximum_fusion.1), calls=%async_computation.1 | async-start | bytes 6291456 | tf_op jit(solution)/shard_map/all_to_all | solution.py:20
  159.7 2.4 %copy-start.5 = (f32[2,512,512]{2,1,0:T(8,128)S(1)}, f32[2,512,512]{2,1,0:T(8,128)}, u32[]{:S(2)}) copy-start(f32[2,512,512]{2,1,0:T(8,128)} %get-tuple-element.14) | copy-start | bytes 6291460
  164.8 6.3 %copy-start.4 = (f32[1536,512]{1,0:T(8,128)S(1)}, f32[1536,512]{1,0:T(8,128)}, u32[]{:S(2)}) copy-start(f32[1536,512]{1,0:T(8,128)} %fusion.1) | copy-start | bytes 9437188

commit v4 on v3

--- a/solution.py
+++ b/solution.py
@@ -40,14 +40,11 @@
     hit = targets[:, :, None] == slot_id[None, None, :]
     which = jnp.sum(jnp.where(hit, matrix_ids[None, None, :], 0), axis=2)
 
+    got_grads = exchange(jnp.take(gradients, which, axis=0, mode="clip"))
     new_moments = (0.9 * moments.astype(jnp.float32) + 0.1 * gradients.astype(jnp.float32)).astype(
         jnp.bfloat16
     )
-    outgoing = jnp.stack(
-        [jnp.take(gradients, which, axis=0, mode="clip"), jnp.take(new_moments, which, axis=0, mode="clip")],
-        axis=2,
-    )
-    incoming = exchange(outgoing)
+    got_moms = exchange(jnp.take(new_moments, which, axis=0, mode="clip"))
 
     def column_blocks(pieces):
         return pieces.reshape(tensors, owners * piece_rows, piece_cols)
@@ -55,9 +52,9 @@
     full_rows = owners * piece_rows
     full_cols = tensors * piece_cols
     basis_b = bases.astype(jnp.bfloat16)
-    steps, stat_list, second_list = [], [], []
+    stat_list, second_list = [], []
     for c in range(capacity):
-        grad_b = column_blocks(incoming[:, c, 0])
+        grad_b = column_blocks(got_grads[:, c])
         basis_rows = basis_b[c].reshape(tensors, piece_cols, full_cols)
         gram = jnp.einsum(
             "tik,sil->tksl", grad_b, grad_b, preferred_element_type=jnp.float32
@@ -66,13 +63,16 @@
         rotated = jnp.einsum(
             "tik,tkj->ij", grad_b, basis_rows, preferred_element_type=jnp.float32
         )
-        second_next = 0.95 * second[c].astype(jnp.float32) + 0.05 * rotated * rotated
-        second_list.append(second_next)
+        second_list.append(0.95 * second[c].astype(jnp.float32) + 0.05 * rotated * rotated)
+    got_moms, second_list = lax.optimization_barrier((got_moms, second_list))
+    steps = []
+    for c in range(capacity):
+        basis_rows = basis_b[c].reshape(tensors, piece_cols, full_cols)
         moment_rot = jnp.einsum(
-            "tik,tkj->ij", column_blocks(incoming[:, c, 1]), basis_rows,
+            "tik,tkj->ij", column_blocks(got_moms[:, c]), basis_rows,
             preferred_element_type=jnp.float32,
         )
-        scaled = (moment_rot / (jnp.sqrt(second_next) + 1e-06)).astype(jnp.bfloat16)
+        scaled = (moment_rot / (jnp.sqrt(second_list[c]) + 1e-06)).astype(jnp.bfloat16)
         step_b = jnp.einsum(
             "ij,tkj->tik", scaled, basis_rows, preferred_element_type=jnp.float32
         ).astype(jnp.bfloat16)

time: 189 us -> 173 us (0.915)
  waiting for transfers between devices: 82.8 us -> 66.4 us
  matrix products: 39.2 us -> 41.8 us
  other arithmetic: 21.3 us -> 19 us
    all_to_all x2 -> x3, waiting for transfers between devices: 82.8 us -> 66.4 us  [exchange(): lax.all_to_all(pieces, ('tensor', 'owner'), split_axis=0, concat_axis=0,...]
    another operation x1 -> x0, other arithmetic: 5.07 us -> none  [local(): jnp.stack([jnp.take(gradients, which, axis=0, mode='clip'), jnp.take(new_...]
    dot_general x2, matrix products: 9.01 us -> 12.8 us  [refine(): jnp.einsum('cik,ckj->cij', iter_b, square, preferred_element_type=jnp.flo...]
    convert_element_type x1, other arithmetic: 0.13 us -> 2.7 us  [local(): basis_b = bases.astype(jnp.bfloat16)]
    gather x1, local copies, waits for them, and re-layouts: 4.1 us -> 2.2 us  [local(): jnp.take(returned.reshape(devices * capacity, piece_rows, piece_cols), ow...]
    slice x1 -> x2, local copies, waits for them, and re-layouts: 5.59 us -> 5.06 us  [the longest x1 2.86 us: local(): grad_b = column_blocks(got_grads[:, c])]
    all_to_all x2 -> x3, starting transfers between devices: 20.7 us -> 21.2 us  [exchange(): lax.all_to_all(pieces, ('tensor', 'owner'), split_axis=0, concat_axis=0,...]
  transfers between devices with their start and end apart: 2 -> 3, of which waited for: 2 -> 3; matrix products, arithmetic and copies ran while one was open for 17% -> 34% of each run, Pallas kernels for 0% -> 0%
where the time goes in v4:
time: 173 us; the launch traced here: 172 us
  waiting for transfers between devices  66.4 us (38%)
  matrix products  41.8 us (24%)
  local copies, waits for them, and re-layouts  22.7 us (13%)
  starting transfers between devices  21.2 us (12%)
  other arithmetic  19 us (11%)
    all_to_all x3, waiting for transfers between devices, exchange(): lax.all_to_all(pieces, ('tensor', 'owner'), split_axis=0, concat_axis=0,...  66.4 us
    all_to_all x3, starting transfers between devices, exchange(): lax.all_to_all(pieces, ('tensor', 'owner'), split_axis=0, concat_axis=0,...  21.2 us
    dot_general x2, matrix products, refine(): jnp.einsum('cik,ckj->cij', iter_b, square, preferred_element_type=jnp.flo...  12.8 us
    dot_general x2, matrix products, local(): jnp.einsum('ij,tkj->tik', scaled, basis_rows, preferred_element_type=jnp....  11.2 us
    dot_general x2, matrix products, local(): jnp.einsum('tik,sil->tksl', grad_b, grad_b, preferred_element_type=jnp.fl...  7.49 us
    dot_general x2, matrix products, local(): jnp.einsum('tik,tkj->ij', grad_b, basis_rows, preferred_element_type=jnp....  5.6 us
    convert_element_type x1, other arithmetic, local(): new_second = jnp.where(filled, second_next, 0.0).astype(jnp.bfloat16)  5.43 us
    dot_general x2, local copies, waits for them, and re-layouts, local(): jnp.einsum('tik,sil->tksl', grad_b, grad_b, preferred_element_type=jnp.fl...  5.16 us
  transfers between devices with their start and end apart: 3, of which 3 were waited for; matrix products, arithmetic and copies ran while one was open for 34% of the time, Pallas kernels for 0%

profile of v4, /device:TPU:1, one launch (start us, length us, event | category | flops | bytes accessed | tf_op | source)
XLA Modules:
  0.0 172.0 jit_solution(3766507159672972763)
XLA Ops:
  0.7 0.9 convert_reduce_fusion
  1.5 0.7 multiply_add_fusion
  2.2 0.1 select_reduce_fusion
  2.3 0.1 copy.30
  2.4 0.1 reshape.95
  2.6 4.2 %gather_fusion.1 = bf16[256,48,128]{2,1,0:T(8,128)(2,1)} fusion(bf16[160,48,128]{2,1,0:T(8,128)(2,1)} %param.6, s32[1024]{0:T(1024)S(1)} %pad_clamp_fusion.1), kind=kCustom, calls=%fused_computation.1 | custom fusion | bytes 6292480 | tf_op jit(solution)/shard_map/jit(_take)/gather | solution.py:43
  6.8 11.9 %all-to-all-start.1 = ((bf16[128,2,48,128]{3,2,1,0:T(8,128)(2,1)}), bf16[128,2,48,128]{3,2,1,0:T(8,128)(2,1)}, u32[]{:S(2)}, u32[]{:S(2)}) async-start(bf16[128,2,48,128]{3,2,1,0:T(8,128)(2,1)} %bitcast.91), calls=%async_computation.1 | async-start | bytes 6291456 | tf_op jit(solution)/shard_map/all_to_all | solution.py:20
  18.7 0.0 copy-done
  18.7 3.6 %add_convert_fusion = bf16[160,48,128]{2,1,0:T(8,128)(2,1)} fusion(bf16[160,48,128]{2,1,0:T(8,128)(2,1)S(1)} %copy-done, bf16[160,48,128]{2,1,0:T(8,128)(2,1)} %param.7), kind=kLoop, calls=%fused_computation.7 | loop fusion | flops 5898240 | bytes 5898240 | tf_op jit(solution)/shard_map/convert_element_type | solution.py:44
  22.3 4.2 %gather_fusion = bf16[256,48,128]{2,1,0:T(8,128)(2,1)} fusion(bf16[160,48,128]{2,1,0:T(8,128)(2,1)} %add_convert_fusion, s32[1024]{0:T(1024)S(1)} %pad_clamp_fusion.1), kind=kCustom, calls=%fused_computation | custom fusion | bytes 6292480 | tf_op jit(solution)/shard_map/jit(_take)/gather | solution.py:47
  26.5 33.5 %all-to-all-done.1 = bf16[128,2,48,128]{3,2,1,0:T(8,128)(2,1)} async-done(((bf16[128,2,48,128]{3,2,1,0:T(8,128)(2,1)}), bf16[128,2,48,128]{3,2,1,0:T(8,128)(2,1)}, u32[]{:S(2)}, u32[]{:S(2)}) %all-to-all-start.1) | async-done | bytes 3145760 | tf_op jit(solution)/shard_map/all_to_all | solution.py:20
  60.0 4.7 %all-to-all-start = ((bf16[128,2,48,128]{3,2,1,0:T(8,128)(2,1)}), bf16[128,2,48,128]{3,2,1,0:T(8,128)(2,1)S(1)}, u32[]{:S(2)}, u32[]{:S(2)}) async-start(bf16[128,2,48,128]{3,2,1,0:T(8,128)(2,1)} %bitcast.90), calls=%async_computation | async-start | bytes 6291456 | tf_op jit(solution)/shard_map/all_to_all | solution.py:20
  64.6 2.7 %convert_element_type.61 = bf16[2,512,512]{2,1,0:T(8,128)(2,1)} convert(f32[2,512,512]{2,1,0:T(8,128)} %param.9) | non-fusion elementwise | flops 524288 | bytes 3145728 | tf_op jit(solution)/shard_map/convert_element_type | solution.py:54
  67.4 0.2 compare_reduce_fusion
  67.5 1.3 fusion.30
  68.8 0.0 copy-start.6
  68.8 0.0 copy-start.7
  68.8 0.0 copy-start.8
  68.8 2.9 %fusion.29 = (bf16[128,1,48,128]{3,2,1,0:T(8,128)(2,1)S(1)}, bf16[128,1,48,128]{3,2,1,0:T(8,128)(2,1)S(1)}) fusion(bf16[128,2,48,128]{3,2,1,0:T(8,128)(2,1)} %all-to-all-done.1), kind=kLoop, calls=%fused_computation.70 | loop fusion | bytes 6291456 | tf_op jit(solution)/shard_map/slice | solution.py:57
  71.7 0.0 copy-start.2
  71.7 0.0 copy-start.3
  71.7 0.0 copy-done.6
  71.7 0.3 copy-done.8
  72.1 2.8 %fusion.2 = f32[1536,512]{1,0:T(8,128)} fusion(bf16[4,1536,128]{2,1,0:T(8,128)(2,1)S(1)} %bitcast.93, bf16[4,128,512]{2,1,0:T(8,128)(2,1)S(1)} %bitcast.105, bf16[2,1536,512]{2,1,0:T(8,128)(2,1)S(1)} %copy-done.8), kind=kOutput, calls=%fused_computation.13 | convolution fusion | flops 809238528 | bytes 6815744 | tf_op jit(solution)/shard_map/tik,tkj->ij/dot_general | solution.py:63
  74.9 0.0 copy-done.2
  74.9 0.0 copy-done.7
  74.9 0.0 copy-done.3
  74.9 2.8 %fusion.1 = f32[1536,512]{1,0:T(8,128)} fusion(bf16[4,1536,128]{2,1,0:T(8,128)(2,1)S(1)} %bitcast.95, bf16[4,128,512]{2,1,0:T(8,128)(2,1)S(1)} %bitcast.107, bf16[2,1536,512]{2,1,0:T(8,128)(2,1)S(1)} %copy-done.8), kind=kOutput, calls=%fused_computation.11 | convolution fusion | flops 809238528 | bytes 6815744 | tf_op jit(solution)/shard_map/tik,tkj->ij/dot_general | solution.py:63
  77.7 28.6 %all-to-all-done = bf16[128,2,48,128]{3,2,1,0:T(8,128)(2,1)S(1)} async-done(((bf16[128,2,48,128]{3,2,1,0:T(8,128)(2,1)}), bf16[128,2,48,128]{3,2,1,0:T(8,128)(2,1)S(1)}, u32[]{:S(2)}, u32[]{:S(2)}) %all-to-all-start) | async-done | bytes 3145760 | tf_op jit(solution)/shard_map/all_to_all | solution.py:20
  106.3 2.2 %fusion.28 = (bf16[128,1,48,128]{3,2,1,0:T(8,128)(2,1)}, bf16[128,1,48,128]{3,2,1,0:T(8,128)(2,1)}) fusion(bf16[128,2,48,128]{3,2,1,0:T(8,128)(2,1)S(1)} %all-to-all-done), kind=kLoop, calls=%fused_computation.69 | loop fusion | bytes 6291456 | tf_op jit(solution)/shard_map/slice | solution.py:72
  108.5 6.1 %convolution_convert_fusion = bf16[1536,4,128]{2,0,1:T(8,128)(2,1)} fusion(bf16[4,128,512]{2,1,0:T(8,128)(2,1)} %bitcast.108, f32[1536,512]{1,0:T(8,128)} %fusion.1, bf16[4,1536,128]{2,1,0:T(8,128)(2,1)} %bitcast.103), kind=kOutput, calls=%fused_computation.17 | convolution fusion | flops 1613758464 | bytes 6815744 | tf_op jit(solution)/shard_map/ij,tkj->tik/dot_general | solution.py:76
  114.6 0.0 copy-done.5
  114.6 5.0 %convolution_convert_fusion.1 = bf16[1536,4,128]{2,0,1:T(8,128)(2,1)} fusion(bf16[4,128,512]{2,1,0:T(8,128)(2,1)} %bitcast.106, f32[1536,512]{1,0:T(8,128)S(1)} %copy-done.5, bf16[4,1536,128]{2,1,0:T(8,128)(2,1)} %bitcast.101), kind=kOutput, calls=%fused_computation.18 | convolution fusion | flops 1613758464 | bytes 6815744 | tf_op jit(solution)/shard_map/ij,tkj->tik/dot_general | solution.py:76
  119.6 3.8 %pad_maximum_fusion = bf16[128,2,48,128]{3,2,1,0:T(8,128)(2,1)} fusion(bf16[128,1,48,128]{3,2,1,0:T(8,128)(2,1)} %bitcast.102, bf16[128,1,48,128]{3,2,1,0:T(8,128)(2,1)} %bitcast.104), kind=kLoop, calls=%fused_computation.14 | loop fusion | flops 1572864 | bytes 6291456 | tf_op jit(solution)/shard_map/stack | solution.py:80
  123.5 4.7 %all-to-all-start.2 = ((bf16[128,2,48,128]{3,2,1,0:T(8,128)(2,1)}), bf16[128,2,48,128]{3,2,1,0:T(8,128)(2,1)S(1)}, u32[]{:S(2)}, u32[]{:S(2)}) async-start(bf16[128,2,48,128]{3,2,1,0:T(8,128)(2,1)} %pad_maximum_fusion), calls=%async_computation.2 | async-start | bytes 6291456 | tf_op jit(solution)/shard_map/all_to_all | solution.py:20
  128.2 2.6 %copy.34 = bf16[4,128,1536]{2,1,0:T(8,128)(2,1)} copy(bf16[4,128,1536]{1,2,0:T(8,128)(2,1)} %bitcast.96) | data formatting | bytes 3145728 | tf_op jit(solution)/shard_map/tik,sil->tksl/dot_general | solution.py:59
  130.7 4.2 %fusion.14 = f32[1,512,512]{2,1,0:T(8,128)} fusion(bf16[512,1536]{1,0:T(8,128)(2,1)} %bitcast.99, f32[2,512,512]{2,1,0:T(8,128)} %param.8), kind=kOutput, calls=%fused_computation.36 | convolution fusion | flops 806092800 | bytes 5242880 | tf_op jit(solution)/shard_map/tik,sil->tksl/dot_general | solution.py:59
  134.9 2.6 %copy.33 = bf16[4,128,1536]{2,1,0:T(8,128)(2,1)} copy(bf16[4,128,1536]{1,2,0:T(8,128)(2,1)} %bitcast.94) | data formatting | bytes 3145728 | tf_op jit(solution)/shard_map/tik,sil->tksl/dot_general | solution.py:59
  137.5 3.3 %fusion.12 = f32[1,512,512]{2,1,0:T(8,128)S(1)} fusion(bf16[512,1536]{1,0:T(8,128)(2,1)} %bitcast.100, f32[2,512,512]{2,1,0:T(8,128)} %param.8), kind=kOutput, calls=%fused_computation.34 | convolution fusion | flops 806092800 | bytes 5242880 | tf_op jit(solution)/shard_map/tik,sil->tksl/dot_general | solution.py:59
  140.8 0.0 copy-done.1
  140.8 0.0 copy-done.4
  140.8 4.8 %multiply_reduce_fusion = (f32[2]{0:T(128)S(1)}, f32[2,512,512]{2,1,0:T(8,128)}) fusion(f32[2,512,512]{2,1,0:T(8,128)S(1)} %copy-done.1, f32[1,512,512]{2,1,0:T(8,128)S(1)} %copy-done.4, f32[1,512,512]{2,1,0:T(8,128)S(1)} %fusion.12), kind=kOutput, calls=%fused_computation.24 | convolution fusion | flops 3222798336 | bytes 6291464 | tf_op jit(solution)/shard_map/cij,cjk->cik/dot_general | solution.py:89
  145.7 1.6 fusion.6
  147.3 6.4 %multiply_subtract_fusion = f32[2,512,512]{2,1,0:T(8,128)} fusion(f32[2,512,512]{2,1,0:T(8,128)} %get-tuple-element.20, f32[2]{0:T(128)S(1)} %sqrt_multiply_fusion), kind=kOutput, calls=%fused_computation.23 | convolution fusion | flops 1078460416 | bytes 4194312 | tf_op jit(solution)/shard_map/cik,ckj->cij/dot_general | solution.py:13
  153.7 6.3 %subtract_select_fusion = f32[2,512,512]{2,1,0:T(8,128)} fusion(f32[2,512,512]{2,1,0:T(8,128)} %multiply_subtract_fusion, pred[2]{0:T(512)(128)(4,1)S(1)} %compare_reduce_fusion), kind=kOutput, calls=%fused_computation.22 | convolution fusion | flops 1077411840 | bytes 4194306 | tf_op jit(solution)/shard_map/cik,ckj->cij/dot_general | solution.py:13
  160.1 5.4 %fusion = bf16[2,1536,512]{2,1,0:T(8,128)(2,1)} fusion(f32[1,1536,512]{2,1,0:T(8,128)} %bitcast.98, f32[1,1536,512]{2,1,0:T(8,128)} %bitcast.97, pred[2]{0:T(512)(128)(4,1)S(1)} %compare_reduce_fusion), kind=kLoop, calls=%fused_computation.4 | loop fusion | flops 7864320 | bytes 9437186 | tf_op jit(solution)/shard_map/convert_element_type | solution.py:105
  165.5 4.3 %all-to-all-done.2 = bf16[128,2,48,128]{3,2,1,0:T(8,128)(2,1)S(1)} async-done(((bf16[128,2,48,128]{3,2,1,0:T(8,128)(2,1)}), bf16[128,2,48,128]{3,2,1,0:T(8,128)(2,1)S(1)}, u32[]{:S(2)}, u32[]{:S(2)}) %all-to-all-start.2) | async-done | bytes 3145760 | tf_op jit(solution)/shard_map/all_to_all | solution.py:20
  169.8 2.2 %gather_fusion.2 = bf16[160,48,128]{2,1,0:T(8,128)(2,1)} fusion(bf16[256,48,128]{2,1,0:T(8,128)(2,1)S(1)} %bitcast.92, s32[1024]{0:T(1024)S(1)} %pad_clamp_fusion), kind=kCustom, calls=%fused_computation.2 | custom fusion | bytes 3932800 | tf_op jit(solution)/shard_map/jit(_take)/gather | solution.py:82
  (10 shorter events, 0.0 us)
Async XLA Ops:
  6.8 11.9 %copy-start = (bf16[160,48,128]{2,1,0:T(8,128)(2,1)S(1)}, bf16[160,48,128]{2,1,0:T(8,128)(2,1)}, u32[]{:S(2)}) copy-start(bf16[160,48,128]{2,1,0:T(8,128)(2,1)} %param.6) | copy-start | bytes 5898244
  6.8 53.2 %all-to-all-start.1 = ((bf16[128,2,48,128]{3,2,1,0:T(8,128)(2,1)}), bf16[128,2,48,128]{3,2,1,0:T(8,128)(2,1)}, u32[]{:S(2)}, u32[]{:S(2)}) async-start(bf16[128,2,48,128]{3,2,1,0:T(8,128)(2,1)} %bitcast.91), calls=%async_computation.1 | async-start | bytes 6291456 | tf_op jit(solution)/shard_map/all_to_all | solution.py:20
  60.0 46.3 %all-to-all-start = ((bf16[128,2,48,128]{3,2,1,0:T(8,128)(2,1)}), bf16[128,2,48,128]{3,2,1,0:T(8,128)(2,1)S(1)}, u32[]{:S(2)}, u32[]{:S(2)}) async-start(bf16[128,2,48,128]{3,2,1,0:T(8,128)(2,1)} %bitcast.90), calls=%async_computation | async-start | bytes 6291456 | tf_op jit(solution)/shard_map/all_to_all | solution.py:20
  68.8 2.9 %copy-start.6 = (bf16[1,512,512]{2,1,0:T(8,128)(2,1)}, bf16[1,512,512]{2,1,0:T(8,128)(2,1)S(1)}, u32[]{:S(2)}) copy-start(bf16[1,512,512]{2,1,0:T(8,128)(2,1)S(1)} %get-tuple-element.15) | copy-start | bytes 1572868
  68.8 6.1 %copy-start.7 = (bf16[1,512,512]{2,1,0:T(8,128)(2,1)}, bf16[1,512,512]{2,1,0:T(8,128)(2,1)S(1)}, u32[]{:S(2)}) copy-start(bf16[1,512,512]{2,1,0:T(8,128)(2,1)S(1)} %get-tuple-element.16) | copy-start | bytes 1572868
  68.8 3.2 %copy-start.8 = (bf16[2,1536,512]{2,1,0:T(8,128)(2,1)S(1)}, bf16[2,1536,512]{2,1,0:T(8,128)(2,1)}, u32[]{:S(2)}) copy-start(bf16[2,1536,512]{2,1,0:T(8,128)(2,1)} %param.10) | copy-start | bytes 9437188
  71.7 3.2 %copy-start.2 = (bf16[128,1,48,128]{3,2,1,0:T(8,128)(2,1)}, bf16[128,1,48,128]{3,2,1,0:T(8,128)(2,1)S(1)}, u32[]{:S(2)}) copy-start(bf16[128,1,48,128]{3,2,1,0:T(8,128)(2,1)S(1)} %get-tuple-element.14) | copy-start | bytes 4718596
  71.7 3.2 %copy-start.3 = (bf16[128,1,48,128]{3,2,1,0:T(8,128)(2,1)}, bf16[128,1,48,128]{3,2,1,0:T(8,128)(2,1)S(1)}, u32[]{:S(2)}) copy-start(bf16[128,1,48,128]{3,2,1,0:T(8,128)(2,1)S(1)} %get-tuple-element.13) | copy-start | bytes 4718596
  108.5 6.1 %copy-start.5 = (f32[1536,512]{1,0:T(8,128)S(1)}, f32[1536,512]{1,0:T(8,128)}, u32[]{:S(2)}) copy-start(f32[1536,512]{1,0:T(8,128)} %fusion.2) | copy-start | bytes 9437188
  123.5 46.3 %all-to-all-start.2 = ((bf16[128,2,48,128]{3,2,1,0:T(8,128)(2,1)}), bf16[128,2,48,128]{3,2,1,0:T(8,128)(2,1)S(1)}, u32[]{:S(2)}, u32[]{:S(2)}) async-start(bf16[128,2,48,128]{3,2,1,0:T(8,128)(2,1)} %pad_maximum_fusion), calls=%async_computation.2 | async-start | bytes 6291456 | tf_op jit(solution)/shard_map/all_to_all | solution.py:20
  137.5 3.3 %copy-start.1 = (f32[2,512,512]{2,1,0:T(8,128)S(1)}, f32[2,512,512]{2,1,0:T(8,128)}, u32[]{:S(2)}) copy-start(f32[2,512,512]{2,1,0:T(8,128)} %param.9) | copy-start | bytes 6291460
  137.5 3.4 %copy-start.4 = (f32[1,512,512]{2,1,0:T(8,128)S(1)}, f32[1,512,512]{2,1,0:T(8,128)}, u32[]{:S(2)}) copy-start(f32[1,512,512]{2,1,0:T(8,128)} %fusion.14) | copy-start | bytes 3145732

commit v5 on v4

--- a/solution.py
+++ b/solution.py
@@ -73,6 +73,7 @@
             preferred_element_type=jnp.float32,
         )
         scaled = (moment_rot / (jnp.sqrt(second_list[c]) + 1e-06)).astype(jnp.bfloat16)
+        scaled = lax.optimization_barrier(scaled)
         step_b = jnp.einsum(
             "ij,tkj->tik", scaled, basis_rows, preferred_element_type=jnp.float32
         ).astype(jnp.bfloat16)

time: 173 us -> 166 us (0.960)
  matrix products: 41.8 us -> 36 us
  other arithmetic: 19 us -> 17.2 us
    dot_general x2, matrix products: 11.2 us -> 2.03 us  [local(): jnp.einsum('ij,tkj->tik', scaled, basis_rows, preferred_element_type=jnp....]
    dot_general x0 -> x2, matrix products: none -> 3.25 us  [local(): jnp.einsum('tik,tkj->ij', column_blocks(got_moms[:, c]), basis_rows, pref...]
    unnamed x18 -> x24, local copies, waits for them, and re-layouts: 0.36 us -> 2.76 us
    another operation x1, other arithmetic: 3.84 us -> 1.95 us  [local(): returned = exchange(jnp.stack(steps, axis=1))]
  transfers between devices with their start and end apart: 3 -> 3, of which waited for: 3 -> 3; matrix products, arithmetic and copies ran while one was open for 34% -> 35% of each run, Pallas kernels for 0% -> 0%
where the time goes in v5:
time: 166 us; the launch traced here: 165 us
  waiting for transfers between devices  66.5 us (40%)
  matrix products  36 us (22%)
  local copies, waits for them, and re-layouts  23.4 us (14%)
  starting transfers between devices  21.2 us (13%)
  other arithmetic  17.2 us (10%)
    all_to_all x3, waiting for transfers between devices, exchange(): lax.all_to_all(pieces, ('tensor', 'owner'), split_axis=0, concat_axis=0,...  66.5 us
    all_to_all x3, starting transfers between devices, exchange(): lax.all_to_all(pieces, ('tensor', 'owner'), split_axis=0, concat_axis=0,...  21.2 us
    dot_general x2, matrix products, refine(): jnp.einsum('cik,ckj->cij', iter_b, square, preferred_element_type=jnp.flo...  12.8 us
    dot_general x2, matrix products, local(): jnp.einsum('tik,sil->tksl', grad_b, grad_b, preferred_element_type=jnp.fl...  7.51 us
    dot_general x2, matrix products, local(): jnp.einsum('tik,tkj->ij', grad_b, basis_rows, preferred_element_type=jnp....  5.6 us
    convert_element_type x1, other arithmetic, local(): new_second = jnp.where(filled, second_next, 0.0).astype(jnp.bfloat16)  5.43 us
    dot_general x2, local copies, waits for them, and re-layouts, local(): jnp.einsum('tik,sil->tksl', grad_b, grad_b, preferred_element_type=jnp.fl...  5.16 us
    dot_general x1, matrix products, local(): jnp.einsum('cij,cjk->cik', stat_next, bases, precision=lax.Precision.HIGH...  4.84 us
  transfers between devices with their start and end apart: 3, of which 3 were waited for; matrix products, arithmetic and copies ran while one was open for 35% of the time, Pallas kernels for 0%

profile of v5, /device:TPU:1, one launch (start us, length us, event | category | flops | bytes accessed | tf_op | source)
XLA Modules:
  0.0 165.1 jit_solution(7831261869902956461)
XLA Ops:
  0.7 0.9 convert_reduce_fusion
  1.5 0.7 multiply_add_fusion
  2.2 0.1 select_reduce_fusion
  2.3 0.1 copy.30
  2.4 0.1 reshape.95
  2.6 4.2 %gather_fusion.1 = bf16[256,48,128]{2,1,0:T(8,128)(2,1)} fusion(bf16[160,48,128]{2,1,0:T(8,128)(2,1)} %param.6, s32[1024]{0:T(1024)S(1)} %pad_clamp_fusion.1), kind=kCustom, calls=%fused_computation.1 | custom fusion | bytes 6292480 | tf_op jit(solution)/shard_map/jit(_take)/gather | solution.py:43
  6.8 11.9 %all-to-all-start.1 = ((bf16[128,2,48,128]{3,2,1,0:T(8,128)(2,1)}), bf16[128,2,48,128]{3,2,1,0:T(8,128)(2,1)}, u32[]{:S(2)}, u32[]{:S(2)}) async-start(bf16[128,2,48,128]{3,2,1,0:T(8,128)(2,1)} %bitcast.81), calls=%async_computation.1 | async-start | bytes 6291456 | tf_op jit(solution)/shard_map/all_to_all | solution.py:20
  18.7 3.6 %add_convert_fusion = bf16[160,48,128]{2,1,0:T(8,128)(2,1)} fusion(bf16[160,48,128]{2,1,0:T(8,128)(2,1)S(1)} %copy-done, bf16[160,48,128]{2,1,0:T(8,128)(2,1)} %param.7), kind=kLoop, calls=%fused_computation.7 | loop fusion | flops 5898240 | bytes 5898240 | tf_op jit(solution)/shard_map/convert_element_type | solution.py:44
  22.3 4.2 %gather_fusion = bf16[256,48,128]{2,1,0:T(8,128)(2,1)} fusion(bf16[160,48,128]{2,1,0:T(8,128)(2,1)} %add_convert_fusion, s32[1024]{0:T(1024)S(1)} %pad_clamp_fusion.1), kind=kCustom, calls=%fused_computation | custom fusion | bytes 6292480 | tf_op jit(solution)/shard_map/jit(_take)/gather | solution.py:47
  26.4 33.5 %all-to-all-done.1 = bf16[128,2,48,128]{3,2,1,0:T(8,128)(2,1)} async-done(((bf16[128,2,48,128]{3,2,1,0:T(8,128)(2,1)}), bf16[128,2,48,128]{3,2,1,0:T(8,128)(2,1)}, u32[]{:S(2)}, u32[]{:S(2)}) %all-to-all-start.1) | async-done | bytes 3145760 | tf_op jit(solution)/shard_map/all_to_all | solution.py:20
  60.0 4.7 %all-to-all-start = ((bf16[128,2,48,128]{3,2,1,0:T(8,128)(2,1)}), bf16[128,2,48,128]{3,2,1,0:T(8,128)(2,1)S(1)}, u32[]{:S(2)}, u32[]{:S(2)}) async-start(bf16[128,2,48,128]{3,2,1,0:T(8,128)(2,1)} %bitcast.80), calls=%async_computation | async-start | bytes 6291456 | tf_op jit(solution)/shard_map/all_to_all | solution.py:20
  64.6 2.7 %convert_element_type.61 = bf16[2,512,512]{2,1,0:T(8,128)(2,1)} convert(f32[2,512,512]{2,1,0:T(8,128)} %param.9) | non-fusion elementwise | flops 524288 | bytes 3145728 | tf_op jit(solution)/shard_map/convert_element_type | solution.py:54
  67.4 0.2 compare_reduce_fusion
  67.5 1.3 fusion.28
  68.8 0.0 copy-start.7
  68.8 0.0 copy-start.9
  68.8 0.0 copy-start.11
  68.8 2.9 %fusion.27 = (bf16[128,1,48,128]{3,2,1,0:T(8,128)(2,1)S(1)}, bf16[128,1,48,128]{3,2,1,0:T(8,128)(2,1)S(1)}) fusion(bf16[128,2,48,128]{3,2,1,0:T(8,128)(2,1)} %all-to-all-done.1), kind=kLoop, calls=%fused_computation.68 | loop fusion | bytes 6291456 | tf_op jit(solution)/shard_map/slice | solution.py:57
  71.7 0.0 copy-start.2
  71.7 0.0 copy-start.3
  71.7 0.3 copy-done.11
  72.1 2.8 %fusion.2 = f32[1536,512]{1,0:T(8,128)} fusion(bf16[4,1536,128]{2,1,0:T(8,128)(2,1)S(1)} %bitcast.83, bf16[4,128,512]{2,1,0:T(8,128)(2,1)S(1)} %bitcast.95, bf16[2,1536,512]{2,1,0:T(8,128)(2,1)S(1)} %copy-done.11), kind=kOutput, calls=%fused_computation.13 | convolution fusion | flops 809238528 | bytes 6815744 | tf_op jit(solution)/shard_map/tik,tkj->ij/dot_general | solution.py:63
  74.9 2.8 %fusion.1 = f32[1536,512]{1,0:T(8,128)} fusion(bf16[4,1536,128]{2,1,0:T(8,128)(2,1)S(1)} %bitcast.85, bf16[4,128,512]{2,1,0:T(8,128)(2,1)S(1)} %bitcast.98, bf16[2,1536,512]{2,1,0:T(8,128)(2,1)S(1)} %copy-done.11), kind=kOutput, calls=%fused_computation.11 | convolution fusion | flops 809238528 | bytes 6815744 | tf_op jit(solution)/shard_map/tik,tkj->ij/dot_general | solution.py:63
  77.7 28.6 %all-to-all-done = bf16[128,2,48,128]{3,2,1,0:T(8,128)(2,1)S(1)} async-done(((bf16[128,2,48,128]{3,2,1,0:T(8,128)(2,1)}), bf16[128,2,48,128]{3,2,1,0:T(8,128)(2,1)S(1)}, u32[]{:S(2)}, u32[]{:S(2)}) %all-to-all-start) | async-done | bytes 3145760 | tf_op jit(solution)/shard_map/all_to_all | solution.py:20
  106.3 0.5 fusion.26
  106.8 1.3 copy-done.6
  108.2 0.1 copy-done.10
  108.3 1.6 divide_convert_fusion
  109.9 0.0 copy-start.8
  109.9 1.0 convolution_convert_fusion
  110.9 0.8 copy-done.5
  111.8 0.1 copy-done.8
  111.9 1.6 divide_convert_fusion.1
  113.5 1.0 convolution_convert_fusion.1
  114.5 1.9 %pad_maximum_fusion = bf16[128,2,48,128]{3,2,1,0:T(8,128)(2,1)} fusion(bf16[128,1,48,128]{3,2,1,0:T(8,128)(2,1)S(1)} %bitcast.91, bf16[128,1,48,128]{3,2,1,0:T(8,128)(2,1)S(1)} %bitcast.94), kind=kLoop, calls=%fused_computation.14 | loop fusion | flops 1572864 | bytes 6291456 | tf_op jit(solution)/shard_map/stack | solution.py:81
  116.5 4.7 %all-to-all-start.2 = ((bf16[128,2,48,128]{3,2,1,0:T(8,128)(2,1)}), bf16[128,2,48,128]{3,2,1,0:T(8,128)(2,1)S(1)}, u32[]{:S(2)}, u32[]{:S(2)}) async-start(bf16[128,2,48,128]{3,2,1,0:T(8,128)(2,1)} %pad_maximum_fusion), calls=%async_computation.2 | async-start | bytes 6291456 | tf_op jit(solution)/shard_map/all_to_all | solution.py:20
  121.2 2.6 %copy.34 = bf16[4,128,1536]{2,1,0:T(8,128)(2,1)} copy(bf16[4,128,1536]{1,2,0:T(8,128)(2,1)} %bitcast.86) | data formatting | bytes 3145728 | tf_op jit(solution)/shard_map/tik,sil->tksl/dot_general | solution.py:59
  123.8 4.2 %fusion.14 = f32[1,512,512]{2,1,0:T(8,128)} fusion(bf16[512,1536]{1,0:T(8,128)(2,1)} %bitcast.89, f32[2,512,512]{2,1,0:T(8,128)} %param.8), kind=kOutput, calls=%fused_computation.36 | convolution fusion | flops 806092800 | bytes 5242880 | tf_op jit(solution)/shard_map/tik,sil->tksl/dot_general | solution.py:59
  127.9 2.6 %copy.33 = bf16[4,128,1536]{2,1,0:T(8,128)(2,1)} copy(bf16[4,128,1536]{1,2,0:T(8,128)(2,1)} %bitcast.84) | data formatting | bytes 3145728 | tf_op jit(solution)/shard_map/tik,sil->tksl/dot_general | solution.py:59
  130.5 3.3 %fusion.12 = f32[1,512,512]{2,1,0:T(8,128)S(1)} fusion(bf16[512,1536]{1,0:T(8,128)(2,1)} %bitcast.90, f32[2,512,512]{2,1,0:T(8,128)} %param.8), kind=kOutput, calls=%fused_computation.34 | convolution fusion | flops 806092800 | bytes 5242880 | tf_op jit(solution)/shard_map/tik,sil->tksl/dot_general | solution.py:59
  133.9 0.0 copy-done.1
  133.9 4.8 %multiply_reduce_fusion = (f32[2]{0:T(128)S(1)}, f32[2,512,512]{2,1,0:T(8,128)}) fusion(f32[2,512,512]{2,1,0:T(8,128)S(1)} %copy-done.1, f32[1,512,512]{2,1,0:T(8,128)S(1)} %copy-done.4, f32[1,512,512]{2,1,0:T(8,128)S(1)} %fusion.12), kind=kOutput, calls=%fused_computation.22 | convolution fusion | flops 3222798336 | bytes 6291464 | tf_op jit(solution)/shard_map/cij,cjk->cik/dot_general | solution.py:90
  138.7 1.6 fusion.4
  140.3 6.5 %multiply_subtract_fusion = f32[2,512,512]{2,1,0:T(8,128)} fusion(f32[2,512,512]{2,1,0:T(8,128)} %get-tuple-element.20, f32[2]{0:T(128)S(1)} %sqrt_multiply_fusion), kind=kOutput, calls=%fused_computation.21 | convolution fusion | flops 1078460416 | bytes 4194312 | tf_op jit(solution)/shard_map/cik,ckj->cij/dot_general | solution.py:13
  146.8 6.3 %subtract_select_fusion = f32[2,512,512]{2,1,0:T(8,128)} fusion(f32[2,512,512]{2,1,0:T(8,128)} %multiply_subtract_fusion, pred[2]{0:T(512)(128)(4,1)S(1)} %compare_reduce_fusion), kind=kOutput, calls=%fused_computation.20 | convolution fusion | flops 1077411840 | bytes 4194306 | tf_op jit(solution)/shard_map/cik,ckj->cij/dot_general | solution.py:13
  153.2 5.4 %fusion = bf16[2,1536,512]{2,1,0:T(8,128)(2,1)} fusion(f32[1,1536,512]{2,1,0:T(8,128)} %bitcast.88, f32[1,1536,512]{2,1,0:T(8,128)} %bitcast.87, pred[2]{0:T(512)(128)(4,1)S(1)} %compare_reduce_fusion), kind=kLoop, calls=%fused_computation.4 | loop fusion | flops 7864320 | bytes 9437186 | tf_op jit(solution)/shard_map/convert_element_type | solution.py:106
  158.6 4.3 %all-to-all-done.2 = bf16[128,2,48,128]{3,2,1,0:T(8,128)(2,1)S(1)} async-done(((bf16[128,2,48,128]{3,2,1,0:T(8,128)(2,1)}), bf16[128,2,48,128]{3,2,1,0:T(8,128)(2,1)S(1)}, u32[]{:S(2)}, u32[]{:S(2)}) %all-to-all-start.2) | async-done | bytes 3145760 | tf_op jit(solution)/shard_map/all_to_all | solution.py:20
  162.9 2.2 %gather_fusion.2 = bf16[160,48,128]{2,1,0:T(8,128)(2,1)} fusion(bf16[256,48,128]{2,1,0:T(8,128)(2,1)S(1)} %bitcast.82, s32[1024]{0:T(1024)S(1)} %pad_clamp_fusion), kind=kCustom, calls=%fused_computation.2 | custom fusion | bytes 3932800 | tf_op jit(solution)/shard_map/jit(_take)/gather | solution.py:83
  (18 shorter events, 0.1 us)
Async XLA Ops:
  6.8 11.9 %copy-start = (bf16[160,48,128]{2,1,0:T(8,128)(2,1)S(1)}, bf16[160,48,128]{2,1,0:T(8,128)(2,1)}, u32[]{:S(2)}) copy-start(bf16[160,48,128]{2,1,0:T(8,128)(2,1)} %param.6) | copy-start | bytes 5898244
  6.8 53.2 %all-to-all-start.1 = ((bf16[128,2,48,128]{3,2,1,0:T(8,128)(2,1)}), bf16[128,2,48,128]{3,2,1,0:T(8,128)(2,1)}, u32[]{:S(2)}, u32[]{:S(2)}) async-start(bf16[128,2,48,128]{3,2,1,0:T(8,128)(2,1)} %bitcast.81), calls=%async_computation.1 | async-start | bytes 6291456 | tf_op jit(solution)/shard_map/all_to_all | solution.py:20
  60.0 46.3 %all-to-all-start = ((bf16[128,2,48,128]{3,2,1,0:T(8,128)(2,1)}), bf16[128,2,48,128]{3,2,1,0:T(8,128)(2,1)S(1)}, u32[]{:S(2)}, u32[]{:S(2)}) async-start(bf16[128,2,48,128]{3,2,1,0:T(8,128)(2,1)} %bitcast.80), calls=%async_computation | async-start | bytes 6291456 | tf_op jit(solution)/shard_map/all_to_all | solution.py:20
  68.8 2.9 %copy-start.7 = (bf16[1,512,512]{2,1,0:T(8,128)(2,1)}, bf16[1,512,512]{2,1,0:T(8,128)(2,1)S(1)}, u32[]{:S(2)}) copy-start(bf16[1,512,512]{2,1,0:T(8,128)(2,1)S(1)} %get-tuple-element.15) | copy-start | bytes 1572868
  68.8 6.1 %copy-start.9 = (bf16[1,512,512]{2,1,0:T(8,128)(2,1)}, bf16[1,512,512]{2,1,0:T(8,128)(2,1)S(1)}, u32[]{:S(2)}) copy-start(bf16[1,512,512]{2,1,0:T(8,128)(2,1)S(1)} %get-tuple-element.16) | copy-start | bytes 1572868
  68.8 3.2 %copy-start.11 = (bf16[2,1536,512]{2,1,0:T(8,128)(2,1)S(1)}, bf16[2,1536,512]{2,1,0:T(8,128)(2,1)}, u32[]{:S(2)}) copy-start(bf16[2,1536,512]{2,1,0:T(8,128)(2,1)} %param.10) | copy-start | bytes 9437188
  71.7 3.2 %copy-start.2 = (bf16[128,1,48,128]{3,2,1,0:T(8,128)(2,1)}, bf16[128,1,48,128]{3,2,1,0:T(8,128)(2,1)S(1)}, u32[]{:S(2)}) copy-start(bf16[128,1,48,128]{3,2,1,0:T(8,128)(2,1)S(1)} %get-tuple-element.14) | copy-start | bytes 4718596
  71.7 3.2 %copy-start.3 = (bf16[128,1,48,128]{3,2,1,0:T(8,128)(2,1)}, bf16[128,1,48,128]{3,2,1,0:T(8,128)(2,1)S(1)}, u32[]{:S(2)}) copy-start(bf16[128,1,48,128]{3,2,1,0:T(8,128)(2,1)S(1)} %get-tuple-element.13) | copy-start | bytes 4718596
  106.3 1.9 %copy-start.6 = (f32[1536,512]{1,0:T(8,128)S(1)}, f32[1536,512]{1,0:T(8,128)}, u32[]{:S(2)}) copy-start(f32[1536,512]{1,0:T(8,128)} %fusion.1) | copy-start | bytes 9437188
  106.3 2.0 %copy-start.10 = (bf16[1,512,512]{2,1,0:T(8,128)(2,1)S(1)}, bf16[1,512,512]{2,1,0:T(8,128)(2,1)}, u32[]{:S(2)}) copy-start(bf16[1,512,512]{2,1,0:T(8,128)(2,1)} %copy-done.9) | copy-start | bytes 1572868
  109.9 1.9 %copy-start.5 = (f32[1536,512]{1,0:T(8,128)S(1)}, f32[1536,512]{1,0:T(8,128)}, u32[]{:S(2)}) copy-start(f32[1536,512]{1,0:T(8,128)} %fusion.2) | copy-start | bytes 9437188
  109.9 2.0 %copy-start.8 = (bf16[1,512,512]{2,1,0:T(8,128)(2,1)S(1)}, bf16[1,512,512]{2,1,0:T(8,128)(2,1)}, u32[]{:S(2)}) copy-start(bf16[1,512,512]{2,1,0:T(8,128)(2,1)} %copy-done.7) | copy-start | bytes 1572868
  116.5 46.5 %all-to-all-start.2 = ((bf16[128,2,48,128]{3,2,1,0:T(8,128)(2,1)}), bf16[128,2,48,128]{3,2,1,0:T(8,128)(2,1)S(1)}, u32[]{:S(2)}, u32[]{:S(2)}) async-start(bf16[128,2,48,128]{3,2,1,0:T(8,128)(2,1)} %pad_maximum_fusion), calls=%async_computation.2 | async-start | bytes 6291456 | tf_op jit(solution)/shard_map/all_to_all | solution.py:20
  130.5 3.3 %copy-start.1 = (f32[2,512,512]{2,1,0:T(8,128)S(1)}, f32[2,512,512]{2,1,0:T(8,128)}, u32[]{:S(2)}) copy-start(f32[2,512,512]{2,1,0:T(8,128)} %param.9) | copy-start | bytes 6291460
  130.5 3.4 %copy-start.4 = (f32[1,512,512]{2,1,0:T(8,128)S(1)}, f32[1,512,512]{2,1,0:T(8,128)}, u32[]{:S(2)}) copy-start(f32[1,512,512]{2,1,0:T(8,128)} %fusion.14) | copy-start | bytes 3145732

commit v6 on v5

--- a/solution.py
+++ b/solution.py
@@ -64,7 +64,21 @@
             "tik,tkj->ij", grad_b, basis_rows, preferred_element_type=jnp.float32
         )
         second_list.append(0.95 * second[c].astype(jnp.float32) + 0.05 * rotated * rotated)
-    got_moms, second_list = lax.optimization_barrier((got_moms, second_list))
+    stat_next = jnp.stack(stat_list)
+    power = jnp.einsum(
+        "cij,cjk->cik",
+        stat_next,
+        bases,
+        precision=lax.Precision.HIGHEST,
+        preferred_element_type=jnp.float32,
+    )
+    iterate = power / (
+        2.0 * jnp.sqrt(full_cols * jnp.mean(power * power, axis=(1, 2), keepdims=True) + 1e-06)
+    )
+    iterate = refine(iterate)
+    got_moms, second_list, stat_next, iterate = lax.optimization_barrier(
+        (got_moms, second_list, stat_next, iterate)
+    )
     steps = []
     for c in range(capacity):
         basis_rows = basis_b[c].reshape(tensors, piece_cols, full_cols)
@@ -85,19 +99,7 @@
         owner_place * capacity + position, axis=0, mode="clip",
     )
 
-    stat_next = jnp.stack(stat_list)
     second_next = jnp.stack(second_list)
-    power = jnp.einsum(
-        "cij,cjk->cik",
-        stat_next,
-        bases,
-        precision=lax.Precision.HIGHEST,
-        preferred_element_type=jnp.float32,
-    )
-    iterate = power / (
-        2.0 * jnp.sqrt(full_cols * jnp.mean(power * power, axis=(1, 2), keepdims=True) + 1e-06)
-    )
-    iterate = refine(iterate)
 
     my_slots = myself * capacity + jnp.arange(capacity, dtype=jnp.int32)
     filled = jnp.any(my_slots[:, None] == slot_id[None, :], axis=1)[:, None, None]

time: 166 us -> 173 us (1.042)
  starting transfers between devices: 21.2 us -> 26.5 us
  local copies, waits for them, and re-layouts: 23.4 us -> 26.8 us
  other arithmetic: 17.2 us -> 15 us
    all_to_all x3, starting transfers between devices: 21.2 us -> 26.5 us  [exchange(): lax.all_to_all(pieces, ('tensor', 'owner'), split_axis=0, concat_axis=0,...]
    dot_general x2, matrix products: 7.51 us -> 4.34 us  [local(): jnp.einsum('tik,sil->tksl', grad_b, grad_b, preferred_element_type=jnp.fl...]
    select_n x1, other arithmetic: 1.62 us -> 4.54 us  [local(): new_bases = jnp.where(filled, iterate, 0.0)]
    convert_element_type x1, other arithmetic: 5.43 us -> 2.67 us  [local(): new_second = jnp.where(filled, second_next, 0.0).astype(jnp.bfloat16)]
    convert_element_type x1, other arithmetic: 2.7 us -> 0.13 us  [local(): basis_b = bases.astype(jnp.bfloat16)]
    dot_general x2, matrix products: 5.6 us -> 7.74 us  [local(): jnp.einsum('tik,tkj->ij', grad_b, basis_rows, preferred_element_type=jnp....]
    unnamed x24 -> x32, local copies, waits for them, and re-layouts: 2.76 us -> 4.69 us
    gather x1, local copies, waits for them, and re-layouts: 2.2 us -> 4.1 us  [local(): jnp.take(returned.reshape(devices * capacity, piece_rows, piece_cols), ow...]
  transfers between devices with their start and end apart: 3 -> 3, of which waited for: 3 -> 3; matrix products, arithmetic and copies ran while one was open for 35% -> 31% of each run, Pallas kernels for 0% -> 0%
where the time goes in v6:
time: 173 us; the launch traced here: 172 us
  waiting for transfers between devices  67.8 us (39%)
  matrix products  35.2 us (20%)
  local copies, waits for them, and re-layouts  26.8 us (15%)
  starting transfers between devices  26.5 us (15%)
  other arithmetic  15 us (9%)
    all_to_all x3, waiting for transfers between devices, exchange(): lax.all_to_all(pieces, ('tensor', 'owner'), split_axis=0, concat_axis=0,...  67.8 us
    all_to_all x3, starting transfers between devices, exchange(): lax.all_to_all(pieces, ('tensor', 'owner'), split_axis=0, concat_axis=0,...  26.5 us
    dot_general x2, matrix products, refine(): jnp.einsum('cik,ckj->cij', iter_b, square, preferred_element_type=jnp.flo...  12.8 us
    dot_general x2, matrix products, local(): jnp.einsum('tik,tkj->ij', grad_b, basis_rows, preferred_element_type=jnp....  7.74 us
    dot_general x2, local copies, waits for them, and re-layouts, local(): jnp.einsum('tik,sil->tksl', grad_b, grad_b, preferred_element_type=jnp.fl...  5.15 us
    dot_general x1, matrix products, local(): jnp.einsum('cij,cjk->cik', stat_next, bases, precision=lax.Precision.HIGH...  4.83 us
    unnamed x32, local copies, waits for them, and re-layouts  4.69 us
    select_n x1, other arithmetic, local(): new_bases = jnp.where(filled, iterate, 0.0)  4.54 us
  transfers between devices with their start and end apart: 3, of which 3 were waited for; matrix products, arithmetic and copies ran while one was open for 31% of the time, Pallas kernels for 0%

profile of v6, /device:TPU:1, one launch (start us, length us, event | category | flops | bytes accessed | tf_op | source)
XLA Modules:
  0.0 172.1 jit_solution(747604593301515491)
XLA Ops:
  0.7 0.9 convert_reduce_fusion
  1.5 0.7 multiply_add_fusion
  2.2 0.1 select_reduce_fusion
  2.3 0.1 copy.30
  2.4 0.1 reshape.95
  2.6 4.2 %gather_fusion.1 = bf16[256,48,128]{2,1,0:T(8,128)(2,1)} fusion(bf16[160,48,128]{2,1,0:T(8,128)(2,1)} %param.6, s32[1024]{0:T(1024)S(1)} %pad_clamp_fusion.1), kind=kCustom, calls=%fused_computation.1 | custom fusion | bytes 6292480 | tf_op jit(solution)/shard_map/jit(_take)/gather | solution.py:43
  6.8 11.9 %all-to-all-start.1 = ((bf16[128,2,48,128]{3,2,1,0:T(8,128)(2,1)}), bf16[128,2,48,128]{3,2,1,0:T(8,128)(2,1)}, u32[]{:S(2)}, u32[]{:S(2)}) async-start(bf16[128,2,48,128]{3,2,1,0:T(8,128)(2,1)} %bitcast.2), calls=%async_computation.1 | async-start | bytes 6291456 | tf_op jit(solution)/shard_map/all_to_all | solution.py:20
  18.7 0.0 copy-start
  18.7 0.1 convert_element_type.61
  18.8 1.4 copy-done
  20.2 2.3 %add_convert_fusion = bf16[160,48,128]{2,1,0:T(8,128)(2,1)S(1)} fusion(bf16[160,48,128]{2,1,0:T(8,128)(2,1)S(1)} %copy-done, bf16[160,48,128]{2,1,0:T(8,128)(2,1)} %param.7), kind=kLoop, calls=%fused_computation.7 | loop fusion | flops 5898240 | bytes 5898240 | tf_op jit(solution)/shard_map/convert_element_type | solution.py:44
  22.5 0.0 copy-start.1
  22.6 2.7 %gather_fusion = bf16[256,48,128]{2,1,0:T(8,128)(2,1)} fusion(bf16[160,48,128]{2,1,0:T(8,128)(2,1)S(1)} %add_convert_fusion, s32[1024]{0:T(1024)S(1)} %pad_clamp_fusion.1), kind=kCustom, calls=%fused_computation | custom fusion | bytes 6292480 | tf_op jit(solution)/shard_map/jit(_take)/gather | solution.py:47
  25.2 1.1 fusion.26
  26.3 33.7 %all-to-all-done.1 = bf16[128,2,48,128]{3,2,1,0:T(8,128)(2,1)} async-done(((bf16[128,2,48,128]{3,2,1,0:T(8,128)(2,1)}), bf16[128,2,48,128]{3,2,1,0:T(8,128)(2,1)}, u32[]{:S(2)}, u32[]{:S(2)}) %all-to-all-start.1) | async-done | bytes 3145760 | tf_op jit(solution)/shard_map/all_to_all | solution.py:20
  60.0 4.7 %all-to-all-start = ((bf16[128,2,48,128]{3,2,1,0:T(8,128)(2,1)}), bf16[128,2,48,128]{3,2,1,0:T(8,128)(2,1)S(1)}, u32[]{:S(2)}, u32[]{:S(2)}) async-start(bf16[128,2,48,128]{3,2,1,0:T(8,128)(2,1)} %bitcast.80), calls=%async_computation | async-start | bytes 6291456 | tf_op jit(solution)/shard_map/all_to_all | solution.py:20
  64.6 4.1 %fusion.25 = (bf16[128,1,48,128]{3,2,1,0:T(8,128)(2,1)}, bf16[128,1,48,128]{3,2,1,0:T(8,128)(2,1)}) fusion(bf16[128,2,48,128]{3,2,1,0:T(8,128)(2,1)} %all-to-all-done.1), kind=kLoop, calls=%fused_computation.68 | loop fusion | bytes 6291456 | tf_op jit(solution)/shard_map/slice | solution.py:57
  68.8 2.6 %copy.32 = bf16[4,128,1536]{2,1,0:T(8,128)(2,1)} copy(bf16[4,128,1536]{1,2,0:T(8,128)(2,1)} %bitcast.81) | data formatting | bytes 3145728 | tf_op jit(solution)/shard_map/tik,sil->tksl/dot_general | solution.py:59
  71.3 2.6 %copy.31 = bf16[4,128,1536]{2,1,0:T(8,128)(2,1)} copy(bf16[4,128,1536]{1,2,0:T(8,128)(2,1)} %bitcast.83) | data formatting | bytes 3145728 | tf_op jit(solution)/shard_map/tik,sil->tksl/dot_general | solution.py:59
  73.9 3.3 %fusion.14 = f32[1,512,512]{2,1,0:T(8,128)S(1)} fusion(bf16[512,1536]{1,0:T(8,128)(2,1)} %bitcast.87, f32[2,512,512]{2,1,0:T(8,128)} %param.8), kind=kOutput, calls=%fused_computation.35 | convolution fusion | flops 806092800 | bytes 5242880 | tf_op jit(solution)/shard_map/tik,sil->tksl/dot_general | solution.py:59
  77.3 1.0 fusion.12
  78.3 0.0 copy-start.3
  78.3 1.5 pad_maximum_fusion.1
  79.8 0.9 copy-done.3
  80.6 4.8 %multiply_reduce_fusion = (f32[2]{0:T(128)S(1)}, f32[2,512,512]{2,1,0:T(8,128)}) fusion(f32[2,512,512]{2,1,0:T(8,128)S(1)} %copy-done.3, f32[1,512,512]{2,1,0:T(8,128)S(1)} %fusion.14, f32[1,512,512]{2,1,0:T(8,128)S(1)} %fusion.12), kind=kOutput, calls=%fused_computation.22 | convolution fusion | flops 3222798336 | bytes 6291464 | tf_op jit(solution)/shard_map/cij,cjk->cik/dot_general | solution.py:68
  85.5 6.5 %multiply_subtract_fusion.1 = f32[2,512,512]{2,1,0:T(8,128)} fusion(f32[2,512,512]{2,1,0:T(8,128)} %get-tuple-element.26, f32[2]{0:T(128)S(1)} %sqrt_multiply_fusion), kind=kOutput, calls=%fused_computation.21 | convolution fusion | flops 1078460416 | bytes 4194312 | tf_op jit(solution)/shard_map/cik,ckj->cij/dot_general | solution.py:13
  92.0 6.3 %multiply_subtract_fusion = f32[2,512,512]{2,1,0:T(8,128)} fusion(f32[2,512,512]{2,1,0:T(8,128)} %multiply_subtract_fusion.1), kind=kOutput, calls=%fused_computation.20 | convolution fusion | flops 1076887552 | bytes 4194304 | tf_op jit(solution)/shard_map/cik,ckj->cij/dot_general | solution.py:13
  98.3 4.9 %fusion.2 = f32[1536,512]{1,0:T(8,128)} fusion(bf16[4,1536,128]{2,1,0:T(8,128)(2,1)} %bitcast.84, bf16[4,128,512]{2,1,0:T(8,128)(2,1)} %bitcast.93, bf16[2,1536,512]{2,1,0:T(8,128)(2,1)} %param.10), kind=kOutput, calls=%fused_computation.13 | convolution fusion | flops 809238528 | bytes 6815744 | tf_op jit(solution)/shard_map/tik,tkj->ij/dot_general | solution.py:63
  103.2 0.0 copy-done.12
  103.2 2.8 %fusion.1 = f32[1536,512]{1,0:T(8,128)} fusion(bf16[4,1536,128]{2,1,0:T(8,128)(2,1)S(1)} %bitcast.82, bf16[4,128,512]{2,1,0:T(8,128)(2,1)S(1)} %bitcast.96, bf16[2,1536,512]{2,1,0:T(8,128)(2,1)S(1)} %copy-done.14), kind=kOutput, calls=%fused_computation.11 | convolution fusion | flops 809238528 | bytes 6815744 | tf_op jit(solution)/shard_map/tik,tkj->ij/dot_general | solution.py:63
  106.0 0.2 all-to-all-done
  106.3 0.5 fusion.24
  106.8 1.3 copy-done.8
  108.2 0.1 copy-done.13
  108.3 1.6 divide_convert_fusion
  109.9 1.0 convolution_convert_fusion
  110.9 0.8 copy-done.6
  111.8 0.1 copy-done.11
  111.9 1.8 %divide_convert_fusion.1 = bf16[1536,512]{1,0:T(8,128)(2,1)S(1)} fusion(f32[1536,512]{1,0:T(8,128)S(1)} %copy-done.6, bf16[4,1536,128]{2,1,0:T(8,128)(2,1)S(1)} %bitcast.90, bf16[4,128,512]{2,1,0:T(8,128)(2,1)S(1)} %bitcast.94), kind=kOutput, calls=%fused_computation.16 | convolution fusion | flops 807665664 | bytes 6815744 | tf_op jit(solution)/shard_map/tik,tkj->ij/dot_general | solution.py:85
  113.7 1.0 convolution_convert_fusion.1
  114.8 2.0 %pad_maximum_fusion = bf16[128,2,48,128]{3,2,1,0:T(8,128)(2,1)} fusion(bf16[128,1,48,128]{3,2,1,0:T(8,128)(2,1)S(1)} %bitcast.89, bf16[128,1,48,128]{3,2,1,0:T(8,128)(2,1)S(1)} %bitcast.92), kind=kLoop, calls=%fused_computation.14 | loop fusion | flops 1572864 | bytes 6291456 | tf_op jit(solution)/shard_map/stack | solution.py:95
  116.7 10.0 %all-to-all-start.2 = ((bf16[128,2,48,128]{3,2,1,0:T(8,128)(2,1)}), bf16[128,2,48,128]{3,2,1,0:T(8,128)(2,1)}, u32[]{:S(2)}, u32[]{:S(2)}) async-start(bf16[128,2,48,128]{3,2,1,0:T(8,128)(2,1)} %pad_maximum_fusion), calls=%async_computation.2 | async-start | bytes 6291456 | tf_op jit(solution)/shard_map/all_to_all | solution.py:20
  126.7 0.2 compare_reduce_fusion
  126.9 0.0 copy-start.9
  126.9 4.5 %broadcast_select_fusion = (f32[2,512,512]{2,1,0:T(8,128)}, f32[2,512,512]{2,1,0:T(8,128)}) fusion(f32[2,512,512]{2,1,0:T(8,128)} %multiply_subtract_fusion, pred[2]{0:T(512)(128)(4,1)S(1)} %compare_reduce_fusion, f32[2,512,512]{2,1,0:T(8,128)S(1)} %copy-done.4), kind=kLoop, calls=%fused_computation.36 | loop fusion | flops 1048576 | bytes 8388610 | tf_op jit(solution)/shard_map/jit(_where)/select_n | solution.py:107
  131.5 2.7 %fusion = bf16[2,1536,512]{2,1,0:T(8,128)(2,1)} fusion(f32[1,1536,512]{2,1,0:T(8,128)S(1)} %bitcast.86, f32[1,1536,512]{2,1,0:T(8,128)S(1)} %bitcast.85, pred[2]{0:T(512)(128)(4,1)S(1)} %compare_reduce_fusion), kind=kLoop, calls=%fused_computation.4 | loop fusion | flops 7864320 | bytes 9437186 | tf_op jit(solution)/shard_map/convert_element_type | solution.py:108
  134.2 33.9 %all-to-all-done.2 = bf16[128,2,48,128]{3,2,1,0:T(8,128)(2,1)} async-done(((bf16[128,2,48,128]{3,2,1,0:T(8,128)(2,1)}), bf16[128,2,48,128]{3,2,1,0:T(8,128)(2,1)}, u32[]{:S(2)}, u32[]{:S(2)}) %all-to-all-start.2) | async-done | bytes 3145760 | tf_op jit(solution)/shard_map/all_to_all | solution.py:20
  168.0 4.1 %gather_fusion.2 = bf16[160,48,128]{2,1,0:T(8,128)(2,1)} fusion(bf16[256,48,128]{2,1,0:T(8,128)(2,1)} %bitcast.30, s32[1024]{0:T(1024)S(1)} %pad_clamp_fusion), kind=kCustom, calls=%fused_computation.2 | custom fusion | bytes 3932800 | tf_op jit(solution)/shard_map/jit(_take)/gather | solution.py:97
  (27 shorter events, 0.1 us)
Async XLA Ops:
  6.8 11.9 %copy-start.2 = (f32[2,512,512]{2,1,0:T(8,128)S(1)}, f32[2,512,512]{2,1,0:T(8,128)}, u32[]{:S(2)}) copy-start(f32[2,512,512]{2,1,0:T(8,128)} %param.9) | copy-start | bytes 6291460
  6.8 53.2 %all-to-all-start.1 = ((bf16[128,2,48,128]{3,2,1,0:T(8,128)(2,1)}), bf16[128,2,48,128]{3,2,1,0:T(8,128)(2,1)}, u32[]{:S(2)}, u32[]{:S(2)}) async-start(bf16[128,2,48,128]{3,2,1,0:T(8,128)(2,1)} %bitcast.2), calls=%async_computation.1 | async-start | bytes 6291456 | tf_op jit(solution)/shard_map/all_to_all | solution.py:20
  18.7 1.5 copy-start
  22.5 2.7 %copy-start.1 = (bf16[160,48,128]{2,1,0:T(8,128)(2,1)}, bf16[160,48,128]{2,1,0:T(8,128)(2,1)S(1)}, u32[]{:S(2)}) copy-start(bf16[160,48,128]{2,1,0:T(8,128)(2,1)S(1)} %add_convert_fusion) | copy-start | bytes 5898244
  60.0 46.3 %all-to-all-start = ((bf16[128,2,48,128]{3,2,1,0:T(8,128)(2,1)}), bf16[128,2,48,128]{3,2,1,0:T(8,128)(2,1)S(1)}, u32[]{:S(2)}, u32[]{:S(2)}) async-start(bf16[128,2,48,128]{3,2,1,0:T(8,128)(2,1)} %bitcast.80), calls=%async_computation | async-start | bytes 6291456 | tf_op jit(solution)/shard_map/all_to_all | solution.py:20
  73.9 3.3 %copy-start.10 = (bf16[4,128,1536]{2,1,0:T(8,128)(2,1)S(1)}, bf16[4,128,1536]{2,1,0:T(8,128)(2,1)}, u32[]{:S(2)}) copy-start(bf16[4,128,1536]{2,1,0:T(8,128)(2,1)} %copy.31) | copy-start | bytes 4718596
  73.9 3.4 %copy-start.15 = (f32[2,512,512]{2,1,0:T(8,128)S(1)}, f32[2,512,512]{2,1,0:T(8,128)}, u32[]{:S(2)}) copy-start(f32[2,512,512]{2,1,0:T(8,128)} %param.8) | copy-start | bytes 6291460
  78.3 2.4 %copy-start.3 = (f32[2,512,512]{2,1,0:T(8,128)S(1)}, f32[2,512,512]{2,1,0:T(8,128)}, u32[]{:S(2)}) copy-start(f32[2,512,512]{2,1,0:T(8,128)} %param.9) | copy-start | bytes 6291460
  98.3 4.9 %copy-start.5 = (bf16[128,1,48,128]{3,2,1,0:T(8,128)(2,1)S(1)}, bf16[128,1,48,128]{3,2,1,0:T(8,128)(2,1)}, u32[]{:S(2)}) copy-start(bf16[128,1,48,128]{3,2,1,0:T(8,128)(2,1)} %get-tuple-element.17) | copy-start | bytes 4718596
  98.3 4.9 %copy-start.12 = (bf16[1,512,512]{2,1,0:T(8,128)(2,1)S(1)}, bf16[1,512,512]{2,1,0:T(8,128)(2,1)}, u32[]{:S(2)}) copy-start(bf16[1,512,512]{2,1,0:T(8,128)(2,1)} %get-tuple-element.20) | copy-start | bytes 1572868
  98.3 4.9 %copy-start.14 = (bf16[2,1536,512]{2,1,0:T(8,128)(2,1)S(1)}, bf16[2,1536,512]{2,1,0:T(8,128)(2,1)}, u32[]{:S(2)}) copy-start(bf16[2,1536,512]{2,1,0:T(8,128)(2,1)} %param.10) | copy-start | bytes 9437188
  106.3 1.9 %copy-start.8 = (f32[1536,512]{1,0:T(8,128)S(1)}, f32[1536,512]{1,0:T(8,128)}, u32[]{:S(2)}) copy-start(f32[1536,512]{1,0:T(8,128)} %fusion.1) | copy-start | bytes 9437188
  106.3 2.0 %copy-start.13 = (bf16[1,512,512]{2,1,0:T(8,128)(2,1)S(1)}, bf16[1,512,512]{2,1,0:T(8,128)(2,1)}, u32[]{:S(2)}) copy-start(bf16[1,512,512]{2,1,0:T(8,128)(2,1)} %get-tuple-element.20) | copy-start | bytes 1572868
  109.9 1.9 %copy-start.6 = (f32[1536,512]{1,0:T(8,128)S(1)}, f32[1536,512]{1,0:T(8,128)}, u32[]{:S(2)}) copy-start(f32[1536,512]{1,0:T(8,128)} %fusion.2) | copy-start | bytes 9437188
  109.9 2.0 %copy-start.11 = (bf16[1,512,512]{2,1,0:T(8,128)(2,1)S(1)}, bf16[1,512,512]{2,1,0:T(8,128)(2,1)}, u32[]{:S(2)}) copy-start(bf16[1,512,512]{2,1,0:T(8,128)(2,1)} %get-tuple-element.19) | copy-start | bytes 1572868
  116.7 10.2 %copy-start.4 = (f32[2,512,512]{2,1,0:T(8,128)S(1)}, f32[2,512,512]{2,1,0:T(8,128)}, u32[]{:S(2)}) copy-start(f32[2,512,512]{2,1,0:T(8,128)} %pad_maximum_fusion.1) | copy-start | bytes 6291460
  116.7 51.3 %all-to-all-start.2 = ((bf16[128,2,48,128]{3,2,1,0:T(8,128)(2,1)}), bf16[128,2,48,128]{3,2,1,0:T(8,128)(2,1)}, u32[]{:S(2)}, u32[]{:S(2)}) async-start(bf16[128,2,48,128]{3,2,1,0:T(8,128)(2,1)} %pad_maximum_fusion), calls=%async_computation.2 | async-start | bytes 6291456 | tf_op jit(solution)/shard_map/all_to_all | solution.py:20
  126.9 4.6 %copy-start.7 = (f32[1536,512]{1,0:T(8,128)S(1)}, f32[1536,512]{1,0:T(8,128)}, u32[]{:S(2)}) copy-start(f32[1536,512]{1,0:T(8,128)} %fusion.2) | copy-start | bytes 9437188
  126.9 4.6 %copy-start.9 = (f32[1536,512]{1,0:T(8,128)S(1)}, f32[1536,512]{1,0:T(8,128)}, u32[]{:S(2)}) copy-start(f32[1536,512]{1,0:T(8,128)} %fusion.1) | copy-start | bytes 9437188

commit v7 on v6

--- a/solution.py
+++ b/solution.py
@@ -72,13 +72,7 @@
         precision=lax.Precision.HIGHEST,
         preferred_element_type=jnp.float32,
     )
-    iterate = power / (
-        2.0 * jnp.sqrt(full_cols * jnp.mean(power * power, axis=(1, 2), keepdims=True) + 1e-06)
-    )
-    iterate = refine(iterate)
-    got_moms, second_list, stat_next, iterate = lax.optimization_barrier(
-        (got_moms, second_list, stat_next, iterate)
-    )
+    got_moms, second_list, power = lax.optimization_barrier((got_moms, second_list, power))
     steps = []
     for c in range(capacity):
         basis_rows = basis_b[c].reshape(tensors, piece_cols, full_cols)
@@ -100,6 +94,10 @@
     )
 
     second_next = jnp.stack(second_list)
+    iterate = power / (
+        2.0 * jnp.sqrt(full_cols * jnp.mean(power * power, axis=(1, 2), keepdims=True) + 1e-06)
+    )
+    iterate = refine(iterate)
 
     my_slots = myself * capacity + jnp.arange(capacity, dtype=jnp.int32)
     filled = jnp.any(my_slots[:, None] == slot_id[None, :], axis=1)[:, None, None]

time: 173 us -> 168 us (0.971)
  matrix products: 35.2 us -> 29.1 us
  starting transfers between devices: 26.5 us -> 22.2 us
  waiting for transfers between devices: 67.8 us -> 72 us
    all_to_all x3, starting transfers between devices: 26.5 us -> 22.2 us  [exchange(): lax.all_to_all(pieces, ('tensor', 'owner'), split_axis=0, concat_axis=0,...]
    all_to_all x3, waiting for transfers between devices: 67.8 us -> 72 us  [exchange(): lax.all_to_all(pieces, ('tensor', 'owner'), split_axis=0, concat_axis=0,...]
    dot_general x2, matrix products: 12.8 us -> 9.03 us  [refine(): jnp.einsum('cik,ckj->cij', iter_b, square, preferred_element_type=jnp.flo...]
    select_n x1, other arithmetic: 4.54 us -> 1.63 us  [local(): new_stats = jnp.where(filled, stat_next, 0.0)]
    dot_general x2, matrix products: 7.74 us -> 5.58 us  [local(): jnp.einsum('tik,tkj->ij', grad_b, basis_rows, preferred_element_type=jnp....]
    convert_element_type x1, other arithmetic: 2.67 us -> 4.47 us  [local(): new_second = jnp.where(filled, second_next, 0.0).astype(jnp.bfloat16)]
    unnamed x32 -> x38, local copies, waits for them, and re-layouts: 4.69 us -> 4.28 us
  transfers between devices with their start and end apart: 3 -> 3, of which waited for: 3 -> 3; matrix products, arithmetic and copies ran while one was open for 31% -> 30% of each run, Pallas kernels for 0% -> 0%
where the time goes in v7:
time: 168 us
  waiting for transfers between devices  72 us (43%)
  matrix products  29.1 us (17%)
  local copies, waits for them, and re-layouts  27.9 us (17%)
  starting transfers between devices  22.2 us (13%)
  other arithmetic  15.6 us (9%)
    all_to_all x3, waiting for transfers between devices, exchange(): lax.all_to_all(pieces, ('tensor', 'owner'), split_axis=0, concat_axis=0,...  72 us
    all_to_all x3, starting transfers between devices, exchange(): lax.all_to_all(pieces, ('tensor', 'owner'), split_axis=0, concat_axis=0,...  22.2 us
    dot_general x2, matrix products, refine(): jnp.einsum('cik,ckj->cij', iter_b, square, preferred_element_type=jnp.flo...  9.03 us
    dot_general x2, matrix products, local(): jnp.einsum('tik,tkj->ij', grad_b, basis_rows, preferred_element_type=jnp....  5.58 us
    dot_general x2, local copies, waits for them, and re-layouts, local(): jnp.einsum('tik,sil->tksl', grad_b, grad_b, preferred_element_type=jnp.fl...  5.15 us
    dot_general x1, matrix products, local(): jnp.einsum('cij,cjk->cik', stat_next, bases, precision=lax.Precision.HIGH...  4.83 us
    convert_element_type x1, other arithmetic, local(): new_second = jnp.where(filled, second_next, 0.0).astype(jnp.bfloat16)  4.47 us
    dot_general x2, matrix products, local(): jnp.einsum('tik,sil->tksl', grad_b, grad_b, preferred_element_type=jnp.fl...  4.35 us
  transfers between devices with their start and end apart: 3, of which 3 were waited for; matrix products, arithmetic and copies ran while one was open for 30% of the time, Pallas kernels for 0%

profile of v7, /device:TPU:1, one launch (start us, length us, event | category | flops | bytes accessed | tf_op | source)
XLA Modules:
  0.0 167.7 jit_solution(16765125718461585870)
XLA Ops:
  0.7 0.9 convert_reduce_fusion
  1.5 0.7 multiply_add_fusion
  2.2 0.1 select_reduce_fusion
  2.3 0.1 copy.30
  2.4 0.1 reshape.95
  2.6 4.2 %gather_fusion.1 = bf16[256,48,128]{2,1,0:T(8,128)(2,1)} fusion(bf16[160,48,128]{2,1,0:T(8,128)(2,1)} %param.6, s32[1024]{0:T(1024)S(1)} %pad_clamp_fusion.1), kind=kCustom, calls=%fused_computation.1 | custom fusion | bytes 6292480 | tf_op jit(solution)/shard_map/jit(_take)/gather | solution.py:43
  6.8 11.9 %all-to-all-start.1 = ((bf16[128,2,48,128]{3,2,1,0:T(8,128)(2,1)}), bf16[128,2,48,128]{3,2,1,0:T(8,128)(2,1)}, u32[]{:S(2)}, u32[]{:S(2)}) async-start(bf16[128,2,48,128]{3,2,1,0:T(8,128)(2,1)} %bitcast.81), calls=%async_computation.1 | async-start | bytes 6291456 | tf_op jit(solution)/shard_map/all_to_all | solution.py:20
  18.7 0.0 copy-done
  18.7 3.6 %add_convert_fusion = bf16[160,48,128]{2,1,0:T(8,128)(2,1)} fusion(bf16[160,48,128]{2,1,0:T(8,128)(2,1)S(1)} %copy-done, bf16[160,48,128]{2,1,0:T(8,128)(2,1)} %param.7), kind=kLoop, calls=%fused_computation.7 | loop fusion | flops 5898240 | bytes 5898240 | tf_op jit(solution)/shard_map/convert_element_type | solution.py:44
  22.3 4.2 %gather_fusion = bf16[256,48,128]{2,1,0:T(8,128)(2,1)} fusion(bf16[160,48,128]{2,1,0:T(8,128)(2,1)} %add_convert_fusion, s32[1024]{0:T(1024)S(1)} %pad_clamp_fusion.1), kind=kCustom, calls=%fused_computation | custom fusion | bytes 6292480 | tf_op jit(solution)/shard_map/jit(_take)/gather | solution.py:47
  26.5 33.5 %all-to-all-done.1 = bf16[128,2,48,128]{3,2,1,0:T(8,128)(2,1)} async-done(((bf16[128,2,48,128]{3,2,1,0:T(8,128)(2,1)}), bf16[128,2,48,128]{3,2,1,0:T(8,128)(2,1)}, u32[]{:S(2)}, u32[]{:S(2)}) %all-to-all-start.1) | async-done | bytes 3145760 | tf_op jit(solution)/shard_map/all_to_all | solution.py:20
  60.0 4.7 %all-to-all-start = ((bf16[128,2,48,128]{3,2,1,0:T(8,128)(2,1)}), bf16[128,2,48,128]{3,2,1,0:T(8,128)(2,1)S(1)}, u32[]{:S(2)}, u32[]{:S(2)}) async-start(bf16[128,2,48,128]{3,2,1,0:T(8,128)(2,1)} %bitcast.80), calls=%async_computation | async-start | bytes 6291456 | tf_op jit(solution)/shard_map/all_to_all | solution.py:20
  64.6 1.7 %convert_element_type.61 = bf16[2,512,512]{2,1,0:T(8,128)(2,1)S(1)} convert(f32[2,512,512]{2,1,0:T(8,128)} %param.9) | non-fusion elementwise | flops 524288 | bytes 3145728 | tf_op jit(solution)/shard_map/convert_element_type | solution.py:54
  66.4 1.1 fusion.28
  67.4 4.1 %fusion.27 = (bf16[128,1,48,128]{3,2,1,0:T(8,128)(2,1)}, bf16[128,1,48,128]{3,2,1,0:T(8,128)(2,1)}) fusion(bf16[128,2,48,128]{3,2,1,0:T(8,128)(2,1)} %all-to-all-done.1), kind=kLoop, calls=%fused_computation.68 | loop fusion | bytes 6291456 | tf_op jit(solution)/shard_map/slice | solution.py:57
  71.5 2.6 %copy.32 = bf16[4,128,1536]{2,1,0:T(8,128)(2,1)} copy(bf16[4,128,1536]{1,2,0:T(8,128)(2,1)} %bitcast.82) | data formatting | bytes 3145728 | tf_op jit(solution)/shard_map/tik,sil->tksl/dot_general | solution.py:59
  74.1 2.6 %copy.31 = bf16[4,128,1536]{2,1,0:T(8,128)(2,1)} copy(bf16[4,128,1536]{1,2,0:T(8,128)(2,1)} %bitcast.84) | data formatting | bytes 3145728 | tf_op jit(solution)/shard_map/tik,sil->tksl/dot_general | solution.py:59
  76.7 3.3 %fusion.14 = f32[1,512,512]{2,1,0:T(8,128)S(1)} fusion(bf16[512,1536]{1,0:T(8,128)(2,1)} %bitcast.88, f32[2,512,512]{2,1,0:T(8,128)} %param.8), kind=kOutput, calls=%fused_computation.36 | convolution fusion | flops 806092800 | bytes 5242880 | tf_op jit(solution)/shard_map/tik,sil->tksl/dot_general | solution.py:59
  80.1 0.0 copy-start.1
  80.1 1.0 fusion.12
  81.1 0.9 copy-done.1
  82.0 4.8 %fusion.4 = f32[2,512,512]{2,1,0:T(8,128)} fusion(f32[2,512,512]{2,1,0:T(8,128)S(1)} %copy-done.1, f32[1,512,512]{2,1,0:T(8,128)S(1)} %fusion.14, f32[1,512,512]{2,1,0:T(8,128)S(1)} %fusion.12), kind=kOutput, calls=%fused_computation.24 | convolution fusion | flops 3221749760 | bytes 6291456 | tf_op jit(solution)/shard_map/cij,cjk->cik/dot_general | solution.py:68
  86.9 0.0 copy-start.3
  86.9 2.8 %fusion.2 = f32[1536,512]{1,0:T(8,128)} fusion(bf16[4,1536,128]{2,1,0:T(8,128)(2,1)S(1)} %bitcast.85, bf16[4,128,512]{2,1,0:T(8,128)(2,1)S(1)} %bitcast.94, bf16[2,1536,512]{2,1,0:T(8,128)(2,1)S(1)} %copy-done.17), kind=kOutput, calls=%fused_computation.13 | convolution fusion | flops 809238528 | bytes 6815744 | tf_op jit(solution)/shard_map/tik,tkj->ij/dot_general | solution.py:63
  89.7 2.8 %fusion.1 = f32[1536,512]{1,0:T(8,128)} fusion(bf16[4,1536,128]{2,1,0:T(8,128)(2,1)S(1)} %bitcast.83, bf16[4,128,512]{2,1,0:T(8,128)(2,1)S(1)} %bitcast.97, bf16[2,1536,512]{2,1,0:T(8,128)(2,1)S(1)} %copy-done.17), kind=kOutput, calls=%fused_computation.11 | convolution fusion | flops 809238528 | bytes 6815744 | tf_op jit(solution)/shard_map/tik,tkj->ij/dot_general | solution.py:63
  92.5 13.8 %all-to-all-done = bf16[128,2,48,128]{3,2,1,0:T(8,128)(2,1)S(1)} async-done(((bf16[128,2,48,128]{3,2,1,0:T(8,128)(2,1)}), bf16[128,2,48,128]{3,2,1,0:T(8,128)(2,1)S(1)}, u32[]{:S(2)}, u32[]{:S(2)}) %all-to-all-start) | async-done | bytes 3145760 | tf_op jit(solution)/shard_map/all_to_all | solution.py:20
  106.3 0.5 fusion.26
  106.8 1.3 copy-done.11
  108.2 0.1 copy-done.16
  108.3 1.6 divide_convert_fusion
  109.9 0.0 copy-start.9
  109.9 1.0 convolution_convert_fusion
  110.9 0.8 copy-done.9
  111.8 0.1 copy-done.14
  111.9 1.6 divide_convert_fusion.1
  113.5 1.0 convolution_convert_fusion.1
  114.5 2.0 %pad_maximum_fusion = bf16[128,2,48,128]{3,2,1,0:T(8,128)(2,1)} fusion(bf16[128,1,48,128]{3,2,1,0:T(8,128)(2,1)S(1)} %bitcast.90, bf16[128,1,48,128]{3,2,1,0:T(8,128)(2,1)S(1)} %bitcast.93), kind=kLoop, calls=%fused_computation.14 | loop fusion | flops 1572864 | bytes 6291456 | tf_op jit(solution)/shard_map/stack | solution.py:89
  116.5 5.7 %all-to-all-start.2 = ((bf16[128,2,48,128]{3,2,1,0:T(8,128)(2,1)}), bf16[128,2,48,128]{3,2,1,0:T(8,128)(2,1)}, u32[]{:S(2)}, u32[]{:S(2)}) async-start(bf16[128,2,48,128]{3,2,1,0:T(8,128)(2,1)} %pad_maximum_fusion), calls=%async_computation.2 | async-start | bytes 6291456 | tf_op jit(solution)/shard_map/all_to_all | solution.py:20
  122.2 0.2 compare_reduce_fusion
  122.4 0.4 multiply_reduce_fusion
  122.8 0.6 copy-done.6
  123.4 0.3 copy-done.8
  123.7 1.6 fusion.3
  125.3 2.8 %multiply_subtract_fusion = f32[2,512,512]{2,1,0:T(8,128)} fusion(f32[2,512,512]{2,1,0:T(8,128)S(1)} %copy-done.2, f32[2]{0:T(128)S(1)} %sqrt_multiply_fusion), kind=kOutput, calls=%fused_computation.21 | convolution fusion | flops 1078460416 | bytes 4194312 | tf_op jit(solution)/shard_map/cik,ckj->cij/dot_general | solution.py:13
  128.1 6.3 %subtract_select_fusion = f32[2,512,512]{2,1,0:T(8,128)} fusion(f32[2,512,512]{2,1,0:T(8,128)} %multiply_subtract_fusion, pred[2]{0:T(512)(128)(4,1)S(1)} %compare_reduce_fusion), kind=kOutput, calls=%fused_computation.20 | convolution fusion | flops 1077411840 | bytes 4194306 | tf_op jit(solution)/shard_map/cik,ckj->cij/dot_general | solution.py:13
  134.4 4.5 %fusion = bf16[2,1536,512]{2,1,0:T(8,128)(2,1)} fusion(f32[1,1536,512]{2,1,0:T(8,128)} %bitcast.87, f32[1,1536,512]{2,1,0:T(8,128)S(1)} %bitcast.86, pred[2]{0:T(512)(128)(4,1)S(1)} %compare_reduce_fusion), kind=kLoop, calls=%fused_computation.4 | loop fusion | flops 7864320 | bytes 9437186 | tf_op jit(solution)/shard_map/convert_element_type | solution.py:106
  138.9 24.8 %all-to-all-done.2 = bf16[128,2,48,128]{3,2,1,0:T(8,128)(2,1)} async-done(((bf16[128,2,48,128]{3,2,1,0:T(8,128)(2,1)}), bf16[128,2,48,128]{3,2,1,0:T(8,128)(2,1)}, u32[]{:S(2)}, u32[]{:S(2)}) %all-to-all-start.2) | async-done | bytes 3145760 | tf_op jit(solution)/shard_map/all_to_all | solution.py:20
  163.6 4.1 %gather_fusion.2 = bf16[160,48,128]{2,1,0:T(8,128)(2,1)} fusion(bf16[256,48,128]{2,1,0:T(8,128)(2,1)} %bitcast.30, s32[1024]{0:T(1024)S(1)} %pad_clamp_fusion), kind=kCustom, calls=%fused_computation.2 | custom fusion | bytes 3932800 | tf_op jit(solution)/shard_map/jit(_take)/gather | solution.py:91
  (33 shorter events, 0.1 us)
Async XLA Ops:
  6.8 11.9 %copy-start = (bf16[160,48,128]{2,1,0:T(8,128)(2,1)S(1)}, bf16[160,48,128]{2,1,0:T(8,128)(2,1)}, u32[]{:S(2)}) copy-start(bf16[160,48,128]{2,1,0:T(8,128)(2,1)} %param.6) | copy-start | bytes 5898244
  6.8 53.2 %all-to-all-start.1 = ((bf16[128,2,48,128]{3,2,1,0:T(8,128)(2,1)}), bf16[128,2,48,128]{3,2,1,0:T(8,128)(2,1)}, u32[]{:S(2)}, u32[]{:S(2)}) async-start(bf16[128,2,48,128]{3,2,1,0:T(8,128)(2,1)} %bitcast.81), calls=%async_computation.1 | async-start | bytes 6291456 | tf_op jit(solution)/shard_map/all_to_all | solution.py:20
  60.0 46.3 %all-to-all-start = ((bf16[128,2,48,128]{3,2,1,0:T(8,128)(2,1)}), bf16[128,2,48,128]{3,2,1,0:T(8,128)(2,1)S(1)}, u32[]{:S(2)}, u32[]{:S(2)}) async-start(bf16[128,2,48,128]{3,2,1,0:T(8,128)(2,1)} %bitcast.80), calls=%async_computation | async-start | bytes 6291456 | tf_op jit(solution)/shard_map/all_to_all | solution.py:20
  76.7 3.4 %copy-start.12 = (bf16[4,128,1536]{2,1,0:T(8,128)(2,1)S(1)}, bf16[4,128,1536]{2,1,0:T(8,128)(2,1)}, u32[]{:S(2)}) copy-start(bf16[4,128,1536]{2,1,0:T(8,128)(2,1)} %copy.31) | copy-start | bytes 4718596
  76.7 3.4 %copy-start.18 = (f32[2,512,512]{2,1,0:T(8,128)S(1)}, f32[2,512,512]{2,1,0:T(8,128)}, u32[]{:S(2)}) copy-start(f32[2,512,512]{2,1,0:T(8,128)} %param.8) | copy-start | bytes 6291460
  80.0 1.1 copy-start.5
  80.1 2.0 %copy-start.1 = (f32[2,512,512]{2,1,0:T(8,128)S(1)}, f32[2,512,512]{2,1,0:T(8,128)}, u32[]{:S(2)}) copy-start(f32[2,512,512]{2,1,0:T(8,128)} %param.9) | copy-start | bytes 6291460
  82.0 4.8 %copy-start.7 = (f32[1,512,512]{2,1,0:T(8,128)}, f32[1,512,512]{2,1,0:T(8,128)S(1)}, u32[]{:S(2)}) copy-start(f32[1,512,512]{2,1,0:T(8,128)S(1)} %fusion.12) | copy-start | bytes 3145732
  82.0 4.8 %copy-start.4 = (bf16[128,1,48,128]{3,2,1,0:T(8,128)(2,1)S(1)}, bf16[128,1,48,128]{3,2,1,0:T(8,128)(2,1)}, u32[]{:S(2)}) copy-start(bf16[128,1,48,128]{3,2,1,0:T(8,128)(2,1)} %get-tuple-element.16) | copy-start | bytes 4718596
  82.0 4.8 %copy-start.13 = (bf16[1,512,512]{2,1,0:T(8,128)(2,1)S(1)}, bf16[1,512,512]{2,1,0:T(8,128)(2,1)}, u32[]{:S(2)}) copy-start(bf16[1,512,512]{2,1,0:T(8,128)(2,1)} %get-tuple-element.17) | copy-start | bytes 1572868
  82.0 4.8 %copy-start.17 = (bf16[2,1536,512]{2,1,0:T(8,128)(2,1)S(1)}, bf16[2,1536,512]{2,1,0:T(8,128)(2,1)}, u32[]{:S(2)}) copy-start(bf16[2,1536,512]{2,1,0:T(8,128)(2,1)} %param.10) | copy-start | bytes 9437188
  86.9 2.8 %copy-start.3 = (bf16[128,1,48,128]{3,2,1,0:T(8,128)(2,1)S(1)}, bf16[128,1,48,128]{3,2,1,0:T(8,128)(2,1)}, u32[]{:S(2)}) copy-start(bf16[128,1,48,128]{3,2,1,0:T(8,128)(2,1)} %get-tuple-element.15) | copy-start | bytes 4718596
  86.9 2.8 %copy-start.15 = (bf16[1,512,512]{2,1,0:T(8,128)(2,1)S(1)}, bf16[1,512,512]{2,1,0:T(8,128)(2,1)}, u32[]{:S(2)}) copy-start(bf16[1,512,512]{2,1,0:T(8,128)(2,1)} %get-tuple-element.18) | copy-start | bytes 1572868
  106.3 1.9 %copy-start.11 = (f32[1536,512]{1,0:T(8,128)S(1)}, f32[1536,512]{1,0:T(8,128)}, u32[]{:S(2)}) copy-start(f32[1536,512]{1,0:T(8,128)} %fusion.1) | copy-start | bytes 9437188
  106.3 2.0 %copy-start.16 = (bf16[1,512,512]{2,1,0:T(8,128)(2,1)S(1)}, bf16[1,512,512]{2,1,0:T(8,128)(2,1)}, u32[]{:S(2)}) copy-start(bf16[1,512,512]{2,1,0:T(8,128)(2,1)} %get-tuple-element.18) | copy-start | bytes 1572868
  109.9 1.9 %copy-start.9 = (f32[1536,512]{1,0:T(8,128)S(1)}, f32[1536,512]{1,0:T(8,128)}, u32[]{:S(2)}) copy-start(f32[1536,512]{1,0:T(8,128)} %fusion.2) | copy-start | bytes 9437188
  109.9 2.0 %copy-start.14 = (bf16[1,512,512]{2,1,0:T(8,128)(2,1)S(1)}, bf16[1,512,512]{2,1,0:T(8,128)(2,1)}, u32[]{:S(2)}) copy-start(bf16[1,512,512]{2,1,0:T(8,128)(2,1)} %get-tuple-element.17) | copy-start | bytes 1572868
  116.5 5.9 %copy-start.2 = (f32[2,512,512]{2,1,0:T(8,128)S(1)}, f32[2,512,512]{2,1,0:T(8,128)}, u32[]{:S(2)}) copy-start(f32[2,512,512]{2,1,0:T(8,128)} %fusion.4) | copy-start | bytes 6291460
  116.5 47.1 %all-to-all-start.2 = ((bf16[128,2,48,128]{3,2,1,0:T(8,128)(2,1)}), bf16[128,2,48,128]{3,2,1,0:T(8,128)(2,1)}, u32[]{:S(2)}, u32[]{:S(2)}) async-start(bf16[128,2,48,128]{3,2,1,0:T(8,128)(2,1)} %pad_maximum_fusion), calls=%async_computation.2 | async-start | bytes 6291456 | tf_op jit(solution)/shard_map/all_to_all | solution.py:20
  122.2 1.2 copy-start.6
  122.2 1.5 copy-start.8
  128.1 6.3 %copy-start.10 = (f32[1536,512]{1,0:T(8,128)S(1)}, f32[1536,512]{1,0:T(8,128)}, u32[]{:S(2)}) copy-start(f32[1536,512]{1,0:T(8,128)} %fusion.2) | copy-start | bytes 9437188

commit v8 on v5

--- a/solution.py
+++ b/solution.py
@@ -38,13 +38,18 @@
     device_at = (place % owners) * tensors + place // owners
     targets = device_at[:, None] * capacity + jnp.arange(capacity, dtype=jnp.int32)[None, :]
     hit = targets[:, :, None] == slot_id[None, None, :]
-    which = jnp.sum(jnp.where(hit, matrix_ids[None, None, :], 0), axis=2)
+    pick = hit.astype(jnp.bfloat16)
 
-    got_grads = exchange(jnp.take(gradients, which, axis=0, mode="clip"))
+    def pack(pieces):
+        return jnp.einsum(
+            "dcn,nrk->dcrk", pick, pieces, preferred_element_type=jnp.float32
+        ).astype(jnp.bfloat16)
+
+    got_grads = exchange(pack(gradients))
     new_moments = (0.9 * moments.astype(jnp.float32) + 0.1 * gradients.astype(jnp.float32)).astype(
         jnp.bfloat16
     )
-    got_moms = exchange(jnp.take(new_moments, which, axis=0, mode="clip"))
+    got_moms = exchange(pack(new_moments))
 
     def column_blocks(pieces):
         return pieces.reshape(tensors, owners * piece_rows, piece_cols)
@@ -79,11 +84,9 @@
         ).astype(jnp.bfloat16)
         steps.append(step_b.reshape(devices, piece_rows, piece_cols))
     returned = exchange(jnp.stack(steps, axis=1))
-    owner_place = (owner_list % tensors) * owners + owner_list // tensors
-    update = jnp.take(
-        returned.reshape(devices * capacity, piece_rows, piece_cols),
-        owner_place * capacity + position, axis=0, mode="clip",
-    )
+    update = jnp.einsum(
+        "dcn,dcrk->nrk", pick, returned, preferred_element_type=jnp.float32
+    ).astype(jnp.bfloat16)
 
     stat_next = jnp.stack(stat_list)
     second_next = jnp.stack(second_list)

time: 166 us -> 181 us (1.090)
  other arithmetic: 17.2 us -> 22.5 us
  local copies, waits for them, and re-layouts: 23.4 us -> 28.7 us
  matrix products: 36 us -> 40.6 us
    gather x3 -> x0, local copies, waits for them, and re-layouts: 10.6 us -> none  [the longest x1 4.19 us: local(): got_moms = exchange(jnp.take(new_moments, which, axis=0, mode='clip'))]
    convert_element_type x0 -> x2, local copies, waits for them, and re-layouts: none -> 7.37 us  [pack(): return jnp.einsum('dcn,nrk->dcrk', pick, pieces, preferred_element_type=j...]
    another operation x1, other arithmetic: 1.95 us -> 8.1 us  [local(): returned = exchange(jnp.stack(steps, axis=1))]
    dot_general x0 -> x3, matrix products: none -> 6.08 us  [the longest x2 3.8 us: pack(): jnp.einsum('dcn,nrk->dcrk', pick, pieces, preferred_element_type=jnp.floa...]
    another operation x0 -> x2, local copies, waits for them, and re-layouts: none -> 5.23 us  [local(): returned = exchange(jnp.stack(steps, axis=1))]
    unnamed x24 -> x25, local copies, waits for them, and re-layouts: 2.76 us -> 6.51 us
    slice x1, local copies, waits for them, and re-layouts: 2.86 us -> 0.54 us  [local(): grad_b = column_blocks(got_grads[:, c])]
    slice x1, local copies, waits for them, and re-layouts: 0.54 us -> 2.6 us  [local(): got_moms[:, c]]
  transfers between devices with their start and end apart: 3 -> 3, of which waited for: 3 -> 3; matrix products, arithmetic and copies ran while one was open for 35% -> 30% of each run, Pallas kernels for 0% -> 0%
where the time goes in v8:
time: 181 us
  waiting for transfers between devices  66.4 us (37%)
  matrix products  40.6 us (22%)
  local copies, waits for them, and re-layouts  28.7 us (16%)
  other arithmetic  22.5 us (12%)
  starting transfers between devices  21.8 us (12%)
    all_to_all x3, waiting for transfers between devices, exchange(): lax.all_to_all(pieces, ('tensor', 'owner'), split_axis=0, concat_axis=0,...  66.4 us
    all_to_all x3, starting transfers between devices, exchange(): lax.all_to_all(pieces, ('tensor', 'owner'), split_axis=0, concat_axis=0,...  21.8 us
    dot_general x2, matrix products, refine(): jnp.einsum('cik,ckj->cij', iter_b, square, preferred_element_type=jnp.flo...  12.9 us
    another operation x1, other arithmetic, local(): returned = exchange(jnp.stack(steps, axis=1))  8.1 us
    dot_general x2, matrix products, local(): jnp.einsum('tik,sil->tksl', grad_b, grad_b, preferred_element_type=jnp.fl...  7.62 us
    convert_element_type x2, local copies, waits for them, and re-layouts, pack(): return jnp.einsum('dcn,nrk->dcrk', pick, pieces, preferred_element_type=j...  7.37 us
    unnamed x25, local copies, waits for them, and re-layouts  6.51 us
    convert_element_type x1, other arithmetic, local(): new_second = jnp.where(filled, second_next, 0.0).astype(jnp.bfloat16)  5.43 us
  transfers between devices with their start and end apart: 3, of which 3 were waited for; matrix products, arithmetic and copies ran while one was open for 30% of the time, Pallas kernels for 0%

profile of v8, /device:TPU:1, one launch (start us, length us, event | category | flops | bytes accessed | tf_op | source)
XLA Modules:
  0.0 180.9 jit_solution(1340134154484936040)
XLA Ops:
  0.6 0.9 convert_reduce_fusion
  1.5 0.7 multiply_add_fusion
  2.2 2.7 %convolution_convert_fusion.2 = bf16[128,2,48,128]{3,0,2,1:T(8,128)(2,1)S(1)} fusion(bf16[160,48,128]{2,1,0:T(8,128)(2,1)} %param.6, s32[128,2]{0,1:T(2,128)S(1)} %iota_add_fusion, s32[160]{0:T(256)S(1)} %multiply_add_fusion), kind=kOutput, calls=%fused_computation.19 | convolution fusion | flops 504930304 | bytes 5113472 | tf_op jit(solution)/shard_map/dcn,nrk->dcrk/dot_general | solution.py:44
  4.9 3.7 %copy.46 = bf16[128,2,48,128]{3,2,1,0:T(8,128)(2,1)} copy(bf16[128,2,48,128]{3,0,2,1:T(8,128)(2,1)S(1)} %convolution_convert_fusion.2) | data formatting | bytes 6291456 | tf_op jit(solution)/shard_map/convert_element_type | solution.py:46
  8.6 11.5 %all-to-all-start.1 = ((bf16[128,2,48,128]{3,2,1,0:T(8,128)(2,1)}), bf16[128,2,48,128]{3,2,1,0:T(8,128)(2,1)S(1)}, u32[]{:S(2)}, u32[]{:S(2)}) async-start(bf16[128,2,48,128]{3,2,1,0:T(8,128)(2,1)} %copy.46), calls=%async_computation.1 | async-start | bytes 6291456 | tf_op jit(solution)/shard_map/all_to_all | solution.py:20
  20.0 2.9 %add_convert_fusion = bf16[160,48,128]{2,1,0:T(8,128)(2,1)S(1)} fusion(bf16[160,48,128]{2,1,0:T(8,128)(2,1)} %param.6, bf16[160,48,128]{2,1,0:T(8,128)(2,1)} %param.7), kind=kLoop, calls=%fused_computation.5 | loop fusion | flops 5898240 | bytes 5898240 | tf_op jit(solution)/shard_map/convert_element_type | solution.py:49
  23.0 0.0 copy-start.1
  23.0 1.3 copy-done.1
  24.2 1.1 convolution_convert_fusion.3
  25.4 3.7 %copy.44 = bf16[128,2,48,128]{3,2,1,0:T(8,128)(2,1)} copy(bf16[128,2,48,128]{3,0,2,1:T(8,128)(2,1)S(1)} %convolution_convert_fusion.3) | data formatting | bytes 6291456 | tf_op jit(solution)/shard_map/convert_element_type | solution.py:46
  29.1 32.6 %all-to-all-done.1 = bf16[128,2,48,128]{3,2,1,0:T(8,128)(2,1)S(1)} async-done(((bf16[128,2,48,128]{3,2,1,0:T(8,128)(2,1)}), bf16[128,2,48,128]{3,2,1,0:T(8,128)(2,1)S(1)}, u32[]{:S(2)}, u32[]{:S(2)}) %all-to-all-start.1) | async-done | bytes 3145760 | tf_op jit(solution)/shard_map/all_to_all | solution.py:20
  61.7 5.7 %all-to-all-start = ((bf16[128,2,48,128]{3,2,1,0:T(8,128)(2,1)}), bf16[128,2,48,128]{3,2,1,0:T(8,128)(2,1)}, u32[]{:S(2)}, u32[]{:S(2)}) async-start(bf16[128,2,48,128]{3,2,1,0:T(8,128)(2,1)} %copy.44), calls=%async_computation | async-start | bytes 6291456 | tf_op jit(solution)/shard_map/all_to_all | solution.py:20
  67.4 2.7 %convert_element_type.73 = bf16[2,512,512]{2,1,0:T(8,128)(2,1)} convert(f32[2,512,512]{2,1,0:T(8,128)} %param.9) | non-fusion elementwise | flops 524288 | bytes 3145728 | tf_op jit(solution)/shard_map/convert_element_type | solution.py:59
  70.1 0.2 compare_reduce_fusion
  70.3 1.3 fusion.40
  71.5 0.0 copy-start.7
  71.5 0.0 copy-start.9
  71.6 0.0 copy-start.11
  71.6 0.5 fusion.39
  72.1 0.0 copy-start.3
  72.1 0.2 copy-done.7
  72.3 2.6 %copy-done.11 = bf16[2,1536,512]{2,1,0:T(8,128)(2,1)S(1)} copy-done((bf16[2,1536,512]{2,1,0:T(8,128)(2,1)S(1)}, bf16[2,1536,512]{2,1,0:T(8,128)(2,1)}, u32[]{:S(2)}) %copy-start.11) | copy-done | bytes 3145752
  75.0 1.1 fusion.1
  76.1 2.8 %fusion.2 = f32[1536,512]{1,0:T(8,128)} fusion(bf16[4,1536,128]{2,1,0:T(8,128)(2,1)S(1)} %bitcast.98, bf16[4,128,512]{2,1,0:T(8,128)(2,1)S(1)} %bitcast.111, bf16[2,1536,512]{2,1,0:T(8,128)(2,1)S(1)} %copy-done.11), kind=kOutput, calls=%fused_computation.11 | convolution fusion | flops 809238528 | bytes 6815744 | tf_op jit(solution)/shard_map/tik,tkj->ij/dot_general | solution.py:68
  78.9 29.8 %all-to-all-done = bf16[128,2,48,128]{3,2,1,0:T(8,128)(2,1)} async-done(((bf16[128,2,48,128]{3,2,1,0:T(8,128)(2,1)}), bf16[128,2,48,128]{3,2,1,0:T(8,128)(2,1)}, u32[]{:S(2)}, u32[]{:S(2)}) %all-to-all-start) | async-done | bytes 3145760 | tf_op jit(solution)/shard_map/all_to_all | solution.py:20
  108.6 2.6 %fusion.38 = (bf16[128,1,48,128]{3,2,0,1:T(8,128)(2,1)S(1)}, bf16[128,1,48,128]{3,2,0,1:T(8,128)(2,1)S(1)}) fusion(bf16[128,2,48,128]{3,2,1,0:T(8,128)(2,1)} %all-to-all-done), kind=kLoop, calls=%fused_computation.70 | loop fusion | bytes 6291456 | tf_op jit(solution)/shard_map/slice | solution.py:77
  111.2 0.2 copy-done.6
  111.5 0.1 copy-done.10
  111.6 1.6 divide_convert_fusion.1
  113.2 1.0 convolution_convert_fusion.1
  114.3 2.5 %copy.51 = bf16[128,1,48,128]{3,1,2,0:T(2,128)(2,1)S(1)} copy(bf16[128,1,48,128]{3,2,0,1:T(8,128)(2,1)S(1)} %bitcast.106) | data formatting | bytes 3145728 | tf_op jit(solution)/shard_map/stack;reshape | solution.py:86
  116.8 1.6 divide_convert_fusion
  118.4 1.0 convolution_convert_fusion
  119.5 2.7 %copy.52 = bf16[128,1,48,128]{3,1,2,0:T(2,128)(2,1)S(1)} copy(bf16[128,1,48,128]{3,2,0,1:T(8,128)(2,1)S(1)} %bitcast.107) | data formatting | bytes 3145728 | tf_op jit(solution)/shard_map/stack;reshape | solution.py:86
  122.2 8.1 %pad_maximum_fusion = bf16[128,2,48,128]{3,1,2,0:T(2,128)(2,1)} fusion(bf16[128,1,48,128]{3,1,2,0:T(2,128)(2,1)S(1)} %copy.52, bf16[128,1,48,128]{3,1,2,0:T(2,128)(2,1)S(1)} %copy.51), kind=kLoop, calls=%fused_computation.12 | loop fusion | flops 6291456 | bytes 6291456 | tf_op jit(solution)/shard_map/stack | solution.py:86
  130.3 4.7 %all-to-all-start.2 = ((bf16[128,2,48,128]{3,1,2,0:T(2,128)(2,1)}), bf16[128,2,48,128]{3,1,2,0:T(2,128)(2,1)S(1)}, u32[]{:S(2)}, u32[]{:S(2)}) async-start(bf16[128,2,48,128]{3,1,2,0:T(2,128)(2,1)} %pad_maximum_fusion), calls=%async_computation.2 | async-start | bytes 6291456 | tf_op jit(solution)/shard_map/all_to_all | solution.py:20
  134.9 2.6 %copy.54 = bf16[4,128,1536]{2,1,0:T(8,128)(2,1)} copy(bf16[4,128,1536]{1,2,0:T(8,128)(2,1)} %bitcast.99) | data formatting | bytes 3145728 | tf_op jit(solution)/shard_map/tik,sil->tksl/dot_general | solution.py:64
  137.5 4.3 %fusion.20 = f32[1,512,512]{2,1,0:T(8,128)} fusion(bf16[512,1536]{1,0:T(8,128)(2,1)} %bitcast.102, f32[2,512,512]{2,1,0:T(8,128)} %param.8), kind=kOutput, calls=%fused_computation.40 | convolution fusion | flops 806092800 | bytes 5242880 | tf_op jit(solution)/shard_map/tik,sil->tksl/dot_general | solution.py:64
  141.8 2.6 %copy.55 = bf16[4,128,1536]{2,1,0:T(8,128)(2,1)} copy(bf16[4,128,1536]{1,2,0:T(8,128)(2,1)} %bitcast.97) | data formatting | bytes 3145728 | tf_op jit(solution)/shard_map/tik,sil->tksl/dot_general | solution.py:64
  144.4 3.3 %fusion.22 = f32[1,512,512]{2,1,0:T(8,128)S(1)} fusion(bf16[512,1536]{1,0:T(8,128)(2,1)} %bitcast.103, f32[2,512,512]{2,1,0:T(8,128)} %param.8), kind=kOutput, calls=%fused_computation.42 | convolution fusion | flops 806092800 | bytes 5242880 | tf_op jit(solution)/shard_map/tik,sil->tksl/dot_general | solution.py:64
  147.7 4.8 %multiply_reduce_fusion = (f32[2]{0:T(128)S(1)}, f32[2,512,512]{2,1,0:T(8,128)}) fusion(f32[2,512,512]{2,1,0:T(8,128)S(1)} %copy-done, f32[1,512,512]{2,1,0:T(8,128)S(1)} %fusion.22, f32[1,512,512]{2,1,0:T(8,128)S(1)} %copy-done.4), kind=kOutput, calls=%fused_computation.24 | convolution fusion | flops 3222798336 | bytes 6291464 | tf_op jit(solution)/shard_map/cij,cjk->cik/dot_general | solution.py:93
  152.6 1.6 fusion.12
  154.2 6.4 %multiply_subtract_fusion = f32[2,512,512]{2,1,0:T(8,128)} fusion(f32[2,512,512]{2,1,0:T(8,128)} %get-tuple-element.38, f32[2]{0:T(128)S(1)} %sqrt_multiply_fusion), kind=kOutput, calls=%fused_computation.23 | convolution fusion | flops 1078460416 | bytes 4194312 | tf_op jit(solution)/shard_map/cik,ckj->cij/dot_general | solution.py:13
  160.6 6.4 %subtract_select_fusion = f32[2,512,512]{2,1,0:T(8,128)} fusion(f32[2,512,512]{2,1,0:T(8,128)} %multiply_subtract_fusion, pred[2]{0:T(512)(128)(4,1)S(1)} %compare_reduce_fusion), kind=kOutput, calls=%fused_computation.22 | convolution fusion | flops 1077411840 | bytes 4194306 | tf_op jit(solution)/shard_map/cik,ckj->cij/dot_general | solution.py:13
  167.1 5.4 %fusion = bf16[2,1536,512]{2,1,0:T(8,128)(2,1)} fusion(f32[1,1536,512]{2,1,0:T(8,128)} %bitcast.100, f32[1,1536,512]{2,1,0:T(8,128)} %bitcast.101, pred[2]{0:T(512)(128)(4,1)S(1)} %compare_reduce_fusion), kind=kLoop, calls=%fused_computation.1 | loop fusion | flops 7864320 | bytes 9437186 | tf_op jit(solution)/shard_map/convert_element_type | solution.py:109
  172.5 4.0 %all-to-all-done.2 = bf16[128,2,48,128]{3,1,2,0:T(2,128)(2,1)S(1)} async-done(((bf16[128,2,48,128]{3,1,2,0:T(2,128)(2,1)}), bf16[128,2,48,128]{3,1,2,0:T(2,128)(2,1)S(1)}, u32[]{:S(2)}, u32[]{:S(2)}) %all-to-all-start.2) | async-done | bytes 3145760 | tf_op jit(solution)/shard_map/all_to_all | solution.py:20
  176.6 2.3 %bitcast_convert_fusion = bf16[160,48,128]{2,0,1:T(8,128)(2,1)S(1)} fusion(bf16[128,2,48,128]{3,1,2,0:T(2,128)(2,1)S(1)} %all-to-all-done.2, s32[128,2]{0,1:T(2,128)S(1)} %iota_add_fusion, s32[160]{0:T(256)S(1)} %multiply_add_fusion), kind=kOutput, calls=%fused_computation.4 | convolution fusion | flops 504340480 | bytes 5113472 | tf_op jit(solution)/shard_map/dcn,dcrk->nrk/dot_general | solution.py:87
  178.8 2.0 %copy.58 = bf16[160,48,128]{2,1,0:T(8,128)(2,1)} copy(bf16[160,48,128]{2,0,1:T(8,128)(2,1)S(1)} %bitcast_convert_fusion) | data formatting | bytes 3932160
  (18 shorter events, 0.1 us)
Async XLA Ops:
  8.6 53.1 %all-to-all-start.1 = ((bf16[128,2,48,128]{3,2,1,0:T(8,128)(2,1)}), bf16[128,2,48,128]{3,2,1,0:T(8,128)(2,1)S(1)}, u32[]{:S(2)}, u32[]{:S(2)}) async-start(bf16[128,2,48,128]{3,2,1,0:T(8,128)(2,1)} %copy.46), calls=%async_computation.1 | async-start | bytes 6291456 | tf_op jit(solution)/shard_map/all_to_all | solution.py:20
  23.0 1.3 copy-start.1
  61.7 47.0 %all-to-all-start = ((bf16[128,2,48,128]{3,2,1,0:T(8,128)(2,1)}), bf16[128,2,48,128]{3,2,1,0:T(8,128)(2,1)}, u32[]{:S(2)}, u32[]{:S(2)}) async-start(bf16[128,2,48,128]{3,2,1,0:T(8,128)(2,1)} %copy.44), calls=%async_computation | async-start | bytes 6291456 | tf_op jit(solution)/shard_map/all_to_all | solution.py:20
  71.5 0.8 copy-start.7
  71.5 4.6 %copy-start.9 = (bf16[1,512,512]{2,1,0:T(8,128)(2,1)}, bf16[1,512,512]{2,1,0:T(8,128)(2,1)S(1)}, u32[]{:S(2)}) copy-start(bf16[1,512,512]{2,1,0:T(8,128)(2,1)S(1)} %get-tuple-element.35) | copy-start | bytes 1572868
  71.6 3.4 %copy-start.11 = (bf16[2,1536,512]{2,1,0:T(8,128)(2,1)S(1)}, bf16[2,1536,512]{2,1,0:T(8,128)(2,1)}, u32[]{:S(2)}) copy-start(bf16[2,1536,512]{2,1,0:T(8,128)(2,1)} %param.10) | copy-start | bytes 9437188
  72.1 4.0 %copy-start.2 = (bf16[128,1,48,128]{3,2,1,0:T(8,128)(2,1)}, bf16[128,1,48,128]{3,2,1,0:T(8,128)(2,1)S(1)}, u32[]{:S(2)}) copy-start(bf16[128,1,48,128]{3,2,1,0:T(8,128)(2,1)S(1)} %get-tuple-element.33) | copy-start | bytes 4718596
  72.1 4.0 %copy-start.3 = (bf16[128,1,48,128]{3,2,1,0:T(8,128)(2,1)}, bf16[128,1,48,128]{3,2,1,0:T(8,128)(2,1)S(1)}, u32[]{:S(2)}) copy-start(bf16[128,1,48,128]{3,2,1,0:T(8,128)(2,1)S(1)} %get-tuple-element.34) | copy-start | bytes 4718596
  76.1 40.7 %copy-start.5 = (f32[1536,512]{1,0:T(8,128)}, f32[1536,512]{1,0:T(8,128)S(1)}, u32[]{:S(2)}) copy-start(f32[1536,512]{1,0:T(8,128)S(1)} %fusion.1) | copy-start | bytes 9437188
  108.6 2.9 %copy-start.6 = (f32[1536,512]{1,0:T(8,128)S(1)}, f32[1536,512]{1,0:T(8,128)}, u32[]{:S(2)}) copy-start(f32[1536,512]{1,0:T(8,128)} %fusion.2) | copy-start | bytes 9437188
  108.6 2.9 %copy-start.10 = (bf16[1,512,512]{2,1,0:T(8,128)(2,1)S(1)}, bf16[1,512,512]{2,1,0:T(8,128)(2,1)}, u32[]{:S(2)}) copy-start(bf16[1,512,512]{2,1,0:T(8,128)(2,1)} %copy-done.9) | copy-start | bytes 1572868
  114.3 2.5 %copy-start.8 = (bf16[1,512,512]{2,1,0:T(8,128)(2,1)S(1)}, bf16[1,512,512]{2,1,0:T(8,128)(2,1)}, u32[]{:S(2)}) copy-start(bf16[1,512,512]{2,1,0:T(8,128)(2,1)} %copy-done.7) | copy-start | bytes 1572868
  130.3 46.3 %all-to-all-start.2 = ((bf16[128,2,48,128]{3,1,2,0:T(2,128)(2,1)}), bf16[128,2,48,128]{3,1,2,0:T(2,128)(2,1)S(1)}, u32[]{:S(2)}, u32[]{:S(2)}) async-start(bf16[128,2,48,128]{3,1,2,0:T(2,128)(2,1)} %pad_maximum_fusion), calls=%async_computation.2 | async-start | bytes 6291456 | tf_op jit(solution)/shard_map/all_to_all | solution.py:20
  144.4 3.3 %copy-start = (f32[2,512,512]{2,1,0:T(8,128)S(1)}, f32[2,512,512]{2,1,0:T(8,128)}, u32[]{:S(2)}) copy-start(f32[2,512,512]{2,1,0:T(8,128)} %param.9) | copy-start | bytes 6291460
  144.4 3.4 %copy-start.4 = (f32[1,512,512]{2,1,0:T(8,128)S(1)}, f32[1,512,512]{2,1,0:T(8,128)}, u32[]{:S(2)}) copy-start(f32[1,512,512]{2,1,0:T(8,128)} %fusion.20) | copy-start | bytes 3145732

commit v9 on v5

--- a/solution.py
+++ b/solution.py
@@ -1,6 +1,8 @@
 import jax
 import jax.numpy as jnp
 from jax import lax
+from jax.experimental import pallas as pl
+from jax.experimental.pallas import tpu as pltpu
 from jax.sharding import PartitionSpec as P
 
 
@@ -14,6 +16,41 @@
             "cik,ckj->cij", iter_b, square, preferred_element_type=jnp.float32
         )
     return iterate
+
+
+def _gather_kernel(index_ref, source_ref, out_ref, sems):
+    count = out_ref.shape[0]
+
+    def start(i, carry):
+        pltpu.make_async_copy(source_ref.at[index_ref[i]], out_ref.at[i], sems.at[i]).start()
+        return carry
+
+    def wait(i, carry):
+        pltpu.make_async_copy(source_ref.at[0], out_ref.at[i], sems.at[i]).wait()
+        return carry
+
+    lax.fori_loop(0, count, start, 0)
+    lax.fori_loop(0, count, wait, 0)
+
+
+def gather_rows(source, index):
+    count = index.shape[0]
+    index = jnp.clip(index, 0, source.shape[0] - 1).astype(jnp.int32)
+    row_bytes = source.size // source.shape[0] * source.dtype.itemsize
+    return pl.pallas_call(
+        _gather_kernel,
+        out_shape=jax.ShapeDtypeStruct((count,) + source.shape[1:], source.dtype),
+        grid_spec=pltpu.PrefetchScalarGridSpec(
+            num_scalar_prefetch=1,
+            grid=(1,),
+            in_specs=[pl.BlockSpec(memory_space=pl.ANY)],
+            out_specs=pl.BlockSpec(memory_space=pl.ANY),
+            scratch_shapes=[pltpu.SemaphoreType.DMA((count,))],
+        ),
+        cost_estimate=pl.CostEstimate(
+            flops=0, transcendentals=0, bytes_accessed=2 * count * row_bytes
+        ),
+    )(index, source)
 
 
 def exchange(pieces):
@@ -40,11 +77,15 @@
     hit = targets[:, :, None] == slot_id[None, None, :]
     which = jnp.sum(jnp.where(hit, matrix_ids[None, None, :], 0), axis=2)
 
-    got_grads = exchange(jnp.take(gradients, which, axis=0, mode="clip"))
+    got_grads = exchange(
+        gather_rows(gradients, which.reshape(-1)).reshape(devices, capacity, piece_rows, piece_cols)
+    )
     new_moments = (0.9 * moments.astype(jnp.float32) + 0.1 * gradients.astype(jnp.float32)).astype(
         jnp.bfloat16
     )
-    got_moms = exchange(jnp.take(new_moments, which, axis=0, mode="clip"))
+    got_moms = exchange(
+        gather_rows(new_moments, which.reshape(-1)).reshape(devices, capacity, piece_rows, piece_cols)
+    )
 
     def column_blocks(pieces):
         return pieces.reshape(tensors, owners * piece_rows, piece_cols)
@@ -80,9 +121,8 @@
         steps.append(step_b.reshape(devices, piece_rows, piece_cols))
     returned = exchange(jnp.stack(steps, axis=1))
     owner_place = (owner_list % tensors) * owners + owner_list // tensors
-    update = jnp.take(
-        returned.reshape(devices * capacity, piece_rows, piece_cols),
-        owner_place * capacity + position, axis=0, mode="clip",
+    update = gather_rows(
+        returned.reshape(devices * capacity, piece_rows, piece_cols), owner_place * capacity + position
     )
 
     stat_next = jnp.stack(stat_list)

time: 166 us -> 392 us (2.36)
  Pallas kernels: 0 us -> 262 us
  waiting for transfers between devices: 66.5 us -> 34.1 us
  local copies, waits for them, and re-layouts: 23.4 us -> 15.2 us
  starting transfers between devices: 21.2 us -> 26.3 us
    pallas_call x0 -> x3, Pallas kernels: none -> 262 us  [gather_rows(): pl.pallas_call(_gather_kernel, out_shape=jax.ShapeDtypeStruct((count,) +...]
    all_to_all x3, waiting for transfers between devices: 66.5 us -> 34.1 us  [exchange(): lax.all_to_all(pieces, ('tensor', 'owner'), split_axis=0, concat_axis=0,...]
    gather x3 -> x0, local copies, waits for them, and re-layouts: 10.6 us -> none  [the longest x1 4.19 us: local(): got_moms = exchange(jnp.take(new_moments, which, axis=0, mode='clip'))]
    all_to_all x3, starting transfers between devices: 21.2 us -> 26.3 us  [exchange(): lax.all_to_all(pieces, ('tensor', 'owner'), split_axis=0, concat_axis=0,...]
  transfers between devices with their start and end apart: 3 -> 3, of which waited for: 3 -> 2; matrix products, arithmetic and copies ran while one was open for 35% -> 13% of each run, Pallas kernels for 0% -> 25%
where the time goes in v9:
time: 392 us; the launch traced here: 391 us
  Pallas kernels  262 us (67%)
  matrix products  34.3 us (9%)
  waiting for transfers between devices  34.1 us (9%)
  starting transfers between devices  26.3 us (7%)
  other arithmetic  18.3 us (5%)
  local copies, waits for them, and re-layouts  15.2 us (4%)
    pallas_call x3, Pallas kernels, gather_rows(): pl.pallas_call(_gather_kernel, out_shape=jax.ShapeDtypeStruct((count,) +...  262 us
    all_to_all x3, waiting for transfers between devices, exchange(): lax.all_to_all(pieces, ('tensor', 'owner'), split_axis=0, concat_axis=0,...  34.1 us
    all_to_all x3, starting transfers between devices, exchange(): lax.all_to_all(pieces, ('tensor', 'owner'), split_axis=0, concat_axis=0,...  26.3 us
    dot_general x2, matrix products, refine(): jnp.einsum('cik,ckj->cij', iter_b, square, preferred_element_type=jnp.flo...  12.8 us
  transfers between devices with their start and end apart: 3, of which 2 were waited for; matrix products, arithmetic and copies ran while one was open for 13% of the time, Pallas kernels for 25%

profile of v9, /device:TPU:1, one launch (start us, length us, event | category | flops | bytes accessed | tf_op | source)
XLA Modules:
  0.0 391.1 jit_solution(983916960502628666)
XLA Ops:
  0.6 0.9 convert_reduce_fusion
  1.5 1.2 multiply_add_fusion
  2.7 0.1 select_reduce_fusion
  2.9 0.1 copy.17
  3.0 0.7 min.24.index_ref
  3.7 99.5 %shard_map.102 = bf16[256,48,128]{2,1,0:T(8,128)(2,1)} custom-call(s32[256]{0:T(256)} %min.24.index_ref, bf16[160,48,128]{2,1,0:T(8,128)(2,1)} %source_ref.1), custom_call_target="tpu_custom_call" | custom-call | bytes 6291456 | tf_op jit(solution)/shard_map/pallas_call | solution.py:40
  103.2 11.5 %all-to-all-start.1 = ((bf16[128,2,48,128]{3,2,1,0:T(8,128)(2,1)}), bf16[128,2,48,128]{3,2,1,0:T(8,128)(2,1)S(1)}, u32[]{:S(2)}, u32[]{:S(2)}) async-start(bf16[128,2,48,128]{3,2,1,0:T(8,128)(2,1)} %bitcast.82), calls=%async_computation.1 | async-start | bytes 6291456 | tf_op jit(solution)/shard_map/all_to_all | solution.py:57
  114.7 4.2 %add_convert_fusion.source_ref = bf16[160,48,128]{2,1,0:T(8,128)(2,1)} fusion(bf16[160,48,128]{2,1,0:T(8,128)(2,1)} %source_ref.1, bf16[160,48,128]{2,1,0:T(8,128)(2,1)} %param.7), kind=kLoop, calls=%fused_computation.4 | loop fusion | flops 5898240 | bytes 5898240 | tf_op jit(solution)/shard_map/convert_element_type | solution.py:83
  118.8 99.5 %shard_map.101 = bf16[256,48,128]{2,1,0:T(8,128)(2,1)} custom-call(s32[256]{0:T(256)} %min.24.index_ref, bf16[160,48,128]{2,1,0:T(8,128)(2,1)} %add_convert_fusion.source_ref), custom_call_target="tpu_custom_call" | custom-call | bytes 6291456 | tf_op jit(solution)/shard_map/pallas_call | solution.py:40
  218.3 0.0 all-to-all-done.1
  218.3 10.2 %all-to-all-start = ((bf16[128,2,48,128]{3,2,1,0:T(8,128)(2,1)}), bf16[128,2,48,128]{3,2,1,0:T(8,128)(2,1)}, u32[]{:S(2)}, u32[]{:S(2)}) async-start(bf16[128,2,48,128]{3,2,1,0:T(8,128)(2,1)} %bitcast.80), calls=%async_computation | async-start | bytes 6291456 | tf_op jit(solution)/shard_map/all_to_all | solution.py:57
  228.5 2.7 convert_element_type.61
  231.2 0.2 compare_reduce_fusion
  231.4 1.3 fusion.28
  232.7 0.0 copy-start.7
  232.7 0.0 copy-start.9
  232.7 0.0 copy-start.11
  232.7 0.5 fusion.27
  233.2 0.0 copy-start.2
  233.3 0.0 copy-start.3
  233.3 0.2 copy-done.7
  233.5 2.6 copy-done.11
  236.1 1.1 fusion.2
  237.3 2.8 fusion.1
  240.0 29.8 %all-to-all-done = bf16[128,2,48,128]{3,2,1,0:T(8,128)(2,1)} async-done(((bf16[128,2,48,128]{3,2,1,0:T(8,128)(2,1)}), bf16[128,2,48,128]{3,2,1,0:T(8,128)(2,1)}, u32[]{:S(2)}, u32[]{:S(2)}) %all-to-all-start) | async-done | bytes 3145760 | tf_op jit(solution)/shard_map/all_to_all | solution.py:57
  269.8 2.6 fusion.26
  272.4 0.2 copy-done.6
  272.7 0.1 copy-done.10
  272.8 1.6 divide_convert_fusion
  274.4 0.0 copy-start.8
  274.4 1.0 convolution_convert_fusion
  275.4 0.0 copy-done.5
  275.5 1.6 divide_convert_fusion.1
  277.1 1.0 convolution_convert_fusion.1
  278.1 2.0 pad_maximum_fusion
  280.1 4.7 %all-to-all-start.2 = ((bf16[128,2,48,128]{3,2,1,0:T(8,128)(2,1)}), bf16[128,2,48,128]{3,2,1,0:T(8,128)(2,1)S(1)}, u32[]{:S(2)}, u32[]{:S(2)}) async-start(bf16[128,2,48,128]{3,2,1,0:T(8,128)(2,1)} %pad_maximum_fusion), calls=%async_computation.2 | async-start | bytes 6291456 | tf_op jit(solution)/shard_map/all_to_all | solution.py:57
  284.8 2.6 copy.21
  287.3 4.3 %fusion.14 = f32[1,512,512]{2,1,0:T(8,128)} fusion(bf16[512,1536]{1,0:T(8,128)(2,1)} %bitcast.89, f32[2,512,512]{2,1,0:T(8,128)} %param.8), kind=kOutput, calls=%fused_computation.33 | convolution fusion | flops 806092800 | bytes 5242880 | tf_op jit(solution)/shard_map/tik,sil->tksl/dot_general | solution.py:100
  291.6 2.6 copy.20
  294.2 3.3 fusion.12
  297.6 4.8 %multiply_reduce_fusion = (f32[2]{0:T(128)S(1)}, f32[2,512,512]{2,1,0:T(8,128)}) fusion(f32[2,512,512]{2,1,0:T(8,128)S(1)} %copy-done.1, f32[1,512,512]{2,1,0:T(8,128)S(1)} %copy-done.4, f32[1,512,512]{2,1,0:T(8,128)S(1)} %fusion.12), kind=kOutput, calls=%fused_computation.19 | convolution fusion | flops 3222798336 | bytes 6291464 | tf_op jit(solution)/shard_map/cij,cjk->cik/dot_general | solution.py:130
  302.4 1.6 fusion.4
  304.0 6.4 %multiply_subtract_fusion = f32[2,512,512]{2,1,0:T(8,128)} fusion(f32[2,512,512]{2,1,0:T(8,128)} %get-tuple-element.20, f32[2]{0:T(128)S(1)} %sqrt_multiply_fusion), kind=kOutput, calls=%fused_computation.18 | convolution fusion | flops 1078460416 | bytes 4194312 | tf_op jit(solution)/shard_map/cik,ckj->cij/dot_general | solution.py:15
  310.4 6.3 %subtract_select_fusion = f32[2,512,512]{2,1,0:T(8,128)} fusion(f32[2,512,512]{2,1,0:T(8,128)} %multiply_subtract_fusion, pred[2]{0:T(512)(128)(4,1)S(1)} %compare_reduce_fusion), kind=kOutput, calls=%fused_computation.17 | convolution fusion | flops 1077411840 | bytes 4194306 | tf_op jit(solution)/shard_map/cik,ckj->cij/dot_general | solution.py:15
  316.8 5.4 %fusion = bf16[2,1536,512]{2,1,0:T(8,128)(2,1)} fusion(f32[1,1536,512]{2,1,0:T(8,128)} %bitcast.88, f32[1,1536,512]{2,1,0:T(8,128)} %bitcast.87, pred[2]{0:T(512)(128)(4,1)S(1)} %compare_reduce_fusion), kind=kLoop, calls=%fused_computation.1 | loop fusion | flops 7864320 | bytes 9437186 | tf_op jit(solution)/shard_map/convert_element_type | solution.py:146
  322.2 4.3 %all-to-all-done.2 = bf16[128,2,48,128]{3,2,1,0:T(8,128)(2,1)S(1)} async-done(((bf16[128,2,48,128]{3,2,1,0:T(8,128)(2,1)}), bf16[128,2,48,128]{3,2,1,0:T(8,128)(2,1)S(1)}, u32[]{:S(2)}, u32[]{:S(2)}) %all-to-all-start.2) | async-done | bytes 3145760 | tf_op jit(solution)/shard_map/all_to_all | solution.py:57
  326.5 1.6 copy-done
  328.1 62.8 %shard_map.103 = bf16[160,48,128]{2,1,0:T(8,128)(2,1)} custom-call(s32[160]{0:T(256)} %get-tuple-element.18.index_ref, bf16[256,48,128]{2,1,0:T(8,128)(2,1)} %bitcast.81), custom_call_target="tpu_custom_call" | custom-call | bytes 3932160 | tf_op jit(solution)/shard_map/pallas_call | solution.py:40
  (17 shorter events, 0.1 us)
Async XLA Ops:
  103.2 115.2 %all-to-all-start.1 = ((bf16[128,2,48,128]{3,2,1,0:T(8,128)(2,1)}), bf16[128,2,48,128]{3,2,1,0:T(8,128)(2,1)S(1)}, u32[]{:S(2)}, u32[]{:S(2)}) async-start(bf16[128,2,48,128]{3,2,1,0:T(8,128)(2,1)} %bitcast.82), calls=%async_computation.1 | async-start | bytes 6291456 | tf_op jit(solution)/shard_map/all_to_all | solution.py:57
  218.3 51.5 %all-to-all-start = ((bf16[128,2,48,128]{3,2,1,0:T(8,128)(2,1)}), bf16[128,2,48,128]{3,2,1,0:T(8,128)(2,1)}, u32[]{:S(2)}, u32[]{:S(2)}) async-start(bf16[128,2,48,128]{3,2,1,0:T(8,128)(2,1)} %bitcast.80), calls=%async_computation | async-start | bytes 6291456 | tf_op jit(solution)/shard_map/all_to_all | solution.py:57
  232.7 0.8 copy-start.7
  232.7 4.6 %copy-start.9 = (bf16[1,512,512]{2,1,0:T(8,128)(2,1)}, bf16[1,512,512]{2,1,0:T(8,128)(2,1)S(1)}, u32[]{:S(2)}) copy-start(bf16[1,512,512]{2,1,0:T(8,128)(2,1)S(1)} %get-tuple-element.16) | copy-start | bytes 1572868
  232.7 3.4 copy-start.11
  233.2 4.0 %copy-start.2 = (bf16[128,1,48,128]{3,2,1,0:T(8,128)(2,1)}, bf16[128,1,48,128]{3,2,1,0:T(8,128)(2,1)S(1)}, u32[]{:S(2)}) copy-start(bf16[128,1,48,128]{3,2,1,0:T(8,128)(2,1)S(1)} %get-tuple-element.14) | copy-start | bytes 4718596
  233.3 4.0 %copy-start.3 = (bf16[128,1,48,128]{3,2,1,0:T(8,128)(2,1)}, bf16[128,1,48,128]{3,2,1,0:T(8,128)(2,1)S(1)}, u32[]{:S(2)}) copy-start(bf16[128,1,48,128]{3,2,1,0:T(8,128)(2,1)S(1)} %get-tuple-element.13) | copy-start | bytes 4718596
  237.2 38.2 %copy-start.5 = (f32[1536,512]{1,0:T(8,128)}, f32[1536,512]{1,0:T(8,128)S(1)}, u32[]{:S(2)}) copy-start(f32[1536,512]{1,0:T(8,128)S(1)} %fusion.2) | copy-start | bytes 9437188
  269.8 2.9 copy-start.6
  269.8 2.9 copy-start.10
  274.4 1.0 copy-start.8
  280.1 46.4 %all-to-all-start.2 = ((bf16[128,2,48,128]{3,2,1,0:T(8,128)(2,1)}), bf16[128,2,48,128]{3,2,1,0:T(8,128)(2,1)S(1)}, u32[]{:S(2)}, u32[]{:S(2)}) async-start(bf16[128,2,48,128]{3,2,1,0:T(8,128)(2,1)} %pad_maximum_fusion), calls=%async_computation.2 | async-start | bytes 6291456 | tf_op jit(solution)/shard_map/all_to_all | solution.py:57
  294.2 3.3 copy-start.1
  294.2 3.4 copy-start.4
  326.5 1.6 copy-start

commit v10 on v5

--- a/solution.py
+++ b/solution.py
@@ -63,7 +63,9 @@
         rotated = jnp.einsum(
             "tik,tkj->ij", grad_b, basis_rows, preferred_element_type=jnp.float32
         )
-        second_list.append(0.95 * second[c].astype(jnp.float32) + 0.05 * rotated * rotated)
+        second_list.append(
+            (0.95 * second[c].astype(jnp.float32) + 0.05 * rotated * rotated).astype(jnp.bfloat16)
+        )
     got_moms, second_list = lax.optimization_barrier((got_moms, second_list))
     steps = []
     for c in range(capacity):
@@ -72,7 +74,7 @@
             "tik,tkj->ij", column_blocks(got_moms[:, c]), basis_rows,
             preferred_element_type=jnp.float32,
         )
-        scaled = (moment_rot / (jnp.sqrt(second_list[c]) + 1e-06)).astype(jnp.bfloat16)
+        scaled = (moment_rot / (jnp.sqrt(second_list[c].astype(jnp.float32)) + 1e-06)).astype(jnp.bfloat16)
         scaled = lax.optimization_barrier(scaled)
         step_b = jnp.einsum(
             "ij,tkj->tik", scaled, basis_rows, preferred_element_type=jnp.float32
@@ -103,7 +105,7 @@
     filled = jnp.any(my_slots[:, None] == slot_id[None, :], axis=1)[:, None, None]
     new_stats = jnp.where(filled, stat_next, 0.0)
     new_bases = jnp.where(filled, iterate, 0.0)
-    new_second = jnp.where(filled, second_next, 0.0).astype(jnp.bfloat16)
+    new_second = jnp.where(filled, second_next, jnp.zeros_like(second_next))
     return (new_moments, update, new_stats, new_bases, new_second)
 
 

time: 166 us -> 165 us (level)
  waiting for transfers between devices: 66.5 us -> 64.8 us
    convert_element_type x1 -> x0, other arithmetic: 5.43 us -> none  [local(): new_second = jnp.where(filled, second_next, 0.0).astype(jnp.bfloat16)]
    select_n x0 -> x1, other arithmetic: none -> 3.94 us  [local(): new_second = jnp.where(filled, second_next, jnp.zeros_like(second_next))]
    all_to_all x3, waiting for transfers between devices: 66.5 us -> 64.8 us  [exchange(): lax.all_to_all(pieces, ('tensor', 'owner'), split_axis=0, concat_axis=0,...]
  transfers between devices with their start and end apart: 3 -> 3, of which waited for: 3 -> 3; matrix products, arithmetic and copies ran while one was open for 35% -> 36% of each run, Pallas kernels for 0% -> 0%
where the time goes in v10:
time: 165 us; the launch traced here: 164 us
  waiting for transfers between devices  64.8 us (39%)
  matrix products  37.4 us (23%)
  local copies, waits for them, and re-layouts  24.3 us (15%)
  starting transfers between devices  21.2 us (13%)
  other arithmetic  15.6 us (9%)
    all_to_all x3, waiting for transfers between devices, exchange(): lax.all_to_all(pieces, ('tensor', 'owner'), split_axis=0, concat_axis=0,...  64.8 us
    all_to_all x3, starting transfers between devices, exchange(): lax.all_to_all(pieces, ('tensor', 'owner'), split_axis=0, concat_axis=0,...  21.2 us
    dot_general x2, matrix products, refine(): jnp.einsum('cik,ckj->cij', iter_b, square, preferred_element_type=jnp.flo...  12.8 us
    dot_general x2, matrix products, local(): jnp.einsum('tik,sil->tksl', grad_b, grad_b, preferred_element_type=jnp.fl...  7.5 us
    dot_general x2, matrix products, local(): jnp.einsum('tik,tkj->ij', grad_b, basis_rows, preferred_element_type=jnp....  6.8 us
    dot_general x2, local copies, waits for them, and re-layouts, local(): jnp.einsum('tik,sil->tksl', grad_b, grad_b, preferred_element_type=jnp.fl...  5.15 us
    dot_general x1, matrix products, local(): jnp.einsum('cij,cjk->cik', stat_next, bases, precision=lax.Precision.HIGH...  4.83 us
    gather x1, local copies, waits for them, and re-layouts, local(): got_grads = exchange(jnp.take(gradients, which, axis=0, mode='clip'))  4.19 us
  transfers between devices with their start and end apart: 3, of which 3 were waited for; matrix products, arithmetic and copies ran while one was open for 36% of the time, Pallas kernels for 0%

profile of v10, /device:TPU:1, one launch (start us, length us, event | category | flops | bytes accessed | tf_op | source)
XLA Modules:
  0.0 164.2 jit_solution(12914995458773199477)
XLA Ops:
  0.7 0.9 convert_reduce_fusion
  1.5 0.7 multiply_add_fusion
  2.2 0.1 select_reduce_fusion
  2.3 0.1 copy.30
  2.4 0.1 reshape.95
  2.6 4.2 %gather_fusion.1 = bf16[256,48,128]{2,1,0:T(8,128)(2,1)} fusion(bf16[160,48,128]{2,1,0:T(8,128)(2,1)} %param.6, s32[1024]{0:T(1024)S(1)} %pad_clamp_fusion.1), kind=kCustom, calls=%fused_computation.1 | custom fusion | bytes 6292480 | tf_op jit(solution)/shard_map/jit(_take)/gather | solution.py:43
  6.8 11.9 %all-to-all-start.1 = ((bf16[128,2,48,128]{3,2,1,0:T(8,128)(2,1)}), bf16[128,2,48,128]{3,2,1,0:T(8,128)(2,1)}, u32[]{:S(2)}, u32[]{:S(2)}) async-start(bf16[128,2,48,128]{3,2,1,0:T(8,128)(2,1)} %bitcast.89), calls=%async_computation.1 | async-start | bytes 6291456 | tf_op jit(solution)/shard_map/all_to_all | solution.py:20
  18.7 0.0 copy-done
  18.7 3.6 %add_convert_fusion = bf16[160,48,128]{2,1,0:T(8,128)(2,1)} fusion(bf16[160,48,128]{2,1,0:T(8,128)(2,1)S(1)} %copy-done, bf16[160,48,128]{2,1,0:T(8,128)(2,1)} %param.7), kind=kLoop, calls=%fused_computation.5 | loop fusion | flops 5898240 | bytes 5898240 | tf_op jit(solution)/shard_map/convert_element_type | solution.py:44
  22.3 4.2 %gather_fusion = bf16[256,48,128]{2,1,0:T(8,128)(2,1)} fusion(bf16[160,48,128]{2,1,0:T(8,128)(2,1)} %add_convert_fusion, s32[1024]{0:T(1024)S(1)} %pad_clamp_fusion.1), kind=kCustom, calls=%fused_computation | custom fusion | bytes 6292480 | tf_op jit(solution)/shard_map/jit(_take)/gather | solution.py:47
  26.4 33.6 %all-to-all-done.1 = bf16[128,2,48,128]{3,2,1,0:T(8,128)(2,1)} async-done(((bf16[128,2,48,128]{3,2,1,0:T(8,128)(2,1)}), bf16[128,2,48,128]{3,2,1,0:T(8,128)(2,1)}, u32[]{:S(2)}, u32[]{:S(2)}) %all-to-all-start.1) | async-done | bytes 3145760 | tf_op jit(solution)/shard_map/all_to_all | solution.py:20
  60.0 4.7 %all-to-all-start = ((bf16[128,2,48,128]{3,2,1,0:T(8,128)(2,1)}), bf16[128,2,48,128]{3,2,1,0:T(8,128)(2,1)S(1)}, u32[]{:S(2)}, u32[]{:S(2)}) async-start(bf16[128,2,48,128]{3,2,1,0:T(8,128)(2,1)} %bitcast.88), calls=%async_computation | async-start | bytes 6291456 | tf_op jit(solution)/shard_map/all_to_all | solution.py:20
  64.7 2.7 %convert_element_type.70 = bf16[2,512,512]{2,1,0:T(8,128)(2,1)} convert(f32[2,512,512]{2,1,0:T(8,128)} %param.9) | non-fusion elementwise | flops 524288 | bytes 3145728 | tf_op jit(solution)/shard_map/convert_element_type | solution.py:54
  67.4 0.2 compare_reduce_fusion
  67.6 2.3 %fusion.29 = (bf16[1,512,512]{2,1,0:T(8,128)(2,1)}, bf16[1,512,512]{2,1,0:T(8,128)(2,1)}) fusion(bf16[2,512,512]{2,1,0:T(8,128)(2,1)} %convert_element_type.70), kind=kLoop, calls=%fused_computation.70 | loop fusion | bytes 2097152 | tf_op jit(solution)/shard_map/slice | solution.py:72
  69.8 4.1 %fusion.28 = (bf16[128,1,48,128]{3,2,1,0:T(8,128)(2,1)}, bf16[128,1,48,128]{3,2,1,0:T(8,128)(2,1)}) fusion(bf16[128,2,48,128]{3,2,1,0:T(8,128)(2,1)} %all-to-all-done.1), kind=kLoop, calls=%fused_computation.69 | loop fusion | bytes 6291456 | tf_op jit(solution)/shard_map/slice | solution.py:57
  73.9 2.6 %copy.33 = bf16[4,128,1536]{2,1,0:T(8,128)(2,1)} copy(bf16[4,128,1536]{1,2,0:T(8,128)(2,1)} %bitcast.93) | data formatting | bytes 3145728 | tf_op jit(solution)/shard_map/tik,sil->tksl/dot_general | solution.py:59
  76.5 4.5 %fusion.2 = bf16[1536,512]{1,0:T(8,128)(2,1)} fusion(bf16[4,1536,128]{2,1,0:T(8,128)(2,1)} %bitcast.94, bf16[4,128,512]{2,1,0:T(8,128)(2,1)} %bitcast.106, bf16[2,1536,512]{2,1,0:T(8,128)(2,1)} %param.10), kind=kOutput, calls=%fused_computation.16 | convolution fusion | flops 810024960 | bytes 5242880 | tf_op jit(solution)/shard_map/tik,tkj->ij/dot_general | solution.py:63
  81.0 0.0 copy-done.2
  81.0 0.0 copy-done.6
  81.0 0.0 copy-done.9
  81.0 2.3 %fusion.3 = bf16[1536,512]{1,0:T(8,128)(2,1)} fusion(bf16[4,1536,128]{2,1,0:T(8,128)(2,1)S(1)} %bitcast.92, bf16[4,128,512]{2,1,0:T(8,128)(2,1)S(1)} %bitcast.103, bf16[2,1536,512]{2,1,0:T(8,128)(2,1)S(1)} %copy-done.9), kind=kOutput, calls=%fused_computation.17 | convolution fusion | flops 810024960 | bytes 5242880 | tf_op jit(solution)/shard_map/tik,tkj->ij/dot_general | solution.py:63
  83.3 22.9 %all-to-all-done = bf16[128,2,48,128]{3,2,1,0:T(8,128)(2,1)S(1)} async-done(((bf16[128,2,48,128]{3,2,1,0:T(8,128)(2,1)}), bf16[128,2,48,128]{3,2,1,0:T(8,128)(2,1)S(1)}, u32[]{:S(2)}, u32[]{:S(2)}) %all-to-all-start) | async-done | bytes 3145760 | tf_op jit(solution)/shard_map/all_to_all | solution.py:20
  106.3 0.5 fusion.27
  106.8 0.9 copy-done.4
  107.7 0.1 copy-done.8
  107.8 1.7 %divide_convert_fusion.1 = bf16[1536,512]{1,0:T(8,128)(2,1)S(1)} fusion(bf16[1536,512]{1,0:T(8,128)(2,1)S(1)} %copy-done.4, bf16[4,1536,128]{2,1,0:T(8,128)(2,1)S(1)} %bitcast.101, bf16[4,128,512]{2,1,0:T(8,128)(2,1)S(1)} %bitcast.107), kind=kOutput, calls=%fused_computation.15 | convolution fusion | flops 808452096 | bytes 5242880 | tf_op jit(solution)/shard_map/tik,tkj->ij/dot_general | solution.py:73
  109.5 0.0 copy-start.5
  109.5 0.0 copy-start.7
  109.5 1.0 convolution_convert_fusion.1
  110.6 0.4 copy-done.5
  110.9 0.1 copy-done.7
  111.0 1.7 %divide_convert_fusion = bf16[1536,512]{1,0:T(8,128)(2,1)S(1)} fusion(bf16[1536,512]{1,0:T(8,128)(2,1)S(1)} %copy-done.5, bf16[4,1536,128]{2,1,0:T(8,128)(2,1)S(1)} %bitcast.100, bf16[4,128,512]{2,1,0:T(8,128)(2,1)S(1)} %bitcast.104), kind=kOutput, calls=%fused_computation.14 | convolution fusion | flops 808452096 | bytes 5242880 | tf_op jit(solution)/shard_map/tik,tkj->ij/dot_general | solution.py:73
  112.7 1.0 convolution_convert_fusion
  113.8 1.9 %pad_maximum_fusion = bf16[128,2,48,128]{3,2,1,0:T(8,128)(2,1)} fusion(bf16[128,1,48,128]{3,2,1,0:T(8,128)(2,1)S(1)} %bitcast.102, bf16[128,1,48,128]{3,2,1,0:T(8,128)(2,1)S(1)} %bitcast.99), kind=kLoop, calls=%fused_computation.12 | loop fusion | flops 1572864 | bytes 6291456 | tf_op jit(solution)/shard_map/stack | solution.py:83
  115.7 4.7 %all-to-all-start.2 = ((bf16[128,2,48,128]{3,2,1,0:T(8,128)(2,1)}), bf16[128,2,48,128]{3,2,1,0:T(8,128)(2,1)S(1)}, u32[]{:S(2)}, u32[]{:S(2)}) async-start(bf16[128,2,48,128]{3,2,1,0:T(8,128)(2,1)} %pad_maximum_fusion), calls=%async_computation.2 | async-start | bytes 6291456 | tf_op jit(solution)/shard_map/all_to_all | solution.py:20
  120.3 4.2 %fusion.13 = f32[1,512,512]{2,1,0:T(8,128)} fusion(bf16[512,1536]{1,0:T(8,128)(2,1)} %bitcast.95, f32[2,512,512]{2,1,0:T(8,128)} %param.8), kind=kOutput, calls=%fused_computation.35 | convolution fusion | flops 806092800 | bytes 5242880 | tf_op jit(solution)/shard_map/tik,sil->tksl/dot_general | solution.py:59
  124.5 2.6 %copy.34 = bf16[4,128,1536]{2,1,0:T(8,128)(2,1)} copy(bf16[4,128,1536]{1,2,0:T(8,128)(2,1)} %bitcast.91) | data formatting | bytes 3145728 | tf_op jit(solution)/shard_map/tik,sil->tksl/dot_general | solution.py:59
  127.1 3.3 %fusion.15 = f32[1,512,512]{2,1,0:T(8,128)S(1)} fusion(bf16[512,1536]{1,0:T(8,128)(2,1)} %bitcast.96, f32[2,512,512]{2,1,0:T(8,128)} %param.8), kind=kOutput, calls=%fused_computation.37 | convolution fusion | flops 806092800 | bytes 5242880 | tf_op jit(solution)/shard_map/tik,sil->tksl/dot_general | solution.py:59
  130.4 0.0 copy-done.1
  130.4 0.0 copy-done.3
  130.4 4.8 %multiply_reduce_fusion = (f32[2]{0:T(128)S(1)}, f32[2,512,512]{2,1,0:T(8,128)}) fusion(f32[2,512,512]{2,1,0:T(8,128)S(1)} %copy-done.1, f32[1,512,512]{2,1,0:T(8,128)S(1)} %fusion.15, f32[1,512,512]{2,1,0:T(8,128)S(1)} %copy-done.3), kind=kOutput, calls=%fused_computation.23 | convolution fusion | flops 3222798336 | bytes 6291464 | tf_op jit(solution)/shard_map/cij,cjk->cik/dot_general | solution.py:92
  135.3 1.6 fusion.5
  136.9 6.5 %multiply_subtract_fusion = f32[2,512,512]{2,1,0:T(8,128)} fusion(f32[2,512,512]{2,1,0:T(8,128)} %get-tuple-element.20, f32[2]{0:T(128)S(1)} %sqrt_multiply_fusion), kind=kOutput, calls=%fused_computation.22 | convolution fusion | flops 1078460416 | bytes 4194312 | tf_op jit(solution)/shard_map/cik,ckj->cij/dot_general | solution.py:13
  143.4 6.3 %subtract_select_fusion = f32[2,512,512]{2,1,0:T(8,128)} fusion(f32[2,512,512]{2,1,0:T(8,128)} %multiply_subtract_fusion, pred[2]{0:T(512)(128)(4,1)S(1)} %compare_reduce_fusion), kind=kOutput, calls=%fused_computation.21 | convolution fusion | flops 1077411840 | bytes 4194306 | tf_op jit(solution)/shard_map/cik,ckj->cij/dot_general | solution.py:13
  149.7 3.9 %maximum_select_fusion = bf16[2,1536,512]{2,1,0:T(8,128)(2,1)} fusion(bf16[1,1536,512]{2,1,0:T(8,128)(2,1)} %bitcast.98, bf16[1,1536,512]{2,1,0:T(8,128)(2,1)} %bitcast.97, pred[2]{0:T(512)(128)(4,1)S(1)} %compare_reduce_fusion), kind=kLoop, calls=%fused_computation.13 | loop fusion | flops 3145728 | bytes 6291458 | tf_op jit(solution)/shard_map/jit(_where)/select_n | solution.py:108
  153.7 8.3 %all-to-all-done.2 = bf16[128,2,48,128]{3,2,1,0:T(8,128)(2,1)S(1)} async-done(((bf16[128,2,48,128]{3,2,1,0:T(8,128)(2,1)}), bf16[128,2,48,128]{3,2,1,0:T(8,128)(2,1)S(1)}, u32[]{:S(2)}, u32[]{:S(2)}) %all-to-all-start.2) | async-done | bytes 3145760 | tf_op jit(solution)/shard_map/all_to_all | solution.py:20
  161.9 2.2 %gather_fusion.2 = bf16[160,48,128]{2,1,0:T(8,128)(2,1)} fusion(bf16[256,48,128]{2,1,0:T(8,128)(2,1)S(1)} %bitcast.90, s32[1024]{0:T(1024)S(1)} %pad_clamp_fusion), kind=kCustom, calls=%fused_computation.2 | custom fusion | bytes 3932800 | tf_op jit(solution)/shard_map/jit(_take)/gather | solution.py:85
  (14 shorter events, 0.1 us)
Async XLA Ops:
  6.8 11.9 %copy-start = (bf16[160,48,128]{2,1,0:T(8,128)(2,1)S(1)}, bf16[160,48,128]{2,1,0:T(8,128)(2,1)}, u32[]{:S(2)}) copy-start(bf16[160,48,128]{2,1,0:T(8,128)(2,1)} %param.6) | copy-start | bytes 5898244
  6.8 53.2 %all-to-all-start.1 = ((bf16[128,2,48,128]{3,2,1,0:T(8,128)(2,1)}), bf16[128,2,48,128]{3,2,1,0:T(8,128)(2,1)}, u32[]{:S(2)}, u32[]{:S(2)}) async-start(bf16[128,2,48,128]{3,2,1,0:T(8,128)(2,1)} %bitcast.89), calls=%async_computation.1 | async-start | bytes 6291456 | tf_op jit(solution)/shard_map/all_to_all | solution.py:20
  60.0 46.3 %all-to-all-start = ((bf16[128,2,48,128]{3,2,1,0:T(8,128)(2,1)}), bf16[128,2,48,128]{3,2,1,0:T(8,128)(2,1)S(1)}, u32[]{:S(2)}, u32[]{:S(2)}) async-start(bf16[128,2,48,128]{3,2,1,0:T(8,128)(2,1)} %bitcast.88), calls=%async_computation | async-start | bytes 6291456 | tf_op jit(solution)/shard_map/all_to_all | solution.py:20
  76.5 4.5 %copy-start.2 = (bf16[128,1,48,128]{3,2,1,0:T(8,128)(2,1)S(1)}, bf16[128,1,48,128]{3,2,1,0:T(8,128)(2,1)}, u32[]{:S(2)}) copy-start(bf16[128,1,48,128]{3,2,1,0:T(8,128)(2,1)} %get-tuple-element.13) | copy-start | bytes 4718596
  76.5 4.5 %copy-start.6 = (bf16[1,512,512]{2,1,0:T(8,128)(2,1)S(1)}, bf16[1,512,512]{2,1,0:T(8,128)(2,1)}, u32[]{:S(2)}) copy-start(bf16[1,512,512]{2,1,0:T(8,128)(2,1)} %get-tuple-element.16) | copy-start | bytes 1572868
  76.5 4.5 %copy-start.9 = (bf16[2,1536,512]{2,1,0:T(8,128)(2,1)S(1)}, bf16[2,1536,512]{2,1,0:T(8,128)(2,1)}, u32[]{:S(2)}) copy-start(bf16[2,1536,512]{2,1,0:T(8,128)(2,1)} %param.10) | copy-start | bytes 9437188
  106.3 1.4 copy-start.4
  106.3 1.5 copy-start.8
  109.5 1.4 copy-start.5
  109.5 1.5 copy-start.7
  115.7 46.3 %all-to-all-start.2 = ((bf16[128,2,48,128]{3,2,1,0:T(8,128)(2,1)}), bf16[128,2,48,128]{3,2,1,0:T(8,128)(2,1)S(1)}, u32[]{:S(2)}, u32[]{:S(2)}) async-start(bf16[128,2,48,128]{3,2,1,0:T(8,128)(2,1)} %pad_maximum_fusion), calls=%async_computation.2 | async-start | bytes 6291456 | tf_op jit(solution)/shard_map/all_to_all | solution.py:20
  127.1 3.3 %copy-start.1 = (f32[2,512,512]{2,1,0:T(8,128)S(1)}, f32[2,512,512]{2,1,0:T(8,128)}, u32[]{:S(2)}) copy-start(f32[2,512,512]{2,1,0:T(8,128)} %param.9) | copy-start | bytes 6291460
  127.1 3.4 %copy-start.3 = (f32[1,512,512]{2,1,0:T(8,128)S(1)}, f32[1,512,512]{2,1,0:T(8,128)}, u32[]{:S(2)}) copy-start(f32[1,512,512]{2,1,0:T(8,128)} %fusion.13) | copy-start | bytes 3145732

commit v11 on v4

--- a/solution.py
+++ b/solution.py
@@ -1,6 +1,7 @@
 import jax
 import jax.numpy as jnp
 from jax import lax
+from jax.experimental import pallas as pl
 from jax.sharding import PartitionSpec as P
 
 
@@ -14,6 +15,40 @@
             "cik,ckj->cij", iter_b, square, preferred_element_type=jnp.float32
         )
     return iterate
+
+
+def _update_kernel(moms_ref, second_ref, basis_ref, out_ref):
+    tensors, owners, piece_rows, piece_cols = moms_ref.shape
+    full_rows = owners * piece_rows
+    basis = basis_ref[...]
+    moment_rot = None
+    for t in range(tensors):
+        block = moms_ref[t].reshape(full_rows, piece_cols)
+        part = jnp.dot(block, basis[t * piece_cols:(t + 1) * piece_cols, :],
+                       preferred_element_type=jnp.float32)
+        moment_rot = part if moment_rot is None else moment_rot + part
+    scaled = (moment_rot / (jnp.sqrt(second_ref[...]) + 1e-06)).astype(jnp.bfloat16)
+    for t in range(tensors):
+        step = lax.dot_general(scaled, basis[t * piece_cols:(t + 1) * piece_cols, :],
+                               (((1,), (1,)), ((), ())), preferred_element_type=jnp.float32)
+        out_ref[t] = step.astype(out_ref.dtype).reshape(owners, piece_rows, piece_cols)
+
+def update_pieces(moms, second_next, basis_b):
+    tensors, owners, capacity, piece_rows, piece_cols = moms.shape
+    full_rows, full_cols = second_next.shape[1:]
+    block = pl.BlockSpec((tensors, owners, None, piece_rows, piece_cols), lambda c: (0, 0, c, 0, 0))
+    return pl.pallas_call(
+        _update_kernel,
+        out_shape=jax.ShapeDtypeStruct(moms.shape, jnp.bfloat16),
+        grid=(capacity,),
+        in_specs=[block,
+                  pl.BlockSpec((None, full_rows, full_cols), lambda c: (c, 0, 0)),
+                  pl.BlockSpec((None, full_cols, full_cols), lambda c: (c, 0, 0))],
+        out_specs=block,
+        cost_estimate=pl.CostEstimate(flops=4 * capacity * full_rows * full_cols * full_cols,
+            transcendentals=capacity * full_rows * full_cols,
+            bytes_accessed=capacity * (4 * full_rows * full_cols + 4 * full_rows * full_cols + 2 * full_cols * full_cols)),
+    )(moms, second_next, basis_b)
 
 
 def exchange(pieces):
@@ -64,20 +99,13 @@
             "tik,tkj->ij", grad_b, basis_rows, preferred_element_type=jnp.float32
         )
         second_list.append(0.95 * second[c].astype(jnp.float32) + 0.05 * rotated * rotated)
-    got_moms, second_list = lax.optimization_barrier((got_moms, second_list))
-    steps = []
-    for c in range(capacity):
-        basis_rows = basis_b[c].reshape(tensors, piece_cols, full_cols)
-        moment_rot = jnp.einsum(
-            "tik,tkj->ij", column_blocks(got_moms[:, c]), basis_rows,
-            preferred_element_type=jnp.float32,
-        )
-        scaled = (moment_rot / (jnp.sqrt(second_list[c]) + 1e-06)).astype(jnp.bfloat16)
-        step_b = jnp.einsum(
-            "ij,tkj->tik", scaled, basis_rows, preferred_element_type=jnp.float32
-        ).astype(jnp.bfloat16)
-        steps.append(step_b.reshape(devices, piece_rows, piece_cols))
-    returned = exchange(jnp.stack(steps, axis=1))
+    got_moms, second_next = lax.optimization_barrier((got_moms, jnp.stack(second_list)))
+    step_pieces = update_pieces(
+        got_moms.reshape(tensors, owners, capacity, piece_rows, piece_cols),
+        second_next,
+        basis_b,
+    )
+    returned = exchange(step_pieces.reshape(devices, capacity, piece_rows, piece_cols))
     owner_place = (owner_list % tensors) * owners + owner_list // tensors
     update = jnp.take(
         returned.reshape(devices * capacity, piece_rows, piece_cols),
@@ -85,7 +113,6 @@
     )
 
     stat_next = jnp.stack(stat_list)
-    second_next = jnp.stack(second_list)
     power = jnp.einsum(
         "cij,cjk->cik",
         stat_next,

time: 173 us -> 172 us (level)
  matrix products: 41.8 us -> 20.6 us
  Pallas kernels: 0 us -> 11.8 us
  waiting for transfers between devices: 66.4 us -> 73.9 us
    pallas_call x0 -> x1, Pallas kernels: none -> 11.8 us  [update_pieces(): pl.pallas_call(_update_kernel, out_shape=jax.ShapeDtypeStruct(moms.shape,...]
    dot_general x2 -> x0, matrix products: 11.2 us -> none  [local(): jnp.einsum('ij,tkj->tik', scaled, basis_rows, preferred_element_type=jnp....]
    all_to_all x3, waiting for transfers between devices: 66.4 us -> 73.9 us  [exchange(): lax.all_to_all(pieces, ('tensor', 'owner'), split_axis=0, concat_axis=0,...]
    dot_general x2, matrix products: 12.8 us -> 9.1 us  [refine(): jnp.einsum('cik,ckj->cij', iter_b, square, preferred_element_type=jnp.flo...]
    dot_general x2, matrix products: 5.6 us -> 2.27 us  [local(): jnp.einsum('tik,tkj->ij', grad_b, basis_rows, preferred_element_type=jnp....]
    dot_general x2, matrix products: 7.49 us -> 4.36 us  [local(): jnp.einsum('tik,sil->tksl', grad_b, grad_b, preferred_element_type=jnp.fl...]
    unnamed x18 -> x22, local copies, waits for them, and re-layouts: 0.36 us -> 3.46 us
    slice x1 -> x0, local copies, waits for them, and re-layouts: 2.2 us -> none  [local(): got_moms[:, c]]
  transfers between devices with their start and end apart: 3 -> 3, of which waited for: 3 -> 3; matrix products, arithmetic and copies ran while one was open for 34% -> 28% of each run, Pallas kernels for 0% -> 0%
where the time goes in v11:
time: 172 us; the launch traced here: 171 us
  waiting for transfers between devices  73.9 us (43%)
  local copies, waits for them, and re-layouts  23.2 us (13%)
  starting transfers between devices  22.2 us (13%)
  matrix products  20.6 us (12%)
  other arithmetic  18.5 us (11%)
  Pallas kernels  11.8 us (7%)
    all_to_all x3, waiting for transfers between devices, exchange(): lax.all_to_all(pieces, ('tensor', 'owner'), split_axis=0, concat_axis=0,...  73.9 us
    all_to_all x3, starting transfers between devices, exchange(): lax.all_to_all(pieces, ('tensor', 'owner'), split_axis=0, concat_axis=0,...  22.2 us
    pallas_call x1, Pallas kernels, update_pieces(): pl.pallas_call(_update_kernel, out_shape=jax.ShapeDtypeStruct(moms.shape,...  11.8 us
    dot_general x2, matrix products, refine(): jnp.einsum('cik,ckj->cij', iter_b, square, preferred_element_type=jnp.flo...  9.1 us
    convert_element_type x1, other arithmetic, local(): new_second = jnp.where(filled, second_next, 0.0).astype(jnp.bfloat16)  5.37 us
    dot_general x1, matrix products, local(): jnp.einsum('cij,cjk->cik', stat_next, bases, precision=lax.Precision.HIGH...  4.84 us
    dot_general x2, matrix products, local(): jnp.einsum('tik,sil->tksl', grad_b, grad_b, preferred_element_type=jnp.fl...  4.36 us
    gather x1, local copies, waits for them, and re-layouts, local(): got_grads = exchange(jnp.take(gradients, which, axis=0, mode='clip'))  4.21 us
  transfers between devices with their start and end apart: 3, of which 3 were waited for; matrix products, arithmetic and copies ran while one was open for 28% of the time, Pallas kernels for 0%

profile of v11, /device:TPU:1, one launch (start us, length us, event | category | flops | bytes accessed | tf_op | source)
XLA Modules:
  0.0 170.9 jit_solution(14262917508548028798)
XLA Ops:
  0.6 0.9 convert_reduce_fusion
  1.5 0.7 multiply_add_fusion
  2.2 0.1 select_reduce_fusion
  2.3 0.1 copy.19
  2.4 0.1 reshape.103
  2.6 4.2 %gather_fusion.1 = bf16[256,48,128]{2,1,0:T(8,128)(2,1)} fusion(bf16[160,48,128]{2,1,0:T(8,128)(2,1)} %param.6, s32[1024]{0:T(1024)S(1)} %pad_clamp_fusion.1), kind=kCustom, calls=%fused_computation.1 | custom fusion | bytes 6292480 | tf_op jit(solution)/shard_map/jit(_take)/gather | solution.py:78
  6.8 11.9 %all-to-all-start.1 = ((bf16[128,2,48,128]{3,2,1,0:T(8,128)(2,1)}), bf16[128,2,48,128]{3,2,1,0:T(8,128)(2,1)}, u32[]{:S(2)}, u32[]{:S(2)}) async-start(bf16[128,2,48,128]{3,2,1,0:T(8,128)(2,1)} %bitcast.56), calls=%async_computation.1 | async-start | bytes 6291456 | tf_op jit(solution)/shard_map/all_to_all | solution.py:55
  18.7 0.0 copy-done
  18.7 3.6 %add_convert_fusion = bf16[160,48,128]{2,1,0:T(8,128)(2,1)} fusion(bf16[160,48,128]{2,1,0:T(8,128)(2,1)S(1)} %copy-done, bf16[160,48,128]{2,1,0:T(8,128)(2,1)} %param.7), kind=kLoop, calls=%fused_computation.7 | loop fusion | flops 5898240 | bytes 5898240 | tf_op jit(solution)/shard_map/convert_element_type | solution.py:79
  22.3 4.2 %gather_fusion = bf16[256,48,128]{2,1,0:T(8,128)(2,1)} fusion(bf16[160,48,128]{2,1,0:T(8,128)(2,1)} %add_convert_fusion, s32[1024]{0:T(1024)S(1)} %pad_clamp_fusion.1), kind=kCustom, calls=%fused_computation | custom fusion | bytes 6292480 | tf_op jit(solution)/shard_map/jit(_take)/gather | solution.py:82
  26.5 33.5 %all-to-all-done.1 = bf16[128,2,48,128]{3,2,1,0:T(8,128)(2,1)} async-done(((bf16[128,2,48,128]{3,2,1,0:T(8,128)(2,1)}), bf16[128,2,48,128]{3,2,1,0:T(8,128)(2,1)}, u32[]{:S(2)}, u32[]{:S(2)}) %all-to-all-start.1) | async-done | bytes 3145760 | tf_op jit(solution)/shard_map/all_to_all | solution.py:55
  60.0 4.7 %all-to-all-start = ((bf16[128,2,48,128]{3,2,1,0:T(8,128)(2,1)}), bf16[128,2,48,128]{3,2,1,0:T(8,128)(2,1)S(1)}, u32[]{:S(2)}, u32[]{:S(2)}) async-start(bf16[128,2,48,128]{3,2,1,0:T(8,128)(2,1)} %bitcast), calls=%async_computation | async-start | bytes 6291456 | tf_op jit(solution)/shard_map/all_to_all | solution.py:55
  64.7 2.7 %convert_element_type.43.basis_ref = bf16[2,512,512]{2,1,0:T(8,128)(2,1)} convert(f32[2,512,512]{2,1,0:T(8,128)} %param.9) | non-fusion elementwise | flops 524288 | bytes 3145728 | tf_op jit(solution)/shard_map/convert_element_type | solution.py:89
  67.4 0.2 compare_reduce_fusion
  67.6 1.3 fusion.26
  68.8 0.0 copy-start.9
  68.9 2.6 %fusion.25 = (bf16[128,1,48,128]{3,2,1,0:T(8,128)(2,1)S(1)}, bf16[128,1,48,128]{3,2,1,0:T(8,128)(2,1)S(1)}) fusion(bf16[128,2,48,128]{3,2,1,0:T(8,128)(2,1)} %all-to-all-done.1), kind=kLoop, calls=%fused_computation.60 | loop fusion | bytes 6291456 | tf_op jit(solution)/shard_map/slice | solution.py:92
  71.5 0.0 copy-start.3
  71.5 0.0 copy-start.5
  71.5 0.2 copy-done.9
  71.7 1.1 fusion.1
  72.8 0.0 copy-done.3
  72.8 0.3 copy-done.5
  73.1 1.1 fusion.3
  74.3 3.4 %pad_maximum_fusion.second_ref = f32[2,1536,512]{2,1,0:T(8,128)} fusion(f32[1,1536,512]{2,1,0:T(8,128)S(1)} %fusion.1, f32[1,1536,512]{2,1,0:T(8,128)S(1)} %fusion.3), kind=kLoop, calls=%fused_computation.3 | loop fusion | flops 1572864 | bytes 12582912 | tf_op jit(solution)/shard_map/stack | solution.py:102
  77.6 28.7 %all-to-all-done = bf16[128,2,48,128]{3,2,1,0:T(8,128)(2,1)S(1)} async-done(((bf16[128,2,48,128]{3,2,1,0:T(8,128)(2,1)}), bf16[128,2,48,128]{3,2,1,0:T(8,128)(2,1)S(1)}, u32[]{:S(2)}, u32[]{:S(2)}) %all-to-all-start) | async-done | bytes 3145760 | tf_op jit(solution)/shard_map/all_to_all | solution.py:55
  106.3 1.7 copy-done.1
  108.0 11.8 %shard_map.101 = bf16[4,32,2,48,128]{4,3,2,1,0:T(8,128)(2,1)} custom-call(bf16[4,32,2,48,128]{4,3,2,1,0:T(8,128)(2,1)} %bitcast.57, f32[2,1536,512]{2,1,0:T(8,128)} %pad_maximum_fusion.second_ref, bf16[2,512,512]{2,1,0:T(8,128)(2,1)} %convert_element_type.43.basis_ref), custom_call_target="tpu_custom_call" | custom-call | flops 3221225472 | bytes 13631488 | tf_op jit(solution)/shard_map/pallas_call | solution.py:40
  119.7 5.7 %all-to-all-start.2 = ((bf16[128,2,48,128]{3,2,1,0:T(8,128)(2,1)}), bf16[128,2,48,128]{3,2,1,0:T(8,128)(2,1)}, u32[]{:S(2)}, u32[]{:S(2)}) async-start(bf16[128,2,48,128]{3,2,1,0:T(8,128)(2,1)} %bitcast.58), calls=%async_computation.2 | async-start | bytes 6291456 | tf_op jit(solution)/shard_map/all_to_all | solution.py:55
  125.4 0.0 copy-start.4
  125.4 0.0 copy-done.6
  125.4 1.6 copy.20
  127.0 0.0 copy-done.4
  127.0 1.6 copy.21
  128.6 3.3 %fusion.11 = f32[1,512,512]{2,1,0:T(8,128)S(1)} fusion(bf16[512,1536]{1,0:T(8,128)(2,1)} %bitcast.63, f32[2,512,512]{2,1,0:T(8,128)} %param.8), kind=kOutput, calls=%fused_computation.27 | convolution fusion | flops 806092800 | bytes 5242880 | tf_op jit(solution)/shard_map/tik,sil->tksl/dot_general | solution.py:94
  131.9 0.0 copy-done.8
  131.9 0.0 copy-done.10
  131.9 0.0 copy-start.2
  131.9 1.0 fusion.13
  133.0 0.5 copy-done.2
  133.5 4.8 %multiply_reduce_fusion = (f32[2]{0:T(128)S(1)}, f32[2,512,512]{2,1,0:T(8,128)}) fusion(f32[2,512,512]{2,1,0:T(8,128)S(1)} %copy-done.2, f32[1,512,512]{2,1,0:T(8,128)S(1)} %fusion.13, f32[1,512,512]{2,1,0:T(8,128)S(1)} %fusion.11), kind=kOutput, calls=%fused_computation.17 | convolution fusion | flops 3222798336 | bytes 6291464 | tf_op jit(solution)/shard_map/cij,cjk->cik/dot_general | solution.py:116
  138.4 1.6 fusion.5
  140.0 0.7 copy-done.7
  140.7 2.8 %multiply_subtract_fusion = f32[2,512,512]{2,1,0:T(8,128)} fusion(f32[2,512,512]{2,1,0:T(8,128)S(1)} %copy-done.7, f32[2]{0:T(128)S(1)} %sqrt_multiply_fusion), kind=kOutput, calls=%fused_computation.16 | convolution fusion | flops 1078460416 | bytes 4194312 | tf_op jit(solution)/shard_map/cik,ckj->cij/dot_general | solution.py:14
  143.5 6.3 %subtract_select_fusion = f32[2,512,512]{2,1,0:T(8,128)} fusion(f32[2,512,512]{2,1,0:T(8,128)} %multiply_subtract_fusion, pred[2]{0:T(512)(128)(4,1)S(1)} %compare_reduce_fusion), kind=kOutput, calls=%fused_computation.15 | convolution fusion | flops 1077411840 | bytes 4194306 | tf_op jit(solution)/shard_map/cik,ckj->cij/dot_general | solution.py:14
  149.8 5.4 %select_convert_fusion = bf16[2,1536,512]{2,1,0:T(8,128)(2,1)} fusion(f32[2,1536,512]{2,1,0:T(8,128)} %pad_maximum_fusion.second_ref, pred[2]{0:T(512)(128)(4,1)S(1)} %compare_reduce_fusion), kind=kLoop, calls=%fused_computation.4 | loop fusion | flops 1572864 | bytes 9437186 | tf_op jit(solution)/shard_map/convert_element_type | solution.py:132
  155.2 11.7 %all-to-all-done.2 = bf16[128,2,48,128]{3,2,1,0:T(8,128)(2,1)} async-done(((bf16[128,2,48,128]{3,2,1,0:T(8,128)(2,1)}), bf16[128,2,48,128]{3,2,1,0:T(8,128)(2,1)}, u32[]{:S(2)}, u32[]{:S(2)}) %all-to-all-start.2) | async-done | bytes 3145760 | tf_op jit(solution)/shard_map/all_to_all | solution.py:55
  166.9 4.1 %gather_fusion.2 = bf16[160,48,128]{2,1,0:T(8,128)(2,1)} fusion(bf16[256,48,128]{2,1,0:T(8,128)(2,1)} %bitcast.14, s32[1024]{0:T(1024)S(1)} %pad_clamp_fusion), kind=kCustom, calls=%fused_computation.2 | custom fusion | bytes 3932800 | tf_op jit(solution)/shard_map/jit(_take)/gather | solution.py:110
  (12 shorter events, 0.0 us)
Async XLA Ops:
  6.8 11.9 %copy-start = (bf16[160,48,128]{2,1,0:T(8,128)(2,1)S(1)}, bf16[160,48,128]{2,1,0:T(8,128)(2,1)}, u32[]{:S(2)}) copy-start(bf16[160,48,128]{2,1,0:T(8,128)(2,1)} %param.6) | copy-start | bytes 5898244
  6.8 53.2 %all-to-all-start.1 = ((bf16[128,2,48,128]{3,2,1,0:T(8,128)(2,1)}), bf16[128,2,48,128]{3,2,1,0:T(8,128)(2,1)}, u32[]{:S(2)}, u32[]{:S(2)}) async-start(bf16[128,2,48,128]{3,2,1,0:T(8,128)(2,1)} %bitcast.56), calls=%async_computation.1 | async-start | bytes 6291456 | tf_op jit(solution)/shard_map/all_to_all | solution.py:55
  60.0 46.3 %all-to-all-start = ((bf16[128,2,48,128]{3,2,1,0:T(8,128)(2,1)}), bf16[128,2,48,128]{3,2,1,0:T(8,128)(2,1)S(1)}, u32[]{:S(2)}, u32[]{:S(2)}) async-start(bf16[128,2,48,128]{3,2,1,0:T(8,128)(2,1)} %bitcast), calls=%async_computation | async-start | bytes 6291456 | tf_op jit(solution)/shard_map/all_to_all | solution.py:55
  68.8 2.9 %copy-start.9 = (bf16[2,1536,512]{2,1,0:T(8,128)(2,1)S(1)}, bf16[2,1536,512]{2,1,0:T(8,128)(2,1)}, u32[]{:S(2)}) copy-start(bf16[2,1536,512]{2,1,0:T(8,128)(2,1)} %param.10) | copy-start | bytes 9437188
  71.5 1.4 copy-start.3
  71.5 1.7 copy-start.5
  106.3 1.7 copy-start.1
  119.7 5.7 %copy-start.6 = (bf16[128,1,48,128]{3,2,1,0:T(8,128)(2,1)S(1)}, bf16[128,1,48,128]{3,2,1,0:T(8,128)(2,1)}, u32[]{:S(2)}) copy-start(bf16[128,1,48,128]{3,2,1,0:T(8,128)(2,1)} %copy-done.5) | copy-start | bytes 4718596
  119.7 47.1 %all-to-all-start.2 = ((bf16[128,2,48,128]{3,2,1,0:T(8,128)(2,1)}), bf16[128,2,48,128]{3,2,1,0:T(8,128)(2,1)}, u32[]{:S(2)}, u32[]{:S(2)}) async-start(bf16[128,2,48,128]{3,2,1,0:T(8,128)(2,1)} %bitcast.58), calls=%async_computation.2 | async-start | bytes 6291456 | tf_op jit(solution)/shard_map/all_to_all | solution.py:55
  125.4 1.6 copy-start.4
  128.6 3.3 %copy-start.8 = (bf16[4,128,1536]{2,1,0:T(8,128)(2,1)S(1)}, bf16[4,128,1536]{2,1,0:T(8,128)(2,1)}, u32[]{:S(2)}) copy-start(bf16[4,128,1536]{2,1,0:T(8,128)(2,1)} %copy.21) | copy-start | bytes 4718596
  128.6 3.4 %copy-start.10 = (f32[2,512,512]{2,1,0:T(8,128)S(1)}, f32[2,512,512]{2,1,0:T(8,128)}, u32[]{:S(2)}) copy-start(f32[2,512,512]{2,1,0:T(8,128)} %param.8) | copy-start | bytes 6291460
  131.9 1.6 copy-start.2
  138.4 2.4 %copy-start.7 = (f32[2,512,512]{2,1,0:T(8,128)S(1)}, f32[2,512,512]{2,1,0:T(8,128)}, u32[]{:S(2)}) copy-start(f32[2,512,512]{2,1,0:T(8,128)} %get-tuple-element.16) | copy-start | bytes 6291460

commit v12 on v11

--- a/solution.py
+++ b/solution.py
@@ -2,6 +2,7 @@
 import jax.numpy as jnp
 from jax import lax
 from jax.experimental import pallas as pl
+from jax.experimental.pallas import tpu as pltpu
 from jax.sharding import PartitionSpec as P
 
 
@@ -17,23 +18,19 @@
     return iterate
 
 
-def _update_kernel(moms_ref, second_ref, basis_ref, out_ref):
+def _update_kernel(moms_ref, second_ref, basis_ref, basis_t_ref, out_ref, assembled):
     tensors, owners, piece_rows, piece_cols = moms_ref.shape
     full_rows = owners * piece_rows
-    basis = basis_ref[...]
-    moment_rot = None
     for t in range(tensors):
-        block = moms_ref[t].reshape(full_rows, piece_cols)
-        part = jnp.dot(block, basis[t * piece_cols:(t + 1) * piece_cols, :],
-                       preferred_element_type=jnp.float32)
-        moment_rot = part if moment_rot is None else moment_rot + part
+        assembled[:, t * piece_cols:(t + 1) * piece_cols] = moms_ref[t].reshape(full_rows, piece_cols)
+    moment_rot = jnp.dot(assembled[...], basis_ref[...], preferred_element_type=jnp.float32)
     scaled = (moment_rot / (jnp.sqrt(second_ref[...]) + 1e-06)).astype(jnp.bfloat16)
+    step = jnp.dot(scaled, basis_t_ref[...], preferred_element_type=jnp.float32).astype(out_ref.dtype)
     for t in range(tensors):
-        step = lax.dot_general(scaled, basis[t * piece_cols:(t + 1) * piece_cols, :],
-                               (((1,), (1,)), ((), ())), preferred_element_type=jnp.float32)
-        out_ref[t] = step.astype(out_ref.dtype).reshape(owners, piece_rows, piece_cols)
+        out_ref[t] = step[:, t * piece_cols:(t + 1) * piece_cols].reshape(owners, piece_rows, piece_cols)
 
-def update_pieces(moms, second_next, basis_b):
+
+def update_pieces(moms, second_next, basis_b, basis_t):
     tensors, owners, capacity, piece_rows, piece_cols = moms.shape
     full_rows, full_cols = second_next.shape[1:]
     block = pl.BlockSpec((tensors, owners, None, piece_rows, piece_cols), lambda c: (0, 0, c, 0, 0))
@@ -43,12 +40,14 @@
         grid=(capacity,),
         in_specs=[block,
                   pl.BlockSpec((None, full_rows, full_cols), lambda c: (c, 0, 0)),
+                  pl.BlockSpec((None, full_cols, full_cols), lambda c: (c, 0, 0)),
                   pl.BlockSpec((None, full_cols, full_cols), lambda c: (c, 0, 0))],
         out_specs=block,
+        scratch_shapes=[pltpu.VMEM((full_rows, full_cols), jnp.bfloat16)],
         cost_estimate=pl.CostEstimate(flops=4 * capacity * full_rows * full_cols * full_cols,
             transcendentals=capacity * full_rows * full_cols,
             bytes_accessed=capacity * (4 * full_rows * full_cols + 4 * full_rows * full_cols + 2 * full_cols * full_cols)),
-    )(moms, second_next, basis_b)
+    )(moms, second_next, basis_b, basis_t)
 
 
 def exchange(pieces):
@@ -99,11 +98,15 @@
             "tik,tkj->ij", grad_b, basis_rows, preferred_element_type=jnp.float32
         )
         second_list.append(0.95 * second[c].astype(jnp.float32) + 0.05 * rotated * rotated)
-    got_moms, second_next = lax.optimization_barrier((got_moms, jnp.stack(second_list)))
+    basis_t = jnp.swapaxes(basis_b, 1, 2)
+    got_moms, second_next, basis_t = lax.optimization_barrier(
+        (got_moms, jnp.stack(second_list), basis_t)
+    )
     step_pieces = update_pieces(
         got_moms.reshape(tensors, owners, capacity, piece_rows, piece_cols),
         second_next,
         basis_b,
+        basis_t,
     )
     returned = exchange(step_pieces.reshape(devices, capacity, piece_rows, piece_cols))
     owner_place = (owner_list % tensors) * owners + owner_list // tensors

time: 172 us -> 167 us (0.971)
  local copies, waits for them, and re-layouts: 23.2 us -> 27.2 us
  waiting for transfers between devices: 73.9 us -> 70.6 us
  Pallas kernels: 11.8 us -> 8.61 us
  other arithmetic: 18.5 us -> 15.8 us
    all_to_all x3, waiting for transfers between devices: 73.9 us -> 70.6 us  [exchange(): lax.all_to_all(pieces, ('tensor', 'owner'), split_axis=0, concat_axis=0,...]
    pallas_call x1, Pallas kernels: 11.8 us -> 8.61 us  [update_pieces(): pl.pallas_call(_update_kernel, out_shape=jax.ShapeDtypeStruct(moms.shape,...]
    convert_element_type x1 -> x0, other arithmetic: 2.7 us -> none  [local(): basis_b = bases.astype(jnp.bfloat16)]
    another operation x0 -> x2, local copies, waits for them, and re-layouts: none -> 2.51 us  [local(): basis_rows = basis_b[c].reshape(tensors, piece_cols, full_cols)]
    dot_general x2, local copies, waits for them, and re-layouts: 3.13 us -> 5.16 us  [local(): jnp.einsum('tik,sil->tksl', grad_b, grad_b, preferred_element_type=jnp.fl...]
    unnamed x22 -> x19, local copies, waits for them, and re-layouts: 3.46 us -> 1.84 us
  transfers between devices with their start and end apart: 3 -> 3, of which waited for: 3 -> 3; matrix products, arithmetic and copies ran while one was open for 28% -> 31% of each run, Pallas kernels for 0% -> 0%
where the time goes in v12:
time: 167 us
  waiting for transfers between devices  70.6 us (42%)
  local copies, waits for them, and re-layouts  27.2 us (16%)
  starting transfers between devices  23.1 us (14%)
  matrix products  20.7 us (12%)
  other arithmetic  15.8 us (9%)
  Pallas kernels  8.61 us (5%)
    all_to_all x3, waiting for transfers between devices, exchange(): lax.all_to_all(pieces, ('tensor', 'owner'), split_axis=0, concat_axis=0,...  70.6 us
    all_to_all x3, starting transfers between devices, exchange(): lax.all_to_all(pieces, ('tensor', 'owner'), split_axis=0, concat_axis=0,...  23.1 us
    dot_general x2, matrix products, refine(): jnp.einsum('cik,ckj->cij', iter_b, square, preferred_element_type=jnp.flo...  9.19 us
    pallas_call x1, Pallas kernels, update_pieces(): pl.pallas_call(_update_kernel, out_shape=jax.ShapeDtypeStruct(moms.shape,...  8.61 us
    convert_element_type x1, other arithmetic, local(): new_second = jnp.where(filled, second_next, 0.0).astype(jnp.bfloat16)  5.37 us
    dot_general x2, local copies, waits for them, and re-layouts, local(): jnp.einsum('tik,sil->tksl', grad_b, grad_b, preferred_element_type=jnp.fl...  5.16 us
    dot_general x1, matrix products, local(): jnp.einsum('cij,cjk->cik', stat_next, bases, precision=lax.Precision.HIGH...  4.84 us
    dot_general x2, matrix products, local(): jnp.einsum('tik,sil->tksl', grad_b, grad_b, preferred_element_type=jnp.fl...  4.35 us
  transfers between devices with their start and end apart: 3, of which 3 were waited for; matrix products, arithmetic and copies ran while one was open for 31% of the time, Pallas kernels for 0%

profile of v12, /device:TPU:1, one launch (start us, length us, event | category | flops | bytes accessed | tf_op | source)
XLA Modules:
  0.0 166.8 jit_solution(16151097833447465254)
XLA Ops:
  0.6 0.9 convert_reduce_fusion
  1.5 0.7 multiply_add_fusion
  2.2 0.1 select_reduce_fusion
  2.3 0.1 copy.31
  2.4 0.1 reshape.103
  2.6 4.2 %gather_fusion.1 = bf16[256,48,128]{2,1,0:T(8,128)(2,1)} fusion(bf16[160,48,128]{2,1,0:T(8,128)(2,1)} %param.6, s32[1024]{0:T(1024)S(1)} %pad_clamp_fusion.1), kind=kCustom, calls=%fused_computation.1 | custom fusion | bytes 6292480 | tf_op jit(solution)/shard_map/jit(_take)/gather | solution.py:77
  6.8 0.0 copy-start.1
  6.8 11.9 %all-to-all-start.1 = ((bf16[128,2,48,128]{3,2,1,0:T(8,128)(2,1)}), bf16[128,2,48,128]{3,2,1,0:T(8,128)(2,1)}, u32[]{:S(2)}, u32[]{:S(2)}) async-start(bf16[128,2,48,128]{3,2,1,0:T(8,128)(2,1)} %bitcast.59), calls=%async_computation.1 | async-start | bytes 6291456 | tf_op jit(solution)/shard_map/all_to_all | solution.py:54
  18.7 0.0 copy-done.1
  18.7 3.6 %add_convert_fusion = bf16[160,48,128]{2,1,0:T(8,128)(2,1)} fusion(bf16[160,48,128]{2,1,0:T(8,128)(2,1)S(1)} %copy-done.1, bf16[160,48,128]{2,1,0:T(8,128)(2,1)} %param.7), kind=kLoop, calls=%fused_computation.7 | loop fusion | flops 5898240 | bytes 5898240 | tf_op jit(solution)/shard_map/convert_element_type | solution.py:78
  22.3 4.2 %gather_fusion = bf16[256,48,128]{2,1,0:T(8,128)(2,1)} fusion(bf16[160,48,128]{2,1,0:T(8,128)(2,1)} %add_convert_fusion, s32[1024]{0:T(1024)S(1)} %pad_clamp_fusion.1), kind=kCustom, calls=%fused_computation | custom fusion | bytes 6292480 | tf_op jit(solution)/shard_map/jit(_take)/gather | solution.py:81
  26.4 33.5 %all-to-all-done.1 = bf16[128,2,48,128]{3,2,1,0:T(8,128)(2,1)} async-done(((bf16[128,2,48,128]{3,2,1,0:T(8,128)(2,1)}), bf16[128,2,48,128]{3,2,1,0:T(8,128)(2,1)}, u32[]{:S(2)}, u32[]{:S(2)}) %all-to-all-start.1) | async-done | bytes 3145760 | tf_op jit(solution)/shard_map/all_to_all | solution.py:54
  60.0 5.6 %all-to-all-start = ((bf16[128,2,48,128]{3,2,1,0:T(8,128)(2,1)}), bf16[128,2,48,128]{3,2,1,0:T(8,128)(2,1)}, u32[]{:S(2)}, u32[]{:S(2)}) async-start(bf16[128,2,48,128]{3,2,1,0:T(8,128)(2,1)} %bitcast), calls=%async_computation | async-start | bytes 6291456 | tf_op jit(solution)/shard_map/all_to_all | solution.py:54
  65.7 0.0 copy-done.2
  65.7 0.6 copy.32
  66.3 0.0 copy-start
  66.3 1.3 copy.35.basis_ref
  67.6 1.0 fusion.26
  68.6 0.0 copy-done
  68.6 1.3 copy.43
  69.9 1.3 copy.42
  71.2 0.2 compare_reduce_fusion
  71.4 2.6 %fusion.25 = (bf16[128,1,48,128]{3,2,1,0:T(8,128)(2,1)S(1)}, bf16[128,1,48,128]{3,2,1,0:T(8,128)(2,1)S(1)}) fusion(bf16[128,2,48,128]{3,2,1,0:T(8,128)(2,1)} %all-to-all-done.1), kind=kLoop, calls=%fused_computation.60 | loop fusion | bytes 6291456 | tf_op jit(solution)/shard_map/slice | solution.py:91
  74.0 0.0 copy-start.3
  74.0 0.0 copy-start.4
  74.0 0.2 copy-done.7
  74.2 1.1 fusion.1
  75.4 0.0 copy-done.3
  75.4 0.3 copy-done.4
  75.6 1.1 fusion.3
  76.8 3.4 %pad_maximum_fusion.second_ref = f32[2,1536,512]{2,1,0:T(8,128)} fusion(f32[1,1536,512]{2,1,0:T(8,128)S(1)} %fusion.1, f32[1,1536,512]{2,1,0:T(8,128)S(1)} %fusion.3), kind=kLoop, calls=%fused_computation.3 | loop fusion | flops 1572864 | bytes 12582912 | tf_op jit(solution)/shard_map/stack | solution.py:103
  80.2 26.9 %all-to-all-done = bf16[128,2,48,128]{3,2,1,0:T(8,128)(2,1)} async-done(((bf16[128,2,48,128]{3,2,1,0:T(8,128)(2,1)}), bf16[128,2,48,128]{3,2,1,0:T(8,128)(2,1)}, u32[]{:S(2)}, u32[]{:S(2)}) %all-to-all-start) | async-done | bytes 3145760 | tf_op jit(solution)/shard_map/all_to_all | solution.py:54
  107.1 8.6 %shard_map.101 = bf16[4,32,2,48,128]{4,3,2,1,0:T(8,128)(2,1)} custom-call(bf16[4,32,2,48,128]{4,3,2,1,0:T(8,128)(2,1)} %bitcast.13.moms_ref, f32[2,1536,512]{2,1,0:T(8,128)} %pad_maximum_fusion.second_ref, bf16[2,512,512]{2,1,0:T(8,128)(2,1)} %copy.35.basis_ref, bf16[2,512,512]{2,1,0:T(8,128)(2,1)} %bitcast.57), custom_call_target="tpu_custom_call" | custom-call | flops 3221225472 | bytes 13631488 | tf_op jit(solution)/shard_map/pallas_call | solution.py:37
  115.7 5.5 %all-to-all-start.2 = ((bf16[128,2,48,128]{3,2,1,0:T(8,128)(2,1)}), bf16[128,2,48,128]{3,2,1,0:T(8,128)(2,1)}, u32[]{:S(2)}, u32[]{:S(2)}) async-start(bf16[128,2,48,128]{3,2,1,0:T(8,128)(2,1)} %bitcast.58), calls=%async_computation.2 | async-start | bytes 6291456 | tf_op jit(solution)/shard_map/all_to_all | solution.py:54
  121.3 2.6 %copy.36 = bf16[4,128,1536]{2,1,0:T(8,128)(2,1)} copy(bf16[4,128,1536]{1,2,0:T(8,128)(2,1)} %bitcast.63) | data formatting | bytes 3145728 | tf_op jit(solution)/shard_map/tik,sil->tksl/dot_general | solution.py:93
  123.8 2.6 %copy.37 = bf16[4,128,1536]{2,1,0:T(8,128)(2,1)} copy(bf16[4,128,1536]{1,2,0:T(8,128)(2,1)} %bitcast.61) | data formatting | bytes 3145728 | tf_op jit(solution)/shard_map/tik,sil->tksl/dot_general | solution.py:93
  126.4 3.3 %fusion.11 = f32[1,512,512]{2,1,0:T(8,128)S(1)} fusion(bf16[512,1536]{1,0:T(8,128)(2,1)} %bitcast.64, f32[2,512,512]{2,1,0:T(8,128)} %param.8), kind=kOutput, calls=%fused_computation.27 | convolution fusion | flops 806092800 | bytes 5242880 | tf_op jit(solution)/shard_map/tik,sil->tksl/dot_general | solution.py:93
  129.8 0.0 copy-done.6
  129.8 0.0 copy-done.8
  129.8 1.0 fusion.13
  130.8 4.8 %multiply_reduce_fusion = (f32[2]{0:T(128)S(1)}, f32[2,512,512]{2,1,0:T(8,128)}) fusion(f32[2,512,512]{2,1,0:T(8,128)S(1)} %copy-done.2, f32[1,512,512]{2,1,0:T(8,128)S(1)} %fusion.13, f32[1,512,512]{2,1,0:T(8,128)S(1)} %fusion.11), kind=kOutput, calls=%fused_computation.17 | convolution fusion | flops 3222798336 | bytes 6291464 | tf_op jit(solution)/shard_map/cij,cjk->cik/dot_general | solution.py:119
  135.7 1.6 fusion.5
  137.3 0.7 copy-done.5
  138.0 2.8 %multiply_subtract_fusion = f32[2,512,512]{2,1,0:T(8,128)} fusion(f32[2,512,512]{2,1,0:T(8,128)S(1)} %copy-done.5, f32[2]{0:T(128)S(1)} %sqrt_multiply_fusion), kind=kOutput, calls=%fused_computation.16 | convolution fusion | flops 1078460416 | bytes 4194312 | tf_op jit(solution)/shard_map/cik,ckj->cij/dot_general | solution.py:15
  140.8 6.4 %subtract_select_fusion = f32[2,512,512]{2,1,0:T(8,128)} fusion(f32[2,512,512]{2,1,0:T(8,128)} %multiply_subtract_fusion, pred[2]{0:T(512)(128)(4,1)S(1)} %compare_reduce_fusion), kind=kOutput, calls=%fused_computation.15 | convolution fusion | flops 1077411840 | bytes 4194306 | tf_op jit(solution)/shard_map/cik,ckj->cij/dot_general | solution.py:15
  147.2 5.4 %select_convert_fusion = bf16[2,1536,512]{2,1,0:T(8,128)(2,1)} fusion(f32[2,1536,512]{2,1,0:T(8,128)} %pad_maximum_fusion.second_ref, pred[2]{0:T(512)(128)(4,1)S(1)} %compare_reduce_fusion), kind=kLoop, calls=%fused_computation.4 | loop fusion | flops 1572864 | bytes 9437186 | tf_op jit(solution)/shard_map/convert_element_type | solution.py:135
  152.6 10.1 %all-to-all-done.2 = bf16[128,2,48,128]{3,2,1,0:T(8,128)(2,1)} async-done(((bf16[128,2,48,128]{3,2,1,0:T(8,128)(2,1)}), bf16[128,2,48,128]{3,2,1,0:T(8,128)(2,1)}, u32[]{:S(2)}, u32[]{:S(2)}) %all-to-all-start.2) | async-done | bytes 3145760 | tf_op jit(solution)/shard_map/all_to_all | solution.py:54
  162.7 4.1 %gather_fusion.2 = bf16[160,48,128]{2,1,0:T(8,128)(2,1)} fusion(bf16[256,48,128]{2,1,0:T(8,128)(2,1)} %bitcast.15, s32[1024]{0:T(1024)S(1)} %pad_clamp_fusion), kind=kCustom, calls=%fused_computation.2 | custom fusion | bytes 3932800 | tf_op jit(solution)/shard_map/jit(_take)/gather | solution.py:113
  (11 shorter events, 0.0 us)
Async XLA Ops:
  6.8 11.9 %copy-start.1 = (bf16[160,48,128]{2,1,0:T(8,128)(2,1)S(1)}, bf16[160,48,128]{2,1,0:T(8,128)(2,1)}, u32[]{:S(2)}) copy-start(bf16[160,48,128]{2,1,0:T(8,128)(2,1)} %param.6) | copy-start | bytes 5898244
  6.8 53.2 %all-to-all-start.1 = ((bf16[128,2,48,128]{3,2,1,0:T(8,128)(2,1)}), bf16[128,2,48,128]{3,2,1,0:T(8,128)(2,1)}, u32[]{:S(2)}, u32[]{:S(2)}) async-start(bf16[128,2,48,128]{3,2,1,0:T(8,128)(2,1)} %bitcast.59), calls=%async_computation.1 | async-start | bytes 6291456 | tf_op jit(solution)/shard_map/all_to_all | solution.py:54
  60.0 5.7 %copy-start.2 = (f32[2,512,512]{2,1,0:T(8,128)S(1)}, f32[2,512,512]{2,1,0:T(8,128)}, u32[]{:S(2)}) copy-start(f32[2,512,512]{2,1,0:T(8,128)} %param.9) | copy-start | bytes 6291460
  60.0 47.1 %all-to-all-start = ((bf16[128,2,48,128]{3,2,1,0:T(8,128)(2,1)}), bf16[128,2,48,128]{3,2,1,0:T(8,128)(2,1)}, u32[]{:S(2)}, u32[]{:S(2)}) async-start(bf16[128,2,48,128]{3,2,1,0:T(8,128)(2,1)} %bitcast), calls=%async_computation | async-start | bytes 6291456 | tf_op jit(solution)/shard_map/all_to_all | solution.py:54
  66.3 2.4 %copy-start = (bf16[2,512,512]{1,2,0:T(8,128)(2,1)}, bf16[2,512,512]{1,2,0:T(8,128)(2,1)S(1)}, u32[]{:S(2)}) copy-start(bf16[2,512,512]{1,2,0:T(8,128)(2,1)S(1)} %copy.32) | copy-start | bytes 3145732
  71.4 2.9 %copy-start.7 = (bf16[2,1536,512]{2,1,0:T(8,128)(2,1)S(1)}, bf16[2,1536,512]{2,1,0:T(8,128)(2,1)}, u32[]{:S(2)}) copy-start(bf16[2,1536,512]{2,1,0:T(8,128)(2,1)} %param.10) | copy-start | bytes 9437188
  74.0 1.4 copy-start.3
  74.0 1.7 copy-start.4
  115.7 47.0 %all-to-all-start.2 = ((bf16[128,2,48,128]{3,2,1,0:T(8,128)(2,1)}), bf16[128,2,48,128]{3,2,1,0:T(8,128)(2,1)}, u32[]{:S(2)}, u32[]{:S(2)}) async-start(bf16[128,2,48,128]{3,2,1,0:T(8,128)(2,1)} %bitcast.58), calls=%async_computation.2 | async-start | bytes 6291456 | tf_op jit(solution)/shard_map/all_to_all | solution.py:54
  126.4 3.3 %copy-start.6 = (bf16[4,128,1536]{2,1,0:T(8,128)(2,1)S(1)}, bf16[4,128,1536]{2,1,0:T(8,128)(2,1)}, u32[]{:S(2)}) copy-start(bf16[4,128,1536]{2,1,0:T(8,128)(2,1)} %copy.37) | copy-start | bytes 4718596
  126.4 3.4 %copy-start.8 = (f32[2,512,512]{2,1,0:T(8,128)S(1)}, f32[2,512,512]{2,1,0:T(8,128)}, u32[]{:S(2)}) copy-start(f32[2,512,512]{2,1,0:T(8,128)} %param.8) | copy-start | bytes 6291460
  135.7 2.4 %copy-start.5 = (f32[2,512,512]{2,1,0:T(8,128)S(1)}, f32[2,512,512]{2,1,0:T(8,128)}, u32[]{:S(2)}) copy-start(f32[2,512,512]{2,1,0:T(8,128)} %get-tuple-element.18) | copy-start | bytes 6291460

commit v13 on v12

--- a/solution.py
+++ b/solution.py
@@ -44,6 +44,7 @@
                   pl.BlockSpec((None, full_cols, full_cols), lambda c: (c, 0, 0))],
         out_specs=block,
         scratch_shapes=[pltpu.VMEM((full_rows, full_cols), jnp.bfloat16)],
+        compiler_params=pltpu.CompilerParams(vmem_limit_bytes=24 * 1024 * 1024),
         cost_estimate=pl.CostEstimate(flops=4 * capacity * full_rows * full_cols * full_cols,
             transcendentals=capacity * full_rows * full_cols,
             bytes_accessed=capacity * (4 * full_rows * full_cols + 4 * full_rows * full_cols + 2 * full_cols * full_cols)),

time: 167 us -> 167 us (level)
  matrix products: 20.7 us -> 24.3 us
  Pallas kernels: 8.61 us -> 6.32 us
    unnamed x19 -> x23, local copies, waits for them, and re-layouts: 1.84 us -> 6.15 us
    dot_general x2, matrix products: 9.19 us -> 12.8 us  [refine(): jnp.einsum('cik,ckj->cij', iter_b, square, preferred_element_type=jnp.flo...]
    pallas_call x1, Pallas kernels: 8.61 us -> 6.32 us  [update_pieces(): pl.pallas_call(_update_kernel, out_shape=jax.ShapeDtypeStruct(moms.shape,...]
    gather x1, local copies, waits for them, and re-layouts: 4.09 us -> 2.2 us  [local(): jnp.take(returned.reshape(devices * capacity, piece_rows, piece_cols), ow...]
  transfers between devices with their start and end apart: 3 -> 3, of which waited for: 3 -> 3; matrix products, arithmetic and copies ran while one was open for 31% -> 32% of each run, Pallas kernels for 0% -> 0%
where the time goes in v13:
time: 167 us; the launch traced here: 166 us
  waiting for transfers between devices  70.3 us (42%)
  local copies, waits for them, and re-layouts  26.6 us (16%)
  matrix products  24.3 us (15%)
  starting transfers between devices  22.2 us (13%)
  other arithmetic  15.8 us (9%)
  Pallas kernels  6.32 us (4%)
    all_to_all x3, waiting for transfers between devices, exchange(): lax.all_to_all(pieces, ('tensor', 'owner'), split_axis=0, concat_axis=0,...  70.3 us
    all_to_all x3, starting transfers between devices, exchange(): lax.all_to_all(pieces, ('tensor', 'owner'), split_axis=0, concat_axis=0,...  22.2 us
    dot_general x2, matrix products, refine(): jnp.einsum('cik,ckj->cij', iter_b, square, preferred_element_type=jnp.flo...  12.8 us
    pallas_call x1, Pallas kernels, update_pieces(): pl.pallas_call(_update_kernel, out_shape=jax.ShapeDtypeStruct(moms.shape,...  6.32 us
    unnamed x23, local copies, waits for them, and re-layouts  6.15 us
    convert_element_type x1, other arithmetic, local(): new_second = jnp.where(filled, second_next, 0.0).astype(jnp.bfloat16)  5.37 us
    dot_general x2, local copies, waits for them, and re-layouts, local(): jnp.einsum('tik,sil->tksl', grad_b, grad_b, preferred_element_type=jnp.fl...  5.16 us
    dot_general x1, matrix products, local(): jnp.einsum('cij,cjk->cik', stat_next, bases, precision=lax.Precision.HIGH...  4.84 us
  transfers between devices with their start and end apart: 3, of which 3 were waited for; matrix products, arithmetic and copies ran while one was open for 32% of the time, Pallas kernels for 0%

profile of v13, /device:TPU:1, one launch (start us, length us, event | category | flops | bytes accessed | tf_op | source)
XLA Modules:
  0.0 166.4 jit_solution(16479862318194287970)
XLA Ops:
  0.6 0.9 convert_reduce_fusion
  1.5 0.7 multiply_add_fusion
  2.2 0.1 select_reduce_fusion
  2.3 0.1 copy.31
  2.4 0.1 reshape.103
  2.6 4.2 %gather_fusion.1 = bf16[256,48,128]{2,1,0:T(8,128)(2,1)} fusion(bf16[160,48,128]{2,1,0:T(8,128)(2,1)} %param.6, s32[1024]{0:T(1024)S(1)} %pad_clamp_fusion.1), kind=kCustom, calls=%fused_computation.1 | custom fusion | bytes 6292480 | tf_op jit(solution)/shard_map/jit(_take)/gather | solution.py:78
  6.8 11.9 %all-to-all-start.1 = ((bf16[128,2,48,128]{3,2,1,0:T(8,128)(2,1)}), bf16[128,2,48,128]{3,2,1,0:T(8,128)(2,1)}, u32[]{:S(2)}, u32[]{:S(2)}) async-start(bf16[128,2,48,128]{3,2,1,0:T(8,128)(2,1)} %bitcast.59), calls=%async_computation.1 | async-start | bytes 6291456 | tf_op jit(solution)/shard_map/all_to_all | solution.py:55
  18.7 0.0 copy-done.2
  18.7 3.6 %add_convert_fusion = bf16[160,48,128]{2,1,0:T(8,128)(2,1)} fusion(bf16[160,48,128]{2,1,0:T(8,128)(2,1)S(1)} %copy-done.2, bf16[160,48,128]{2,1,0:T(8,128)(2,1)} %param.7), kind=kLoop, calls=%fused_computation.7 | loop fusion | flops 5898240 | bytes 5898240 | tf_op jit(solution)/shard_map/convert_element_type | solution.py:79
  22.3 4.2 %gather_fusion = bf16[256,48,128]{2,1,0:T(8,128)(2,1)} fusion(bf16[160,48,128]{2,1,0:T(8,128)(2,1)} %add_convert_fusion, s32[1024]{0:T(1024)S(1)} %pad_clamp_fusion.1), kind=kCustom, calls=%fused_computation | custom fusion | bytes 6292480 | tf_op jit(solution)/shard_map/jit(_take)/gather | solution.py:82
  26.5 33.5 %all-to-all-done.1 = bf16[128,2,48,128]{3,2,1,0:T(8,128)(2,1)} async-done(((bf16[128,2,48,128]{3,2,1,0:T(8,128)(2,1)}), bf16[128,2,48,128]{3,2,1,0:T(8,128)(2,1)}, u32[]{:S(2)}, u32[]{:S(2)}) %all-to-all-start.1) | async-done | bytes 3145760 | tf_op jit(solution)/shard_map/all_to_all | solution.py:55
  60.0 5.6 %all-to-all-start = ((bf16[128,2,48,128]{3,2,1,0:T(8,128)(2,1)}), bf16[128,2,48,128]{3,2,1,0:T(8,128)(2,1)}, u32[]{:S(2)}, u32[]{:S(2)}) async-start(bf16[128,2,48,128]{3,2,1,0:T(8,128)(2,1)} %bitcast), calls=%async_computation | async-start | bytes 6291456 | tf_op jit(solution)/shard_map/all_to_all | solution.py:55
  65.7 0.0 copy-done.3
  65.7 0.6 copy.32
  66.3 0.5 copy.35.basis_ref
  66.8 0.1 fusion.26
  66.9 1.0 copy.43
  67.9 0.2 copy.42
  68.2 0.2 compare_reduce_fusion
  68.4 0.0 copy-start.9
  68.4 2.6 %fusion.25 = (bf16[128,1,48,128]{3,2,1,0:T(8,128)(2,1)S(1)}, bf16[128,1,48,128]{3,2,1,0:T(8,128)(2,1)S(1)}) fusion(bf16[128,2,48,128]{3,2,1,0:T(8,128)(2,1)} %all-to-all-done.1), kind=kLoop, calls=%fused_computation.60 | loop fusion | bytes 6291456 | tf_op jit(solution)/shard_map/slice | solution.py:92
  71.0 0.0 copy-start.5
  71.0 0.0 copy-start.6
  71.0 0.0 copy-done.8
  71.0 0.4 copy-done.9
  71.4 1.1 fusion.1
  72.5 0.0 copy-done.5
  72.5 0.1 copy-done.6
  72.6 1.1 fusion.3
  73.8 3.4 %pad_maximum_fusion.second_ref = f32[2,1536,512]{2,1,0:T(8,128)} fusion(f32[1,1536,512]{2,1,0:T(8,128)S(1)} %fusion.1, f32[1,1536,512]{2,1,0:T(8,128)S(1)} %fusion.3), kind=kLoop, calls=%fused_computation.3 | loop fusion | flops 1572864 | bytes 12582912 | tf_op jit(solution)/shard_map/stack | solution.py:104
  77.2 30.0 %all-to-all-done = bf16[128,2,48,128]{3,2,1,0:T(8,128)(2,1)} async-done(((bf16[128,2,48,128]{3,2,1,0:T(8,128)(2,1)}), bf16[128,2,48,128]{3,2,1,0:T(8,128)(2,1)}, u32[]{:S(2)}, u32[]{:S(2)}) %all-to-all-start) | async-done | bytes 3145760 | tf_op jit(solution)/shard_map/all_to_all | solution.py:55
  107.1 2.8 %copy-done = f32[2,1536,512]{2,1,0:T(8,128)S(1)} copy-done((f32[2,1536,512]{2,1,0:T(8,128)S(1)}, f32[2,1536,512]{2,1,0:T(8,128)}, u32[]{:S(2)}) %copy-start) | copy-done | bytes 6291480
  109.9 6.3 %shard_map.101 = bf16[4,32,2,48,128]{4,3,2,1,0:T(8,128)(2,1)S(1)} custom-call(bf16[4,32,2,48,128]{4,3,2,1,0:T(8,128)(2,1)} %bitcast.13.moms_ref, f32[2,1536,512]{2,1,0:T(8,128)S(1)} %copy-done, bf16[2,512,512]{2,1,0:T(8,128)(2,1)S(1)} %copy.35.basis_ref, bf16[2,512,512]{2,1,0:T(8,128)(2,1)S(1)} %bitcast.57), custom_call_target="tpu_custom_call" | custom-call | flops 3221225472 | bytes 13631488 | tf_op jit(solution)/shard_map/pallas_call | solution.py:37
  116.2 1.7 %copy-done.1 = bf16[4,32,2,48,128]{4,3,2,1,0:T(8,128)(2,1)} copy-done((bf16[4,32,2,48,128]{4,3,2,1,0:T(8,128)(2,1)}, bf16[4,32,2,48,128]{4,3,2,1,0:T(8,128)(2,1)S(1)}, u32[]{:S(2)}) %copy-start.1) | copy-done | bytes 3145752
  117.9 4.7 %all-to-all-start.2 = ((bf16[128,2,48,128]{3,2,1,0:T(8,128)(2,1)}), bf16[128,2,48,128]{3,2,1,0:T(8,128)(2,1)S(1)}, u32[]{:S(2)}, u32[]{:S(2)}) async-start(bf16[128,2,48,128]{3,2,1,0:T(8,128)(2,1)} %bitcast.58), calls=%async_computation.2 | async-start | bytes 6291456 | tf_op jit(solution)/shard_map/all_to_all | solution.py:55
  122.6 2.6 %copy.36 = bf16[4,128,1536]{2,1,0:T(8,128)(2,1)} copy(bf16[4,128,1536]{1,2,0:T(8,128)(2,1)} %bitcast.64) | data formatting | bytes 3145728 | tf_op jit(solution)/shard_map/tik,sil->tksl/dot_general | solution.py:94
  125.2 2.6 %copy.37 = bf16[4,128,1536]{2,1,0:T(8,128)(2,1)} copy(bf16[4,128,1536]{1,2,0:T(8,128)(2,1)} %bitcast.62) | data formatting | bytes 3145728 | tf_op jit(solution)/shard_map/tik,sil->tksl/dot_general | solution.py:94
  127.8 3.3 %fusion.11 = f32[1,512,512]{2,1,0:T(8,128)S(1)} fusion(bf16[512,1536]{1,0:T(8,128)(2,1)} %bitcast.65, f32[2,512,512]{2,1,0:T(8,128)} %param.8), kind=kOutput, calls=%fused_computation.27 | convolution fusion | flops 806092800 | bytes 5242880 | tf_op jit(solution)/shard_map/tik,sil->tksl/dot_general | solution.py:94
  131.1 0.0 copy-start.4
  131.1 1.0 fusion.13
  132.2 0.6 copy-done.4
  132.7 4.8 %multiply_reduce_fusion = (f32[2]{0:T(128)S(1)}, f32[2,512,512]{2,1,0:T(8,128)}) fusion(f32[2,512,512]{2,1,0:T(8,128)S(1)} %copy-done.4, f32[1,512,512]{2,1,0:T(8,128)S(1)} %fusion.13, f32[1,512,512]{2,1,0:T(8,128)S(1)} %fusion.11), kind=kOutput, calls=%fused_computation.17 | convolution fusion | flops 3222798336 | bytes 6291464 | tf_op jit(solution)/shard_map/cij,cjk->cik/dot_general | solution.py:120
  137.6 1.6 fusion.5
  139.2 6.5 %multiply_subtract_fusion = f32[2,512,512]{2,1,0:T(8,128)} fusion(f32[2,512,512]{2,1,0:T(8,128)} %get-tuple-element.18, f32[2]{0:T(128)S(1)} %sqrt_multiply_fusion), kind=kOutput, calls=%fused_computation.16 | convolution fusion | flops 1078460416 | bytes 4194312 | tf_op jit(solution)/shard_map/cik,ckj->cij/dot_general | solution.py:15
  145.7 6.3 %subtract_select_fusion = f32[2,512,512]{2,1,0:T(8,128)} fusion(f32[2,512,512]{2,1,0:T(8,128)} %multiply_subtract_fusion, pred[2]{0:T(512)(128)(4,1)S(1)} %compare_reduce_fusion), kind=kOutput, calls=%fused_computation.15 | convolution fusion | flops 1077411840 | bytes 4194306 | tf_op jit(solution)/shard_map/cik,ckj->cij/dot_general | solution.py:15
  152.0 5.4 %select_convert_fusion = bf16[2,1536,512]{2,1,0:T(8,128)(2,1)} fusion(f32[2,1536,512]{2,1,0:T(8,128)} %pad_maximum_fusion.second_ref, pred[2]{0:T(512)(128)(4,1)S(1)} %compare_reduce_fusion), kind=kLoop, calls=%fused_computation.4 | loop fusion | flops 1572864 | bytes 9437186 | tf_op jit(solution)/shard_map/convert_element_type | solution.py:136
  157.4 6.8 %all-to-all-done.2 = bf16[128,2,48,128]{3,2,1,0:T(8,128)(2,1)S(1)} async-done(((bf16[128,2,48,128]{3,2,1,0:T(8,128)(2,1)}), bf16[128,2,48,128]{3,2,1,0:T(8,128)(2,1)S(1)}, u32[]{:S(2)}, u32[]{:S(2)}) %all-to-all-start.2) | async-done | bytes 3145760 | tf_op jit(solution)/shard_map/all_to_all | solution.py:55
  164.2 2.2 %gather_fusion.2 = bf16[160,48,128]{2,1,0:T(8,128)(2,1)} fusion(bf16[256,48,128]{2,1,0:T(8,128)(2,1)S(1)} %bitcast.60, s32[1024]{0:T(1024)S(1)} %pad_clamp_fusion), kind=kCustom, calls=%fused_computation.2 | custom fusion | bytes 3932800 | tf_op jit(solution)/shard_map/jit(_take)/gather | solution.py:114
  (15 shorter events, 0.1 us)
Async XLA Ops:
  6.8 11.9 %copy-start.2 = (bf16[160,48,128]{2,1,0:T(8,128)(2,1)S(1)}, bf16[160,48,128]{2,1,0:T(8,128)(2,1)}, u32[]{:S(2)}) copy-start(bf16[160,48,128]{2,1,0:T(8,128)(2,1)} %param.6) | copy-start | bytes 5898244
  6.8 53.2 %all-to-all-start.1 = ((bf16[128,2,48,128]{3,2,1,0:T(8,128)(2,1)}), bf16[128,2,48,128]{3,2,1,0:T(8,128)(2,1)}, u32[]{:S(2)}, u32[]{:S(2)}) async-start(bf16[128,2,48,128]{3,2,1,0:T(8,128)(2,1)} %bitcast.59), calls=%async_computation.1 | async-start | bytes 6291456 | tf_op jit(solution)/shard_map/all_to_all | solution.py:55
  60.0 5.7 %copy-start.3 = (f32[2,512,512]{2,1,0:T(8,128)S(1)}, f32[2,512,512]{2,1,0:T(8,128)}, u32[]{:S(2)}) copy-start(f32[2,512,512]{2,1,0:T(8,128)} %param.9) | copy-start | bytes 6291460
  60.0 47.1 %all-to-all-start = ((bf16[128,2,48,128]{3,2,1,0:T(8,128)(2,1)}), bf16[128,2,48,128]{3,2,1,0:T(8,128)(2,1)}, u32[]{:S(2)}, u32[]{:S(2)}) async-start(bf16[128,2,48,128]{3,2,1,0:T(8,128)(2,1)} %bitcast), calls=%async_computation | async-start | bytes 6291456 | tf_op jit(solution)/shard_map/all_to_all | solution.py:55
  68.4 2.6 %copy-start.8 = (bf16[1,512,512]{2,1,0:T(8,128)(2,1)S(1)}, bf16[1,512,512]{2,1,0:T(8,128)(2,1)}, u32[]{:S(2)}) copy-start(bf16[1,512,512]{2,1,0:T(8,128)(2,1)} %copy.43) | copy-start | bytes 1572868
  68.4 3.0 %copy-start.9 = (bf16[2,1536,512]{2,1,0:T(8,128)(2,1)S(1)}, bf16[2,1536,512]{2,1,0:T(8,128)(2,1)}, u32[]{:S(2)}) copy-start(bf16[2,1536,512]{2,1,0:T(8,128)(2,1)} %param.10) | copy-start | bytes 9437188
  71.0 1.6 copy-start.5
  71.0 1.7 copy-start.6
  107.1 2.8 %copy-start = (f32[2,1536,512]{2,1,0:T(8,128)S(1)}, f32[2,1536,512]{2,1,0:T(8,128)}, u32[]{:S(2)}) copy-start(f32[2,1536,512]{2,1,0:T(8,128)} %pad_maximum_fusion.second_ref) | copy-start | bytes 18874372
  116.2 1.7 %copy-start.1 = (bf16[4,32,2,48,128]{4,3,2,1,0:T(8,128)(2,1)}, bf16[4,32,2,48,128]{4,3,2,1,0:T(8,128)(2,1)S(1)}, u32[]{:S(2)}) copy-start(bf16[4,32,2,48,128]{4,3,2,1,0:T(8,128)(2,1)S(1)} %shard_map.101) | copy-start | bytes 9437188
  117.9 46.3 %all-to-all-start.2 = ((bf16[128,2,48,128]{3,2,1,0:T(8,128)(2,1)}), bf16[128,2,48,128]{3,2,1,0:T(8,128)(2,1)S(1)}, u32[]{:S(2)}, u32[]{:S(2)}) async-start(bf16[128,2,48,128]{3,2,1,0:T(8,128)(2,1)} %bitcast.58), calls=%async_computation.2 | async-start | bytes 6291456 | tf_op jit(solution)/shard_map/all_to_all | solution.py:55
  127.8 3.3 %copy-start.7 = (bf16[4,128,1536]{2,1,0:T(8,128)(2,1)S(1)}, bf16[4,128,1536]{2,1,0:T(8,128)(2,1)}, u32[]{:S(2)}) copy-start(bf16[4,128,1536]{2,1,0:T(8,128)(2,1)} %copy.37) | copy-start | bytes 4718596
  127.8 3.4 %copy-start.10 = (f32[2,512,512]{2,1,0:T(8,128)S(1)}, f32[2,512,512]{2,1,0:T(8,128)}, u32[]{:S(2)}) copy-start(f32[2,512,512]{2,1,0:T(8,128)} %param.8) | copy-start | bytes 6291460
  131.1 1.6 copy-start.4

commit v14 on v5

--- a/solution.py
+++ b/solution.py
@@ -36,9 +36,14 @@
     slot_id = owner_list * capacity + position
     place = jnp.arange(devices, dtype=jnp.int32)
     device_at = (place % owners) * tensors + place // owners
-    targets = device_at[:, None] * capacity + jnp.arange(capacity, dtype=jnp.int32)[None, :]
-    hit = targets[:, :, None] == slot_id[None, None, :]
-    which = jnp.sum(jnp.where(hit, matrix_ids[None, None, :], 0), axis=2)
+    owned = device_at[:, None] == owner_list[None, :]
+    which = jnp.stack(
+        [
+            jnp.min(jnp.where(owned, matrix_ids[None, :], matrices - 1), axis=1),
+            jnp.max(jnp.where(owned, matrix_ids[None, :], 0), axis=1),
+        ],
+        axis=1,
+    )
 
     got_grads = exchange(jnp.take(gradients, which, axis=0, mode="clip"))
     new_moments = (0.9 * moments.astype(jnp.float32) + 0.1 * gradients.astype(jnp.float32)).astype(

time: 166 us -> 165 us (level)
  no operation moved by 1% of the time
where the time goes in v14:
time: 165 us; the launch traced here: 164 us
  waiting for transfers between devices  66.3 us (40%)
  matrix products  36.1 us (22%)
  local copies, waits for them, and re-layouts  23.4 us (14%)
  starting transfers between devices  21.2 us (13%)
  other arithmetic  16.4 us (10%)
    all_to_all x3, waiting for transfers between devices, exchange(): lax.all_to_all(pieces, ('tensor', 'owner'), split_axis=0, concat_axis=0,...  66.3 us
    all_to_all x3, starting transfers between devices, exchange(): lax.all_to_all(pieces, ('tensor', 'owner'), split_axis=0, concat_axis=0,...  21.2 us
    dot_general x2, matrix products, refine(): jnp.einsum('cik,ckj->cij', iter_b, square, preferred_element_type=jnp.flo...  12.8 us
    dot_general x2, matrix products, local(): jnp.einsum('tik,sil->tksl', grad_b, grad_b, preferred_element_type=jnp.fl...  7.51 us
    dot_general x2, matrix products, local(): jnp.einsum('tik,tkj->ij', grad_b, basis_rows, preferred_element_type=jnp....  5.6 us
    convert_element_type x1, other arithmetic, local(): new_second = jnp.where(filled, second_next, 0.0).astype(jnp.bfloat16)  5.43 us
    dot_general x2, local copies, waits for them, and re-layouts, local(): jnp.einsum('tik,sil->tksl', grad_b, grad_b, preferred_element_type=jnp.fl...  5.16 us
    dot_general x1, matrix products, local(): jnp.einsum('cij,cjk->cik', stat_next, bases, precision=lax.Precision.HIGH...  4.84 us
  transfers between devices with their start and end apart: 3, of which 3 were waited for; matrix products, arithmetic and copies ran while one was open for 35% of the time, Pallas kernels for 0%

profile of v14, /device:TPU:1, one launch (start us, length us, event | category | flops | bytes accessed | tf_op | source)
XLA Modules:
  0.0 164.3 jit_solution(15794888246530902614)
XLA Ops:
  0.6 0.8 fusion.20
  1.4 0.1 copy.33
  1.6 0.1 reshape.72
  1.7 4.2 %gather_fusion.1 = bf16[256,48,128]{2,1,0:T(8,128)(2,1)} fusion(bf16[160,48,128]{2,1,0:T(8,128)(2,1)} %param.6, s32[1024]{0:T(1024)S(1)} %pad_clamp_fusion.1), kind=kCustom, calls=%fused_computation.1 | custom fusion | bytes 6292480 | tf_op jit(solution)/shard_map/jit(_take)/gather | solution.py:48
  5.9 11.9 %all-to-all-start.1 = ((bf16[128,2,48,128]{3,2,1,0:T(8,128)(2,1)}), bf16[128,2,48,128]{3,2,1,0:T(8,128)(2,1)}, u32[]{:S(2)}, u32[]{:S(2)}) async-start(bf16[128,2,48,128]{3,2,1,0:T(8,128)(2,1)} %bitcast.83), calls=%async_computation.1 | async-start | bytes 6291456 | tf_op jit(solution)/shard_map/all_to_all | solution.py:20
  17.8 0.0 copy-done
  17.8 3.6 %add_convert_fusion = bf16[160,48,128]{2,1,0:T(8,128)(2,1)} fusion(bf16[160,48,128]{2,1,0:T(8,128)(2,1)S(1)} %copy-done, bf16[160,48,128]{2,1,0:T(8,128)(2,1)} %param.7), kind=kLoop, calls=%fused_computation.7 | loop fusion | flops 5898240 | bytes 5898240 | tf_op jit(solution)/shard_map/convert_element_type | solution.py:49
  21.4 4.2 %gather_fusion = bf16[256,48,128]{2,1,0:T(8,128)(2,1)} fusion(bf16[160,48,128]{2,1,0:T(8,128)(2,1)} %add_convert_fusion, s32[1024]{0:T(1024)S(1)} %pad_clamp_fusion.1), kind=kCustom, calls=%fused_computation | custom fusion | bytes 6292480 | tf_op jit(solution)/shard_map/jit(_take)/gather | solution.py:52
  25.6 33.5 %all-to-all-done.1 = bf16[128,2,48,128]{3,2,1,0:T(8,128)(2,1)} async-done(((bf16[128,2,48,128]{3,2,1,0:T(8,128)(2,1)}), bf16[128,2,48,128]{3,2,1,0:T(8,128)(2,1)}, u32[]{:S(2)}, u32[]{:S(2)}) %all-to-all-start.1) | async-done | bytes 3145760 | tf_op jit(solution)/shard_map/all_to_all | solution.py:20
  59.1 4.7 %all-to-all-start = ((bf16[128,2,48,128]{3,2,1,0:T(8,128)(2,1)}), bf16[128,2,48,128]{3,2,1,0:T(8,128)(2,1)S(1)}, u32[]{:S(2)}, u32[]{:S(2)}) async-start(bf16[128,2,48,128]{3,2,1,0:T(8,128)(2,1)} %bitcast.82), calls=%async_computation | async-start | bytes 6291456 | tf_op jit(solution)/shard_map/all_to_all | solution.py:20
  63.8 0.0 copy-start.11
  63.8 2.7 %convert_element_type.60 = bf16[2,512,512]{2,1,0:T(8,128)(2,1)} convert(f32[2,512,512]{2,1,0:T(8,128)} %param.9) | non-fusion elementwise | flops 524288 | bytes 3145728 | tf_op jit(solution)/shard_map/convert_element_type | solution.py:59
  66.5 0.1 convert_reduce_fusion
  66.6 0.2 compare_reduce_fusion
  66.8 1.3 fusion.29
  68.1 0.0 copy-start.7
  68.1 0.0 copy-start.9
  68.1 0.0 copy-start.12
  68.1 2.9 %fusion.28 = (bf16[128,1,48,128]{3,2,1,0:T(8,128)(2,1)S(1)}, bf16[128,1,48,128]{3,2,1,0:T(8,128)(2,1)S(1)}) fusion(bf16[128,2,48,128]{3,2,1,0:T(8,128)(2,1)} %all-to-all-done.1), kind=kLoop, calls=%fused_computation.70 | loop fusion | bytes 6291456 | tf_op jit(solution)/shard_map/slice | solution.py:62
  71.0 0.0 copy-start.2
  71.0 0.0 copy-start.3
  71.0 0.3 copy-done.12
  71.3 2.8 %fusion.2 = f32[1536,512]{1,0:T(8,128)} fusion(bf16[4,1536,128]{2,1,0:T(8,128)(2,1)S(1)} %bitcast.85, bf16[4,128,512]{2,1,0:T(8,128)(2,1)S(1)} %bitcast.97, bf16[2,1536,512]{2,1,0:T(8,128)(2,1)S(1)} %copy-done.12), kind=kOutput, calls=%fused_computation.13 | convolution fusion | flops 809238528 | bytes 6815744 | tf_op jit(solution)/shard_map/tik,tkj->ij/dot_general | solution.py:68
  74.2 2.8 %fusion.1 = f32[1536,512]{1,0:T(8,128)} fusion(bf16[4,1536,128]{2,1,0:T(8,128)(2,1)S(1)} %bitcast.87, bf16[4,128,512]{2,1,0:T(8,128)(2,1)S(1)} %bitcast.100, bf16[2,1536,512]{2,1,0:T(8,128)(2,1)S(1)} %copy-done.12), kind=kOutput, calls=%fused_computation.11 | convolution fusion | flops 809238528 | bytes 6815744 | tf_op jit(solution)/shard_map/tik,tkj->ij/dot_general | solution.py:68
  76.9 28.4 %all-to-all-done = bf16[128,2,48,128]{3,2,1,0:T(8,128)(2,1)S(1)} async-done(((bf16[128,2,48,128]{3,2,1,0:T(8,128)(2,1)}), bf16[128,2,48,128]{3,2,1,0:T(8,128)(2,1)S(1)}, u32[]{:S(2)}, u32[]{:S(2)}) %all-to-all-start) | async-done | bytes 3145760 | tf_op jit(solution)/shard_map/all_to_all | solution.py:20
  105.4 0.5 fusion.27
  105.9 1.3 copy-done.6
  107.3 0.1 copy-done.10
  107.4 1.6 divide_convert_fusion
  109.0 0.0 copy-start.8
  109.0 1.0 convolution_convert_fusion
  110.1 0.8 copy-done.5
  110.9 0.1 copy-done.8
  111.0 1.6 divide_convert_fusion.1
  112.6 1.0 convolution_convert_fusion.1
  113.7 2.0 %pad_maximum_fusion = bf16[128,2,48,128]{3,2,1,0:T(8,128)(2,1)} fusion(bf16[128,1,48,128]{3,2,1,0:T(8,128)(2,1)S(1)} %bitcast.93, bf16[128,1,48,128]{3,2,1,0:T(8,128)(2,1)S(1)} %bitcast.96), kind=kLoop, calls=%fused_computation.14 | loop fusion | flops 1572864 | bytes 6291456 | tf_op jit(solution)/shard_map/stack | solution.py:86
  115.6 4.7 %all-to-all-start.2 = ((bf16[128,2,48,128]{3,2,1,0:T(8,128)(2,1)}), bf16[128,2,48,128]{3,2,1,0:T(8,128)(2,1)S(1)}, u32[]{:S(2)}, u32[]{:S(2)}) async-start(bf16[128,2,48,128]{3,2,1,0:T(8,128)(2,1)} %pad_maximum_fusion), calls=%async_computation.2 | async-start | bytes 6291456 | tf_op jit(solution)/shard_map/all_to_all | solution.py:20
  120.3 2.6 %copy.37 = bf16[4,128,1536]{2,1,0:T(8,128)(2,1)} copy(bf16[4,128,1536]{1,2,0:T(8,128)(2,1)} %bitcast.88) | data formatting | bytes 3145728 | tf_op jit(solution)/shard_map/tik,sil->tksl/dot_general | solution.py:64
  122.9 4.2 %fusion.14 = f32[1,512,512]{2,1,0:T(8,128)} fusion(bf16[512,1536]{1,0:T(8,128)(2,1)} %bitcast.91, f32[2,512,512]{2,1,0:T(8,128)} %param.8), kind=kOutput, calls=%fused_computation.36 | convolution fusion | flops 806092800 | bytes 5242880 | tf_op jit(solution)/shard_map/tik,sil->tksl/dot_general | solution.py:64
  127.1 2.6 %copy.36 = bf16[4,128,1536]{2,1,0:T(8,128)(2,1)} copy(bf16[4,128,1536]{1,2,0:T(8,128)(2,1)} %bitcast.86) | data formatting | bytes 3145728 | tf_op jit(solution)/shard_map/tik,sil->tksl/dot_general | solution.py:64
  129.6 3.3 %fusion.12 = f32[1,512,512]{2,1,0:T(8,128)S(1)} fusion(bf16[512,1536]{1,0:T(8,128)(2,1)} %bitcast.92, f32[2,512,512]{2,1,0:T(8,128)} %param.8), kind=kOutput, calls=%fused_computation.34 | convolution fusion | flops 806092800 | bytes 5242880 | tf_op jit(solution)/shard_map/tik,sil->tksl/dot_general | solution.py:64
  133.0 4.8 %multiply_reduce_fusion = (f32[2]{0:T(128)S(1)}, f32[2,512,512]{2,1,0:T(8,128)}) fusion(f32[2,512,512]{2,1,0:T(8,128)S(1)} %copy-done.1, f32[1,512,512]{2,1,0:T(8,128)S(1)} %copy-done.4, f32[1,512,512]{2,1,0:T(8,128)S(1)} %fusion.12), kind=kOutput, calls=%fused_computation.22 | convolution fusion | flops 3222798336 | bytes 6291464 | tf_op jit(solution)/shard_map/cij,cjk->cik/dot_general | solution.py:95
  137.9 1.6 fusion.4
  139.5 6.5 %multiply_subtract_fusion = f32[2,512,512]{2,1,0:T(8,128)} fusion(f32[2,512,512]{2,1,0:T(8,128)} %get-tuple-element.22, f32[2]{0:T(128)S(1)} %sqrt_multiply_fusion), kind=kOutput, calls=%fused_computation.21 | convolution fusion | flops 1078460416 | bytes 4194312 | tf_op jit(solution)/shard_map/cik,ckj->cij/dot_general | solution.py:13
  146.0 6.3 %subtract_select_fusion = f32[2,512,512]{2,1,0:T(8,128)} fusion(f32[2,512,512]{2,1,0:T(8,128)} %multiply_subtract_fusion, pred[2]{0:T(512)(128)(4,1)S(1)} %compare_reduce_fusion), kind=kOutput, calls=%fused_computation.20 | convolution fusion | flops 1077411840 | bytes 4194306 | tf_op jit(solution)/shard_map/cik,ckj->cij/dot_general | solution.py:13
  152.3 5.4 %fusion = bf16[2,1536,512]{2,1,0:T(8,128)(2,1)} fusion(f32[1,1536,512]{2,1,0:T(8,128)} %bitcast.90, f32[1,1536,512]{2,1,0:T(8,128)} %bitcast.89, pred[2]{0:T(512)(128)(4,1)S(1)} %compare_reduce_fusion), kind=kLoop, calls=%fused_computation.4 | loop fusion | flops 7864320 | bytes 9437186 | tf_op jit(solution)/shard_map/convert_element_type | solution.py:111
  157.7 4.3 %all-to-all-done.2 = bf16[128,2,48,128]{3,2,1,0:T(8,128)(2,1)S(1)} async-done(((bf16[128,2,48,128]{3,2,1,0:T(8,128)(2,1)}), bf16[128,2,48,128]{3,2,1,0:T(8,128)(2,1)S(1)}, u32[]{:S(2)}, u32[]{:S(2)}) %all-to-all-start.2) | async-done | bytes 3145760 | tf_op jit(solution)/shard_map/all_to_all | solution.py:20
  162.1 2.2 %gather_fusion.2 = bf16[160,48,128]{2,1,0:T(8,128)(2,1)} fusion(bf16[256,48,128]{2,1,0:T(8,128)(2,1)S(1)} %bitcast.84, s32[1024]{0:T(1024)S(1)} %pad_clamp_fusion), kind=kCustom, calls=%fused_computation.2 | custom fusion | bytes 3932800 | tf_op jit(solution)/shard_map/jit(_take)/gather | solution.py:88
  (20 shorter events, 0.1 us)
Async XLA Ops:
  5.9 11.9 %copy-start = (bf16[160,48,128]{2,1,0:T(8,128)(2,1)S(1)}, bf16[160,48,128]{2,1,0:T(8,128)(2,1)}, u32[]{:S(2)}) copy-start(bf16[160,48,128]{2,1,0:T(8,128)(2,1)} %param.6) | copy-start | bytes 5898244
  5.9 53.2 %all-to-all-start.1 = ((bf16[128,2,48,128]{3,2,1,0:T(8,128)(2,1)}), bf16[128,2,48,128]{3,2,1,0:T(8,128)(2,1)}, u32[]{:S(2)}, u32[]{:S(2)}) async-start(bf16[128,2,48,128]{3,2,1,0:T(8,128)(2,1)} %bitcast.83), calls=%async_computation.1 | async-start | bytes 6291456 | tf_op jit(solution)/shard_map/all_to_all | solution.py:20
  59.1 46.3 %all-to-all-start = ((bf16[128,2,48,128]{3,2,1,0:T(8,128)(2,1)}), bf16[128,2,48,128]{3,2,1,0:T(8,128)(2,1)S(1)}, u32[]{:S(2)}, u32[]{:S(2)}) async-start(bf16[128,2,48,128]{3,2,1,0:T(8,128)(2,1)} %bitcast.82), calls=%async_computation | async-start | bytes 6291456 | tf_op jit(solution)/shard_map/all_to_all | solution.py:20
  63.8 2.7 %copy-start.11 = (s32[160]{0:T(256)S(1)}, s32[160]{0:T(256)}, u32[]{:S(2)}) copy-start(s32[160]{0:T(256)} %param.11) | copy-start | bytes 1924
  68.1 2.9 %copy-start.7 = (bf16[1,512,512]{2,1,0:T(8,128)(2,1)}, bf16[1,512,512]{2,1,0:T(8,128)(2,1)S(1)}, u32[]{:S(2)}) copy-start(bf16[1,512,512]{2,1,0:T(8,128)(2,1)S(1)} %get-tuple-element.17) | copy-start | bytes 1572868
  68.1 6.1 %copy-start.9 = (bf16[1,512,512]{2,1,0:T(8,128)(2,1)}, bf16[1,512,512]{2,1,0:T(8,128)(2,1)S(1)}, u32[]{:S(2)}) copy-start(bf16[1,512,512]{2,1,0:T(8,128)(2,1)S(1)} %get-tuple-element.18) | copy-start | bytes 1572868
  68.1 3.2 %copy-start.12 = (bf16[2,1536,512]{2,1,0:T(8,128)(2,1)S(1)}, bf16[2,1536,512]{2,1,0:T(8,128)(2,1)}, u32[]{:S(2)}) copy-start(bf16[2,1536,512]{2,1,0:T(8,128)(2,1)} %param.10) | copy-start | bytes 9437188
  71.0 3.2 %copy-start.2 = (bf16[128,1,48,128]{3,2,1,0:T(8,128)(2,1)}, bf16[128,1,48,128]{3,2,1,0:T(8,128)(2,1)S(1)}, u32[]{:S(2)}) copy-start(bf16[128,1,48,128]{3,2,1,0:T(8,128)(2,1)S(1)} %get-tuple-element.16) | copy-start | bytes 4718596
  71.0 3.2 %copy-start.3 = (bf16[128,1,48,128]{3,2,1,0:T(8,128)(2,1)}, bf16[128,1,48,128]{3,2,1,0:T(8,128)(2,1)S(1)}, u32[]{:S(2)}) copy-start(bf16[128,1,48,128]{3,2,1,0:T(8,128)(2,1)S(1)} %get-tuple-element.15) | copy-start | bytes 4718596
  105.4 1.9 %copy-start.6 = (f32[1536,512]{1,0:T(8,128)S(1)}, f32[1536,512]{1,0:T(8,128)}, u32[]{:S(2)}) copy-start(f32[1536,512]{1,0:T(8,128)} %fusion.1) | copy-start | bytes 9437188
  105.4 2.0 %copy-start.10 = (bf16[1,512,512]{2,1,0:T(8,128)(2,1)S(1)}, bf16[1,512,512]{2,1,0:T(8,128)(2,1)}, u32[]{:S(2)}) copy-start(bf16[1,512,512]{2,1,0:T(8,128)(2,1)} %copy-done.9) | copy-start | bytes 1572868
  109.0 1.9 %copy-start.5 = (f32[1536,512]{1,0:T(8,128)S(1)}, f32[1536,512]{1,0:T(8,128)}, u32[]{:S(2)}) copy-start(f32[1536,512]{1,0:T(8,128)} %fusion.2) | copy-start | bytes 9437188
  109.0 2.0 %copy-start.8 = (bf16[1,512,512]{2,1,0:T(8,128)(2,1)S(1)}, bf16[1,512,512]{2,1,0:T(8,128)(2,1)}, u32[]{:S(2)}) copy-start(bf16[1,512,512]{2,1,0:T(8,128)(2,1)} %copy-done.7) | copy-start | bytes 1572868
  115.6 46.4 %all-to-all-start.2 = ((bf16[128,2,48,128]{3,2,1,0:T(8,128)(2,1)}), bf16[128,2,48,128]{3,2,1,0:T(8,128)(2,1)S(1)}, u32[]{:S(2)}, u32[]{:S(2)}) async-start(bf16[128,2,48,128]{3,2,1,0:T(8,128)(2,1)} %pad_maximum_fusion), calls=%async_computation.2 | async-start | bytes 6291456 | tf_op jit(solution)/shard_map/all_to_all | solution.py:20
  129.6 3.3 %copy-start.1 = (f32[2,512,512]{2,1,0:T(8,128)S(1)}, f32[2,512,512]{2,1,0:T(8,128)}, u32[]{:S(2)}) copy-start(f32[2,512,512]{2,1,0:T(8,128)} %param.9) | copy-start | bytes 6291460
  129.6 3.4 %copy-start.4 = (f32[1,512,512]{2,1,0:T(8,128)S(1)}, f32[1,512,512]{2,1,0:T(8,128)}, u32[]{:S(2)}) copy-start(f32[1,512,512]{2,1,0:T(8,128)} %fusion.14) | copy-start | bytes 3145732
